TPU v7x, 32 devices: a whole 2x2x4 slice. The times are simulated.
32 devices in a mesh: block: 8 (over y, x, core), tm: 4 (over z).
Axes of the slice: x: 2, y: 2, z: 4, core: 2. Of those that a mesh axis runs over, the one named last changes fastest.
Arguments:
- traces: bfloat16 [2048, 8, 6, 1024], P('block', 'tm')
- valid: int32 [2048, 8, 6], P('block', 'tm'), may hold values from 0 to 1, as said below
- panel_owner: int32 [4], replicated, may hold values from 0 to 7, as said below
- panel_start: int32 [4], replicated, may hold values from 0 to 252, as said below
Outputs:
- xcorr: float32 [16, 2048, 1024], P('tm', 'block')
Inputs may be any that keep to these rules, and one draw needn't show every extreme that they name: Within one block-tm cell (256 channels by 2 windows by 6 segments) at least an eighth of the segments are valid. `panel_owner`: the panels lie on distinct blocks. `panel_start`: multiples of 4.
All inputs are finite; a program needn't handle non-finite values.
Results may differ from a plain program's by a relative error of at most 0.0051.
Values may be sent and summed in bfloat16 or wider, within the bound.
No kernel may reach another device: no remote copies, remote signals or barrier semaphores. Data moves between devices by JAX's collectives and lax.ppermute only.
A program may use at most 128 MiB of HBM per device.

v0:
```python
import math

import jax
import jax.numpy as jnp
from jax import lax
from jax.sharding import PartitionSpec as P
from jax.experimental import pallas as pl
from jax.experimental.pallas import tpu as pltpu

PP = 4
NP = 4


def spread(value, axis, source):
    kept = jnp.where(lax.axis_index(axis) == source, value, 0).astype(value.dtype)
    return lax.psum(kept, axis)


def forward_table(length):
    sample = jnp.arange(length, dtype=jnp.int32)
    bin_index = jnp.arange(length // 2, dtype=jnp.int32)
    angles = (sample[:, None] * bin_index[None, :] % length).astype(jnp.float32) * (
        2.0 * math.pi / length
    )
    return jnp.concatenate([jnp.cos(angles), -jnp.sin(angles)], axis=1).astype(jnp.bfloat16)


def inverse_table(length, factor):
    bin_index = jnp.arange(length // 2, dtype=jnp.int32)
    lag_index = jnp.arange(length, dtype=jnp.int32)
    angles = (bin_index[:, None] * lag_index[None, :] % length).astype(jnp.float32) * (
        2.0 * math.pi / length
    )
    weight = jnp.where(bin_index == 0, 1.0, 2.0).astype(jnp.float32)[:, None] * factor
    return jnp.concatenate([weight * jnp.cos(angles), -weight * jnp.sin(angles)], axis=0)


def whiten(segment_rows, valid_mask, forward):
    spectrum = jnp.dot(segment_rows, forward, preferred_element_type=jnp.float32)
    energy = jnp.mean(spectrum * spectrum, axis=1, keepdims=True)
    return (spectrum * lax.rsqrt(energy + 1e-06) * valid_mask[:, None].astype(jnp.float32)).astype(
        jnp.bfloat16
    )


def spectra_rows(segment_rows, valid_mask, forward):
    return whiten(segment_rows, valid_mask, forward)


def correlate(left, right):
    bins = left.shape[-1] // 2
    left_both = jnp.concatenate([left[..., :bins], left[..., bins:]], axis=1)
    right_both = jnp.concatenate([right[..., :bins], right[..., bins:]], axis=1)
    right_turn = jnp.concatenate([right[..., bins:], -right[..., :bins]], axis=1)
    real_part = jnp.einsum(
        "jmk,imk->jik", left_both, right_both, preferred_element_type=jnp.float32
    )
    imag_part = jnp.einsum(
        "jmk,imk->jik", left_both, right_turn, preferred_element_type=jnp.float32
    )
    return jnp.concatenate([real_part, imag_part], axis=-1)


def fetch_panel(whitened, panel_root, panel_first):
    candidate = lax.dynamic_slice_in_dim(whitened, panel_first, PP, 0)
    return spread(candidate, "block", panel_root)


def on_device(traces, valid, panel_owner, panel_start):
    channels, windows_here, segments, length = traces.shape
    bins = length // 2
    forward = forward_table(length)
    whitened = spectra_rows(
        traces.reshape(channels * windows_here * segments, length),
        valid.reshape(channels * windows_here * segments),
        forward,
    )
    whitened = whitened.reshape(channels, windows_here, segments, 2 * bins)
    pieces = []
    for panel in range(NP):
        pieces.append(fetch_panel(whitened, panel_owner[panel], panel_start[panel]))
    sources = jnp.concatenate(pieces, axis=0)
    groups = lax.axis_size("tm")
    inverse = inverse_table(length, 1.0 / math.sqrt(bins * windows_here * segments * groups))
    source_count = sources.shape[0]
    own_rows = whitened.reshape(channels, windows_here * segments, 2 * bins)
    source_rows = sources.reshape(source_count, windows_here * segments, 2 * bins)
    stacked = lax.psum_scatter(
        correlate(source_rows, own_rows), "tm", scatter_dimension=0, tiled=True
    )
    return jnp.dot(stacked, inverse, precision=lax.Precision.HIGHEST)


def edge_first(values, groups):
    return lax.ppermute(values, "tm", [(0, 1), (groups - 1, groups - 2)])


def whiten_kernel(rows_ref, forward_ref, mask_ref, out_ref):
    spectrum = jnp.dot(rows_ref[...], forward_ref[...], preferred_element_type=jnp.float32)
    energy = jnp.mean(spectrum * spectrum, axis=1, keepdims=True)
    scaled = spectrum * lax.rsqrt(energy + 1e-06) * mask_ref[...]
    out_ref[...] = scaled.astype(jnp.bfloat16).reshape(out_ref.shape)


def whiten_segments(rows, mask, forward, chunks):
    segments, channels, length = rows.shape
    width = channels // chunks
    return pl.pallas_call(
        whiten_kernel,
        grid=(segments,),
        in_specs=[
            pl.BlockSpec((None, channels, length), lambda m: (m, 0, 0)),
            pl.BlockSpec((length, length), lambda m: (0, 0)),
            pl.BlockSpec((None, channels, 1), lambda m: (m, 0, 0)),
        ],
        out_specs=pl.BlockSpec((chunks, None, width, length), lambda m: (0, m, 0, 0)),
        out_shape=jax.ShapeDtypeStruct((chunks, segments, width, length), jnp.bfloat16),
    )(rows, forward, mask)


LANES = 128
ROWS = 8


def cross_kernel(own_ref, src_ref, out_ref):
    segments = own_ref.shape[0]
    sources = src_ref.shape[1]
    rows = own_ref.shape[1]
    bins = own_ref.shape[-1] // 2

    def tile_body(tile, carry):
        re_lanes = pl.ds(pl.multiple_of(tile * LANES, LANES), LANES)
        im_lanes = pl.ds(pl.multiple_of(bins + tile * LANES, LANES), LANES)

        def step(m, acc):
            wr = own_ref[m, :, re_lanes].astype(jnp.float32)
            wi = own_ref[m, :, im_lanes].astype(jnp.float32)
            out = []
            for j in range(sources):
                sr = jnp.concatenate([src_ref[m, j, :, re_lanes]] * (rows // ROWS), axis=0)
                si = jnp.concatenate([src_ref[m, j, :, im_lanes]] * (rows // ROWS), axis=0)
                out.append(acc[2 * j] + (wr * sr + wi * si))
                out.append(acc[2 * j + 1] + (wi * sr - wr * si))
            return tuple(out)

        acc = tuple(jnp.zeros((rows, LANES), jnp.float32) for _ in range(2 * sources))
        acc = lax.fori_loop(0, segments, step, acc)
        for j in range(sources):
            out_ref[j, :, re_lanes] = acc[2 * j]
            out_ref[j, :, im_lanes] = acc[2 * j + 1]
        return carry

    lax.fori_loop(0, bins // LANES, tile_body, 0)


def cross_chunk(own, src):
    segments, width, length = own.shape
    sources = src.shape[1]
    step_rows = 2 * ROWS
    return pl.pallas_call(
        cross_kernel,
        grid=(width // step_rows,),
        in_specs=[
            pl.BlockSpec((segments, step_rows, length), lambda i: (0, i, 0)),
            pl.BlockSpec((segments, sources, ROWS, length), lambda i: (0, 0, 0, 0)),
        ],
        out_specs=pl.BlockSpec((sources, step_rows, length), lambda i: (0, i, 0)),
        out_shape=jax.ShapeDtypeStruct((sources, width, length), jnp.float32),
    )(own, src)


def butterfly_sum(values, axis):
    count = lax.axis_size(axis)
    step = 1
    while step < count:
        values = values + lax.ppermute(values, axis, [(b, b ^ step) for b in range(count)])
        step *= 2
    return values


def widen(values, length):
    segments, count = values.shape[0], values.shape[1]
    return jnp.broadcast_to(values.astype(jnp.float32)[:, :, None, :], (segments, count, ROWS, length))


def on_line(traces, valid, panel_owner, panel_start):
    channels, windows_here, segments, length = traces.shape
    bins = length // 2
    groups = lax.axis_size("tm")
    place = lax.axis_index("tm")
    chunks = 8
    width = channels // chunks
    seg_count = windows_here * segments
    forward = forward_table(length)
    rows = traces.reshape(channels, seg_count, length).transpose(1, 0, 2)
    mask = valid.reshape(channels, seg_count).transpose(1, 0).astype(jnp.float32)[:, :, None]
    whitened = whiten_segments(rows, mask, forward, chunks)
    block_place = lax.axis_index("block")
    pieces = []
    for panel in range(NP):
        first = panel_start[panel]
        chunk_of = first // width
        candidate = lax.dynamic_slice_in_dim(
            lax.dynamic_index_in_dim(whitened, chunk_of, 0, keepdims=False), first - chunk_of * width, PP, 1
        )
        pieces.append(jnp.where(block_place == panel_owner[panel], candidate, 0).astype(candidate.dtype))
    sources = butterfly_sum(jnp.concatenate(pieces, axis=1), "block")
    source_count = sources.shape[1]
    per_group = source_count // groups
    half = source_count // 2
    first_half = place < groups // 2
    turned = jnp.concatenate(
        [sources[:, source_count - per_group:], sources[:, half:source_count - per_group]], axis=1
    )
    far = jnp.where(first_half, turned, sources[:, :half])
    near = jnp.where(first_half, sources[:, :half], turned)
    inverse = inverse_table(length, 1.0 / math.sqrt(bins * seg_count * groups))
    is_edge = jnp.logical_or(place == 0, place == groups - 1)
    far_wide, near_wide = widen(far, length), widen(near, length)
    outs = []
    arrived = []
    for chunk in range(chunks):
        own = whitened[chunk]
        if chunk >= 2:
            own, _ = lax.optimization_barrier((own, arrived[chunk - 2]))
        far_part = cross_chunk(own, far_wide)
        near_part = cross_chunk(own, near_wide)
        edge_out = jnp.concatenate([far_part, near_part[per_group:]], axis=0).astype(jnp.bfloat16)
        if arrived:
            edge_out, _ = lax.optimization_barrier((edge_out, arrived[-1]))
        edge_in = edge_first(edge_out, groups)
        arrived.append(edge_in)
        far_total = far_part + edge_in[:half].astype(jnp.float32)
        got = lax.ppermute(far_total.astype(jnp.bfloat16), "tm", [(1, 2), (2, 1)]).astype(jnp.float32)
        low = near_part[:per_group] + got[:per_group]
        high = near_part[per_group:] + edge_in[half:].astype(jnp.float32) + got[per_group:]
        back = lax.ppermute(low, "tm", [(1, 0), (2, 3)])
        final = jnp.where(is_edge, near_part[:per_group] + back, high)
        outs.append(jnp.dot(final, inverse, precision=lax.Precision.HIGHEST))
    return jnp.concatenate(outs, axis=1)


def solution(mesh):
    in_specs = (P("block", "tm", None, None), P("block", "tm", None), P(), P())
    out_specs = P("tm", "block", None)
    body = on_line if mesh.shape["tm"] == 4 else on_device
    return jax.shard_map(
        body, mesh=mesh, in_specs=in_specs, out_specs=out_specs, check_vma=False
    )
```

profile of v0, /device:TPU:0, one launch (start us, length us, event | category | flops | bytes accessed | tf_op | source)
XLA Modules:
  0.0 353.4 jit_solution(1171497543610609448)
XLA Ops:
  0.0 8.5 %negate_convert_fusion = (bf16[1024,512]{1,0:T(8,128)(2,1)S(1)}, bf16[1024,512]{1,0:T(8,128)(2,1)S(1)}) fusion(), kind=kLoop, calls=%fused_computation.18 | loop fusion | flops 8912896 | bytes 2097152 | tf_op jit(solution)/shard_map/convert.17
  21.9 7.6 %copy.7 = bf16[256,2,6,1024]{3,0,2,1:T(8,128)(2,1)} copy(bf16[256,2,6,1024]{3,1,2,0:T(2,128)(2,1)} %param.4) | data formatting | bytes 12582912 | tf_op args[0]
  36.1 15.2 %shard_map.46 = bf16[8,12,32,1024]{3,2,1,0:T(8,128)(2,1)} custom-call(bf16[12,256,1024]{2,1,0:T(8,128)(2,1)} %bitcast.50, bf16[1024,1024]{1,0:T(8,128)(2,1)} %pad_maximum_fusion.forward_ref, f32[12,256,1]{2,1,0:T(8,128)} %copy.9.mask_ref), custom_call_target="tpu_custom_call" | custom-call | tf_op jit(solution)/shard_map/pallas_call | solution.py:108
  55.3 2.9 collective-permute-start.1
  58.2 9.4 %collective-permute-done.1 = bf16[12,16,1024]{2,1,0:T(8,128)(2,1)S(1)} collective-permute-done((bf16[12,16,1024]{2,1,0:T(8,128)(2,1)S(1)}, bf16[12,16,1024]{2,1,0:T(8,128)(2,1)S(1)}, u32[]{:S(2)}, u32[]{:S(2)}) %collective-permute-start.1) | collective-permute-done | bytes 393248 | tf_op jit(solution)/shard_map/ppermute | solution.py:176
  69.6 5.6 %slice_bitcast_fusion = (bf16[12,32,1024]{2,1,0:T(8,128)(2,1)}, bf16[12,32,1024]{2,1,0:T(8,128)(2,1)}, bf16[12,32,1024]{2,1,0:T(8,128)(2,1)}, bf16[12,32,1024]{2...) fusion(bf16[8,12,32,1024]{3,2,1,0:T(8,128)(2,1)} %shard_map.46), kind=kLoop, calls=%fused_computation.40 | loop fusion | bytes 12582912 | tf_op jit(solution)/shard_map/squeeze | solution.py:223
  75.2 3.3 collective-permute-done.2
  78.9 2.1 broadcast_in_dim.38.src_ref
  80.9 6.0 %shard_map.48 = f32[8,32,1024]{2,1,0:T(8,128)} custom-call(bf16[12,32,1024]{2,1,0:T(8,128)(2,1)} %get-tuple-element.38.own_ref, f32[12,8,8,1024]{3,2,1,0:T(8,128)} %broadcast_in_dim.38.src_ref), custom_call_target="tpu_custom_call" | custom-call | tf_op jit(solution)/shard_map/pallas_call | solution.py:160
  86.9 2.0 broadcast_in_dim.37.src_ref
  88.9 6.1 %shard_map.47 = f32[8,32,1024]{2,1,0:T(8,128)} custom-call(bf16[12,32,1024]{2,1,0:T(8,128)(2,1)} %get-tuple-element.38.own_ref, f32[12,8,8,1024]{3,2,1,0:T(8,128)} %broadcast_in_dim.37.src_ref), custom_call_target="tpu_custom_call" | custom-call | tf_op jit(solution)/shard_map/pallas_call | solution.py:160
  96.2 4.3 %collective-permute-start.3 = (bf16[12,32,1024]{2,1,0:T(8,128)(2,1)S(1)}, bf16[12,32,1024]{2,1,0:T(8,128)(2,1)}, u32[]{:S(2)}, u32[]{:S(2)}) collective-permute-start(bf16[12,32,1024]{2,1,0:T(8,128)(2,1)S(1)} %pad_maximum_fusion.1), channel_id=1, source_target_pairs={{0,1},{3,2},{4,5},{7,6},{8,9},{11,10},{12,13},{15,14},{16,17},{19,... | collective-permute-start | bytes 2359304 | tf_op jit(solution)/shard_map/ppermute | solution.py:95
  100.5 6.0 %shard_map.50 = f32[8,32,1024]{2,1,0:T(8,128)} custom-call(bf16[12,32,1024]{2,1,0:T(8,128)(2,1)} %get-tuple-element.37.own_ref, f32[12,8,8,1024]{3,2,1,0:T(8,128)} %broadcast_in_dim.38.src_ref), custom_call_target="tpu_custom_call" | custom-call | tf_op jit(solution)/shard_map/pallas_call | solution.py:160
  106.5 6.1 %shard_map.49 = f32[8,32,1024]{2,1,0:T(8,128)} custom-call(bf16[12,32,1024]{2,1,0:T(8,128)(2,1)} %get-tuple-element.37.own_ref, f32[12,8,8,1024]{3,2,1,0:T(8,128)} %broadcast_in_dim.37.src_ref), custom_call_target="tpu_custom_call" | custom-call | tf_op jit(solution)/shard_map/pallas_call | solution.py:160
  115.0 5.4 %collective-permute-start.6 = (bf16[12,32,1024]{2,1,0:T(8,128)(2,1)}, bf16[12,32,1024]{2,1,0:T(8,128)(2,1)}, u32[]{:S(2)}, u32[]{:S(2)}) collective-permute-start(bf16[12,32,1024]{2,1,0:T(8,128)(2,1)} %pad_maximum_fusion.2), channel_id=1, source_target_pairs={{0,1},{3,2},{4,5},{7,6},{8,9},{11,10},{12,13},{15,14},{16,17},{19,... | collective-permute-start | bytes 2359304 | tf_op jit(solution)/shard_map/ppermute | solution.py:95
  120.4 6.0 %shard_map.52 = f32[8,32,1024]{2,1,0:T(8,128)} custom-call(bf16[12,32,1024]{2,1,0:T(8,128)(2,1)} %get-tuple-element.19.own_ref, f32[12,8,8,1024]{3,2,1,0:T(8,128)} %broadcast_in_dim.38.src_ref), custom_call_target="tpu_custom_call" | custom-call | tf_op jit(solution)/shard_map/pallas_call | solution.py:160
  126.4 6.0 %shard_map.51 = f32[8,32,1024]{2,1,0:T(8,128)} custom-call(bf16[12,32,1024]{2,1,0:T(8,128)(2,1)} %get-tuple-element.19.own_ref, f32[12,8,8,1024]{3,2,1,0:T(8,128)} %broadcast_in_dim.37.src_ref), custom_call_target="tpu_custom_call" | custom-call | tf_op jit(solution)/shard_map/pallas_call | solution.py:160
  134.5 4.9 %collective-permute-start.9 = (bf16[12,32,1024]{2,1,0:T(8,128)(2,1)}, bf16[12,32,1024]{2,1,0:T(8,128)(2,1)}, u32[]{:S(2)}, u32[]{:S(2)}) collective-permute-start(bf16[12,32,1024]{2,1,0:T(8,128)(2,1)} %pad_maximum_fusion.3), channel_id=1, source_target_pairs={{0,1},{3,2},{4,5},{7,6},{8,9},{11,10},{12,13},{15,14},{16,17},{19,... | collective-permute-start | bytes 2359304 | tf_op jit(solution)/shard_map/ppermute | solution.py:95
  139.5 2.0 add_convert_fusion.7
  146.4 9.2 %sine_multiply_fusion = (f32[512,1024]{1,0:T(8,128)S(1)}, f32[512,1024]{1,0:T(8,128)}) fusion(f32[512]{0:T(512)S(1)} %fusion.84, f32[512]{0:T(512)S(1)} %select_multiply_fusion), kind=kLoop, calls=%fused_computation.14 | loop fusion | flops 8388608 | bytes 4198400 | tf_op jit(solution)/shard_map/mul | solution.py:35
  155.6 2.2 convert_element_type.143
  157.7 6.0 %shard_map.54 = f32[8,32,1024]{2,1,0:T(8,128)} custom-call(bf16[12,32,1024]{2,1,0:T(8,128)(2,1)} %get-tuple-element.21.own_ref, f32[12,8,8,1024]{3,2,1,0:T(8,128)} %broadcast_in_dim.38.src_ref), custom_call_target="tpu_custom_call" | custom-call | tf_op jit(solution)/shard_map/pallas_call | solution.py:160
  163.8 6.1 %shard_map.53 = f32[8,32,1024]{2,1,0:T(8,128)} custom-call(bf16[12,32,1024]{2,1,0:T(8,128)(2,1)} %get-tuple-element.21.own_ref, f32[12,8,8,1024]{3,2,1,0:T(8,128)} %broadcast_in_dim.37.src_ref), custom_call_target="tpu_custom_call" | custom-call | tf_op jit(solution)/shard_map/pallas_call | solution.py:160
  172.2 4.4 %collective-permute-start.12 = (bf16[12,32,1024]{2,1,0:T(8,128)(2,1)}, bf16[12,32,1024]{2,1,0:T(8,128)(2,1)}, u32[]{:S(2)}, u32[]{:S(2)}) collective-permute-start(bf16[12,32,1024]{2,1,0:T(8,128)(2,1)} %pad_maximum_fusion.4), channel_id=1, source_target_pairs={{0,1},{3,2},{4,5},{7,6},{8,9},{11,10},{12,13},{15,14},{16,17},{19,... | collective-permute-start | bytes 2359304 | tf_op jit(solution)/shard_map/ppermute | solution.py:95
  182.3 2.0 add_convert_fusion.5
  184.3 6.0 %shard_map.56 = f32[8,32,1024]{2,1,0:T(8,128)} custom-call(bf16[12,32,1024]{2,1,0:T(8,128)(2,1)} %get-tuple-element.23.own_ref, f32[12,8,8,1024]{3,2,1,0:T(8,128)} %broadcast_in_dim.38.src_ref), custom_call_target="tpu_custom_call" | custom-call | tf_op jit(solution)/shard_map/pallas_call | solution.py:160
  190.3 6.0 %shard_map.55 = f32[8,32,1024]{2,1,0:T(8,128)} custom-call(bf16[12,32,1024]{2,1,0:T(8,128)(2,1)} %get-tuple-element.23.own_ref, f32[12,8,8,1024]{3,2,1,0:T(8,128)} %broadcast_in_dim.37.src_ref), custom_call_target="tpu_custom_call" | custom-call | tf_op jit(solution)/shard_map/pallas_call | solution.py:160
  200.6 9.7 %collective-permute-start.15 = (bf16[12,32,1024]{2,1,0:T(8,128)(2,1)}, bf16[12,32,1024]{2,1,0:T(8,128)(2,1)}, u32[]{:S(2)}, u32[]{:S(2)}) collective-permute-start(bf16[12,32,1024]{2,1,0:T(8,128)(2,1)} %pad_maximum_fusion.5), channel_id=1, source_target_pairs={{0,1},{3,2},{4,5},{7,6},{8,9},{11,10},{12,13},{15,14},{16,17},{19,... | collective-permute-start | bytes 2359304 | tf_op jit(solution)/shard_map/ppermute | solution.py:95
  210.3 4.7 %convolution_dynamic-update-slice_fusion.7 = f32[4,256,1024]{2,1,0:T(8,128)} fusion(f32[8,32,1024]{2,1,0:T(8,128)} %convert_element_type.143, f32[4,32,1024]{2,1,0:T(8,128)} %collective-permute-done.5, f32[8,32,1024]{2,1,0:T(8,128)S(1)} %copy-done.21, bf16[12,32,1024]{2,1,0:T(8,128)(2,1)} %collective-permute-done.3, pred[]{:T(512)S(6)} %or.3, ...), kind=kOutput, calls=%fused_computation.31 | convolution fusion | flops 1612316672 | bytes 7077889 | tf_op jit(solution)/shard_map/dot_general | solution.py:239
  215.0 4.5 %convolution_dynamic-update-slice_fusion.6 = f32[4,256,1024]{2,1,0:T(8,128)} fusion(f32[4,256,1024]{2,1,0:T(8,128)} %convolution_dynamic-update-slice_fusion.7, f32[8,32,1024]{2,1,0:T(8,128)S(1)} %copy-done.30, f32[4,32,1024]{2,1,0:T(8,128)} %collective-permute-done.8, f32[8,32,1024]{2,1,0:T(8,128)S(1)} %copy-done.23, ...), kind=kOutput, calls=%fused_computation.30 | convolution fusion | flops 1612316672 | bytes 7077889 | tf_op jit(solution)/shard_map/dot_general | solution.py:239
  222.1 6.0 %shard_map.58 = f32[8,32,1024]{2,1,0:T(8,128)} custom-call(bf16[12,32,1024]{2,1,0:T(8,128)(2,1)} %get-tuple-element.25.own_ref, f32[12,8,8,1024]{3,2,1,0:T(8,128)} %broadcast_in_dim.38.src_ref), custom_call_target="tpu_custom_call" | custom-call | tf_op jit(solution)/shard_map/pallas_call | solution.py:160
  228.1 6.0 %shard_map.57 = f32[8,32,1024]{2,1,0:T(8,128)} custom-call(bf16[12,32,1024]{2,1,0:T(8,128)(2,1)} %get-tuple-element.25.own_ref, f32[12,8,8,1024]{3,2,1,0:T(8,128)} %broadcast_in_dim.37.src_ref), custom_call_target="tpu_custom_call" | custom-call | tf_op jit(solution)/shard_map/pallas_call | solution.py:160
  237.5 6.5 %collective-permute-start.18 = (bf16[12,32,1024]{2,1,0:T(8,128)(2,1)}, bf16[12,32,1024]{2,1,0:T(8,128)(2,1)}, u32[]{:S(2)}, u32[]{:S(2)}) collective-permute-start(bf16[12,32,1024]{2,1,0:T(8,128)(2,1)} %pad_maximum_fusion.6), channel_id=1, source_target_pairs={{0,1},{3,2},{4,5},{7,6},{8,9},{11,10},{12,13},{15,14},{16,17},{19,... | collective-permute-start | bytes 2359304 | tf_op jit(solution)/shard_map/ppermute | solution.py:95
  245.9 2.0 add_convert_fusion.3
  249.4 4.4 %convolution_dynamic-update-slice_fusion.5 = f32[4,256,1024]{2,1,0:T(8,128)} fusion(f32[4,256,1024]{2,1,0:T(8,128)} %convolution_dynamic-update-slice_fusion.6, f32[8,32,1024]{2,1,0:T(8,128)S(1)} %copy-done.32, f32[4,32,1024]{2,1,0:T(8,128)} %collective-permute-done.11, f32[8,32,1024]{2,1,0:T(8,128)S(1)} %copy-done.18, ...), kind=kOutput, calls=%fused_computation.29 | convolution fusion | flops 1612316672 | bytes 7077889 | tf_op jit(solution)/shard_map/dot_general | solution.py:239
  254.9 6.0 %shard_map.60 = f32[8,32,1024]{2,1,0:T(8,128)} custom-call(bf16[12,32,1024]{2,1,0:T(8,128)(2,1)} %get-tuple-element.27.own_ref, f32[12,8,8,1024]{3,2,1,0:T(8,128)} %broadcast_in_dim.38.src_ref), custom_call_target="tpu_custom_call" | custom-call | tf_op jit(solution)/shard_map/pallas_call | solution.py:160
  260.9 6.0 %shard_map.59 = f32[8,32,1024]{2,1,0:T(8,128)} custom-call(bf16[12,32,1024]{2,1,0:T(8,128)(2,1)} %get-tuple-element.27.own_ref, f32[12,8,8,1024]{3,2,1,0:T(8,128)} %broadcast_in_dim.37.src_ref), custom_call_target="tpu_custom_call" | custom-call | tf_op jit(solution)/shard_map/pallas_call | solution.py:160
  269.2 8.7 %collective-permute-start.21 = (bf16[12,32,1024]{2,1,0:T(8,128)(2,1)}, bf16[12,32,1024]{2,1,0:T(8,128)(2,1)}, u32[]{:S(2)}, u32[]{:S(2)}) collective-permute-start(bf16[12,32,1024]{2,1,0:T(8,128)(2,1)} %pad_maximum_fusion.7), channel_id=1, source_target_pairs={{0,1},{3,2},{4,5},{7,6},{8,9},{11,10},{12,13},{15,14},{16,17},{19,... | collective-permute-start | bytes 2359304 | tf_op jit(solution)/shard_map/ppermute | solution.py:95
  283.5 2.0 add_convert_fusion.2
  285.5 6.0 %shard_map.62 = f32[8,32,1024]{2,1,0:T(8,128)} custom-call(bf16[12,32,1024]{2,1,0:T(8,128)(2,1)} %get-tuple-element.29.own_ref, f32[12,8,8,1024]{3,2,1,0:T(8,128)} %broadcast_in_dim.38.src_ref), custom_call_target="tpu_custom_call" | custom-call | tf_op jit(solution)/shard_map/pallas_call | solution.py:160
  291.5 6.0 %shard_map.61 = f32[8,32,1024]{2,1,0:T(8,128)} custom-call(bf16[12,32,1024]{2,1,0:T(8,128)(2,1)} %get-tuple-element.29.own_ref, f32[12,8,8,1024]{3,2,1,0:T(8,128)} %broadcast_in_dim.37.src_ref), custom_call_target="tpu_custom_call" | custom-call | tf_op jit(solution)/shard_map/pallas_call | solution.py:160
  301.0 8.2 %collective-permute-start.24 = (bf16[12,32,1024]{2,1,0:T(8,128)(2,1)S(1)}, bf16[12,32,1024]{2,1,0:T(8,128)(2,1)S(1)}, u32[]{:S(2)}, u32[]{:S(2)}) collective-permute-start(bf16[12,32,1024]{2,1,0:T(8,128)(2,1)S(1)} %pad_maximum_fusion.8), channel_id=1, source_target_pairs={{0,1},{3,2},{4,5},{7,6},{8,9},{11,10},{12,13},{15,14},{16,17},{19,... | collective-permute-start | bytes 2359304 | tf_op jit(solution)/shard_map/ppermute | solution.py:95
  309.2 4.5 %convolution_dynamic-update-slice_fusion.4 = f32[4,256,1024]{2,1,0:T(8,128)} fusion(f32[4,256,1024]{2,1,0:T(8,128)} %convolution_dynamic-update-slice_fusion.5, f32[8,32,1024]{2,1,0:T(8,128)} %convert_element_type.156, f32[4,32,1024]{2,1,0:T(8,128)} %collective-permute-done.14, f32[8,32,1024]{2,1,0:T(8,128)S(1)} %copy-done.13, ...), kind=kOutput, calls=%fused_computation.28 | convolution fusion | flops 1612316672 | bytes 7077889 | tf_op jit(solution)/shard_map/dot_general | solution.py:239
  313.8 4.4 %convolution_dynamic-update-slice_fusion.3 = f32[4,256,1024]{2,1,0:T(8,128)} fusion(f32[4,256,1024]{2,1,0:T(8,128)} %convolution_dynamic-update-slice_fusion.4, f32[8,32,1024]{2,1,0:T(8,128)S(1)} %copy-done.28, f32[4,32,1024]{2,1,0:T(8,128)} %collective-permute-done.17, f32[8,32,1024]{2,1,0:T(8,128)S(1)} %copy-done.16, ...), kind=kOutput, calls=%fused_computation.27 | convolution fusion | flops 1612316672 | bytes 7077889 | tf_op jit(solution)/shard_map/dot_general | solution.py:239
  326.1 12.8 %collective-permute-done.20 = f32[4,32,1024]{2,1,0:T(8,128)S(1)} collective-permute-done((f32[4,32,1024]{2,1,0:T(8,128)S(1)}, f32[4,32,1024]{2,1,0:T(8,128)S(1)}, u32[]{:S(2)}, u32[]{:S(2)}) %collective-permute-start.20) | collective-permute-done | bytes 524320 | tf_op jit(solution)/shard_map/ppermute | solution.py:237
  338.9 4.2 %convolution_dynamic-update-slice_fusion.2 = f32[4,256,1024]{2,1,0:T(8,128)} fusion(f32[4,256,1024]{2,1,0:T(8,128)} %convolution_dynamic-update-slice_fusion.3, f32[8,32,1024]{2,1,0:T(8,128)S(1)} %convert_element_type.164, f32[4,32,1024]{2,1,0:T(8,128)S(1)} %collective-permute-done.20, f32[8,32,1024]{2,1,0:T(8,128)S(1)} %copy-done.14, ...), kind=kOutput, calls=%fused_computation.26 | convolution fusion | flops 1612316672 | bytes 7077889 | tf_op jit(solution)/shard_map/dot_general | solution.py:239
  344.5 4.2 %convolution_dynamic-update-slice_fusion.1 = f32[4,256,1024]{2,1,0:T(8,128)} fusion(f32[4,256,1024]{2,1,0:T(8,128)} %convolution_dynamic-update-slice_fusion.2, f32[8,32,1024]{2,1,0:T(8,128)S(1)} %convert_element_type.168, f32[4,32,1024]{2,1,0:T(8,128)S(1)} %collective-permute-done.23, f32[8,32,1024]{2,1,0:T(8,128)S(1)} %copy-done.19, ...), kind=kOutput, calls=%fused_computation.25 | convolution fusion | flops 1612316672 | bytes 7077889 | tf_op jit(solution)/shard_map/dot_general | solution.py:239
  350.2 3.3 convolution_dynamic-update-slice_fusion
  (173 shorter events, 66.0 us)
Async XLA Ops:
  0.0 8.6 %copy-start.34 = (s32[4]{0:T(128)S(1)}, s32[4]{0:T(128)}, u32[]{:S(2)}) copy-start(s32[4]{0:T(128)} %param.7) | copy-start | bytes 52
  21.9 7.6 %copy-start.33 = (s32[256,2,6]{0,1,2:T(2,128)S(1)}, s32[256,2,6]{0,1,2:T(2,128)}, u32[]{:S(2)}) copy-start(s32[256,2,6]{0,1,2:T(2,128)} %param.5) | copy-start | bytes 36868
  21.9 9.3 %copy-start.35 = (s32[4]{0:T(128)S(1)}, s32[4]{0:T(128)}, u32[]{:S(2)}) copy-start(s32[4]{0:T(128)} %param.6) | copy-start | bytes 52
  53.2 1.9 collective-permute-start
  55.3 12.3 %collective-permute-start.1 = (bf16[12,16,1024]{2,1,0:T(8,128)(2,1)S(1)}, bf16[12,16,1024]{2,1,0:T(8,128)(2,1)S(1)}, u32[]{:S(2)}, u32[]{:S(2)}) collective-permute-start(bf16[12,16,1024]{2,1,0:T(8,128)(2,1)S(1)} %fusion.85), channel_id=1, source_target_pairs={{0,8},{4,12},{8,0},{12,4},{16,24},{20,28},{24,16},{28,20},{1,9},{5... | collective-permute-start | bytes 1179656 | tf_op jit(solution)/shard_map/ppermute | solution.py:176
  67.8 10.7 %collective-permute-start.2 = (bf16[12,16,1024]{2,1,0:T(8,128)(2,1)S(1)}, bf16[12,16,1024]{2,1,0:T(8,128)(2,1)S(1)}, u32[]{:S(2)}, u32[]{:S(2)}) collective-permute-start(bf16[12,16,1024]{2,1,0:T(8,128)(2,1)S(1)} %add.200), channel_id=1, source_target_pairs={{0,16},{4,20},{8,24},{12,28},{16,0},{20,4},{24,8},{28,12},{1,17},{... | collective-permute-start | bytes 1179656 | tf_op jit(solution)/shard_map/ppermute | solution.py:176
  96.2 18.8 %collective-permute-start.3 = (bf16[12,32,1024]{2,1,0:T(8,128)(2,1)S(1)}, bf16[12,32,1024]{2,1,0:T(8,128)(2,1)}, u32[]{:S(2)}, u32[]{:S(2)}) collective-permute-start(bf16[12,32,1024]{2,1,0:T(8,128)(2,1)S(1)} %pad_maximum_fusion.1), channel_id=1, source_target_pairs={{0,1},{3,2},{4,5},{7,6},{8,9},{11,10},{12,13},{15,14},{16,17},{19,... | collective-permute-start | bytes 2359304 | tf_op jit(solution)/shard_map/ppermute | solution.py:95
  115.0 19.6 %collective-permute-start.6 = (bf16[12,32,1024]{2,1,0:T(8,128)(2,1)}, bf16[12,32,1024]{2,1,0:T(8,128)(2,1)}, u32[]{:S(2)}, u32[]{:S(2)}) collective-permute-start(bf16[12,32,1024]{2,1,0:T(8,128)(2,1)} %pad_maximum_fusion.2), channel_id=1, source_target_pairs={{0,1},{3,2},{4,5},{7,6},{8,9},{11,10},{12,13},{15,14},{16,17},{19,... | collective-permute-start | bytes 2359304 | tf_op jit(solution)/shard_map/ppermute | solution.py:95
  134.5 37.6 %collective-permute-start.9 = (bf16[12,32,1024]{2,1,0:T(8,128)(2,1)}, bf16[12,32,1024]{2,1,0:T(8,128)(2,1)}, u32[]{:S(2)}, u32[]{:S(2)}) collective-permute-start(bf16[12,32,1024]{2,1,0:T(8,128)(2,1)} %pad_maximum_fusion.3), channel_id=1, source_target_pairs={{0,1},{3,2},{4,5},{7,6},{8,9},{11,10},{12,13},{15,14},{16,17},{19,... | collective-permute-start | bytes 2359304 | tf_op jit(solution)/shard_map/ppermute | solution.py:95
  141.5 14.1 %collective-permute-start.4 = (bf16[8,32,1024]{2,1,0:T(8,128)(2,1)}, bf16[8,32,1024]{2,1,0:T(8,128)(2,1)}, u32[]{:S(2)}, u32[]{:S(2)}) collective-permute-start(bf16[8,32,1024]{2,1,0:T(8,128)(2,1)} %add_convert_fusion.7), channel_id=1, source_target_pairs={{1,2},{2,1},{5,6},{6,5},{9,10},{10,9},{13,14},{14,13},{17,18},{18,... | collective-permute-start | bytes 1572872 | tf_op jit(solution)/shard_map/ppermute | solution.py:234
  144.9 33.8 %collective-permute-start.7 = (bf16[8,32,1024]{2,1,0:T(8,128)(2,1)}, bf16[8,32,1024]{2,1,0:T(8,128)(2,1)}, u32[]{:S(2)}, u32[]{:S(2)}) collective-permute-start(bf16[8,32,1024]{2,1,0:T(8,128)(2,1)} %add_convert_fusion.6), channel_id=1, source_target_pairs={{1,2},{2,1},{5,6},{6,5},{9,10},{10,9},{13,14},{14,13},{17,18},{18,... | collective-permute-start | bytes 1572872 | tf_op jit(solution)/shard_map/ppermute | solution.py:234
  163.8 7.3 %copy-start.3 = (f32[8,32,1024]{2,1,0:T(8,128)S(1)}, f32[8,32,1024]{2,1,0:T(8,128)}, u32[]{:S(2)}) copy-start(f32[8,32,1024]{2,1,0:T(8,128)} %shard_map.54) | copy-start | bytes 3145732
  171.1 8.8 %copy-start.22 = (f32[8,32,1024]{2,1,0:T(8,128)S(1)}, f32[8,32,1024]{2,1,0:T(8,128)}, u32[]{:S(2)}) copy-start(f32[8,32,1024]{2,1,0:T(8,128)} %shard_map.49) | copy-start | bytes 3145732
  172.2 10.2 %copy-start.6 = (f32[8,32,1024]{2,1,0:T(8,128)S(1)}, f32[8,32,1024]{2,1,0:T(8,128)}, u32[]{:S(2)}) copy-start(f32[8,32,1024]{2,1,0:T(8,128)} %shard_map.52) | copy-start | bytes 3145732
  172.2 28.4 %collective-permute-start.12 = (bf16[12,32,1024]{2,1,0:T(8,128)(2,1)}, bf16[12,32,1024]{2,1,0:T(8,128)(2,1)}, u32[]{:S(2)}, u32[]{:S(2)}) collective-permute-start(bf16[12,32,1024]{2,1,0:T(8,128)(2,1)} %pad_maximum_fusion.4), channel_id=1, source_target_pairs={{0,1},{3,2},{4,5},{7,6},{8,9},{11,10},{12,13},{15,14},{16,17},{19,... | collective-permute-start | bytes 2359304 | tf_op jit(solution)/shard_map/ppermute | solution.py:95
  177.4 32.8 %collective-permute-start.5 = (f32[4,32,1024]{2,1,0:T(8,128)}, f32[4,32,1024]{2,1,0:T(8,128)}, u32[]{:S(2)}, u32[]{:S(2)}) collective-permute-start(f32[4,32,1024]{2,1,0:T(8,128)} %slice_add_fusion.15), channel_id=1, source_target_pairs={{1,0},{2,3},{5,4},{6,7},{9,8},{10,11},{13,12},{14,15},{17,16},{18,... | collective-permute-start | bytes 1572872 | tf_op jit(solution)/shard_map/ppermute | solution.py:237
  180.9 34.1 %collective-permute-start.8 = (f32[4,32,1024]{2,1,0:T(8,128)}, f32[4,32,1024]{2,1,0:T(8,128)}, u32[]{:S(2)}, u32[]{:S(2)}) collective-permute-start(f32[4,32,1024]{2,1,0:T(8,128)} %slice_add_fusion.13), channel_id=1, source_target_pairs={{1,0},{2,3},{5,4},{6,7},{9,8},{10,11},{13,12},{14,15},{17,16},{18,... | collective-permute-start | bytes 1572872 | tf_op jit(solution)/shard_map/ppermute | solution.py:237
  196.3 14.0 %copy-start = (f32[512,1024]{1,0:T(8,128)S(1)}, f32[512,1024]{1,0:T(8,128)}, u32[]{:S(2)}) copy-start(f32[512,1024]{1,0:T(8,128)} %get-tuple-element.58) | copy-start | bytes 6291460
  196.3 14.0 %copy-start.21 = (f32[8,32,1024]{2,1,0:T(8,128)S(1)}, f32[8,32,1024]{2,1,0:T(8,128)}, u32[]{:S(2)}) copy-start(f32[8,32,1024]{2,1,0:T(8,128)} %shard_map.47) | copy-start | bytes 3145732
  196.3 23.1 %collective-permute-start.10 = (bf16[8,32,1024]{2,1,0:T(8,128)(2,1)}, bf16[8,32,1024]{2,1,0:T(8,128)(2,1)S(1)}, u32[]{:S(2)}, u32[]{:S(2)}) collective-permute-start(bf16[8,32,1024]{2,1,0:T(8,128)(2,1)} %add_convert_fusion.5), channel_id=1, source_target_pairs={{1,2},{2,1},{5,6},{6,5},{9,10},{10,9},{13,14},{14,13},{17,18},{18,... | collective-permute-start | bytes 1572872 | tf_op jit(solution)/shard_map/ppermute | solution.py:234
  200.6 36.9 %collective-permute-start.15 = (bf16[12,32,1024]{2,1,0:T(8,128)(2,1)}, bf16[12,32,1024]{2,1,0:T(8,128)(2,1)}, u32[]{:S(2)}, u32[]{:S(2)}) collective-permute-start(bf16[12,32,1024]{2,1,0:T(8,128)(2,1)} %pad_maximum_fusion.5), channel_id=1, source_target_pairs={{0,1},{3,2},{4,5},{7,6},{8,9},{11,10},{12,13},{15,14},{16,17},{19,... | collective-permute-start | bytes 2359304 | tf_op jit(solution)/shard_map/ppermute | solution.py:95
  220.8 28.6 %collective-permute-start.11 = (f32[4,32,1024]{2,1,0:T(8,128)}, f32[4,32,1024]{2,1,0:T(8,128)}, u32[]{:S(2)}, u32[]{:S(2)}) collective-permute-start(f32[4,32,1024]{2,1,0:T(8,128)} %slice_add_fusion.11), channel_id=1, source_target_pairs={{1,0},{2,3},{5,4},{6,7},{9,8},{10,11},{13,12},{14,15},{17,16},{18,... | collective-permute-start | bytes 1572872 | tf_op jit(solution)/shard_map/ppermute | solution.py:237
  236.5 9.4 %copy-start.8 = (f32[8,32,1024]{2,1,0:T(8,128)S(1)}, f32[8,32,1024]{2,1,0:T(8,128)}, u32[]{:S(2)}) copy-start(f32[8,32,1024]{2,1,0:T(8,128)} %shard_map.56) | copy-start | bytes 3145732
  237.5 11.9 %copy-start.1 = (f32[512,1024]{1,0:T(8,128)S(1)}, f32[512,1024]{1,0:T(8,128)}, u32[]{:S(2)}) copy-start(f32[512,1024]{1,0:T(8,128)} %get-tuple-element.58) | copy-start | bytes 6291460
  237.5 11.9 %copy-start.18 = (f32[8,32,1024]{2,1,0:T(8,128)S(1)}, f32[8,32,1024]{2,1,0:T(8,128)}, u32[]{:S(2)}) copy-start(f32[8,32,1024]{2,1,0:T(8,128)} %shard_map.51) | copy-start | bytes 3145732
  237.5 11.9 %copy-start.32 = (f32[8,32,1024]{2,1,0:T(8,128)S(1)}, f32[8,32,1024]{2,1,0:T(8,128)}, u32[]{:S(2)}) copy-start(f32[8,32,1024]{2,1,0:T(8,128)} %copy-done.31) | copy-start | bytes 3145732
  237.5 31.7 %collective-permute-start.18 = (bf16[12,32,1024]{2,1,0:T(8,128)(2,1)}, bf16[12,32,1024]{2,1,0:T(8,128)(2,1)}, u32[]{:S(2)}, u32[]{:S(2)}) collective-permute-start(bf16[12,32,1024]{2,1,0:T(8,128)(2,1)} %pad_maximum_fusion.6), channel_id=1, source_target_pairs={{0,1},{3,2},{4,5},{7,6},{8,9},{11,10},{12,13},{15,14},{16,17},{19,... | collective-permute-start | bytes 2359304 | tf_op jit(solution)/shard_map/ppermute | solution.py:95
  245.2 8.6 %collective-permute-start.13 = (bf16[8,32,1024]{2,1,0:T(8,128)(2,1)S(1)}, bf16[8,32,1024]{2,1,0:T(8,128)(2,1)S(1)}, u32[]{:S(2)}, u32[]{:S(2)}) collective-permute-start(bf16[8,32,1024]{2,1,0:T(8,128)(2,1)S(1)} %add_convert_fusion.4), channel_id=1, source_target_pairs={{1,2},{2,1},{5,6},{6,5},{9,10},{10,9},{13,14},{14,13},{17,18},{18,... | collective-permute-start | bytes 1572872 | tf_op jit(solution)/shard_map/ppermute | solution.py:234
  247.9 32.2 %collective-permute-start.16 = (bf16[8,32,1024]{2,1,0:T(8,128)(2,1)}, bf16[8,32,1024]{2,1,0:T(8,128)(2,1)}, u32[]{:S(2)}, u32[]{:S(2)}) collective-permute-start(bf16[8,32,1024]{2,1,0:T(8,128)(2,1)} %add_convert_fusion.3), channel_id=1, source_target_pairs={{1,2},{2,1},{5,6},{6,5},{9,10},{10,9},{13,14},{14,13},{17,18},{18,... | collective-permute-start | bytes 1572872 | tf_op jit(solution)/shard_map/ppermute | solution.py:234
  260.9 7.3 %copy-start.4 = (f32[8,32,1024]{2,1,0:T(8,128)S(1)}, f32[8,32,1024]{2,1,0:T(8,128)}, u32[]{:S(2)}) copy-start(f32[8,32,1024]{2,1,0:T(8,128)} %shard_map.60) | copy-start | bytes 3145732
  266.9 11.0 %copy-start.12 = (f32[8,32,1024]{2,1,0:T(8,128)S(1)}, f32[8,32,1024]{2,1,0:T(8,128)}, u32[]{:S(2)}) copy-start(f32[8,32,1024]{2,1,0:T(8,128)} %shard_map.53) | copy-start | bytes 3145732
  266.9 11.1 %copy-start.25 = (f32[8,32,1024]{2,1,0:T(8,128)S(1)}, f32[8,32,1024]{2,1,0:T(8,128)}, u32[]{:S(2)}) copy-start(f32[8,32,1024]{2,1,0:T(8,128)} %convert_element_type.156) | copy-start | bytes 3145732
  268.2 13.1 %copy-start.15 = (f32[8,32,1024]{2,1,0:T(8,128)S(1)}, f32[8,32,1024]{2,1,0:T(8,128)}, u32[]{:S(2)}) copy-start(f32[8,32,1024]{2,1,0:T(8,128)} %shard_map.55) | copy-start | bytes 3145732
  269.2 14.3 %copy-start.7 = (f32[8,32,1024]{2,1,0:T(8,128)S(1)}, f32[8,32,1024]{2,1,0:T(8,128)}, u32[]{:S(2)}) copy-start(f32[8,32,1024]{2,1,0:T(8,128)} %shard_map.58) | copy-start | bytes 3145732
  269.2 31.7 %collective-permute-start.21 = (bf16[12,32,1024]{2,1,0:T(8,128)(2,1)}, bf16[12,32,1024]{2,1,0:T(8,128)(2,1)}, u32[]{:S(2)}, u32[]{:S(2)}) collective-permute-start(bf16[12,32,1024]{2,1,0:T(8,128)(2,1)} %pad_maximum_fusion.7), channel_id=1, source_target_pairs={{0,1},{3,2},{4,5},{7,6},{8,9},{11,10},{12,13},{15,14},{16,17},{19,... | collective-permute-start | bytes 2359304 | tf_op jit(solution)/shard_map/ppermute | solution.py:95
  278.9 30.3 %collective-permute-start.14 = (f32[4,32,1024]{2,1,0:T(8,128)}, f32[4,32,1024]{2,1,0:T(8,128)}, u32[]{:S(2)}, u32[]{:S(2)}) collective-permute-start(f32[4,32,1024]{2,1,0:T(8,128)} %slice_add_fusion.9), channel_id=1, source_target_pairs={{1,0},{2,3},{5,4},{6,7},{9,8},{10,11},{13,12},{14,15},{17,16},{18,... | collective-permute-start | bytes 1572872 | tf_op jit(solution)/shard_map/ppermute | solution.py:237
  282.2 31.5 %collective-permute-start.17 = (f32[4,32,1024]{2,1,0:T(8,128)}, f32[4,32,1024]{2,1,0:T(8,128)}, u32[]{:S(2)}, u32[]{:S(2)}) collective-permute-start(f32[4,32,1024]{2,1,0:T(8,128)} %slice_add_fusion.7), channel_id=1, source_target_pairs={{1,0},{2,3},{5,4},{6,7},{9,8},{10,11},{13,12},{14,15},{17,16},{18,... | collective-permute-start | bytes 1572872 | tf_op jit(solution)/shard_map/ppermute | solution.py:237
  297.5 11.7 %copy-start.2 = (f32[512,1024]{1,0:T(8,128)S(1)}, f32[512,1024]{1,0:T(8,128)}, u32[]{:S(2)}) copy-start(f32[512,1024]{1,0:T(8,128)} %get-tuple-element.58) | copy-start | bytes 6291460
  297.5 11.7 %copy-start.13 = (f32[8,32,1024]{2,1,0:T(8,128)S(1)}, f32[8,32,1024]{2,1,0:T(8,128)}, u32[]{:S(2)}) copy-start(f32[8,32,1024]{2,1,0:T(8,128)} %shard_map.53) | copy-start | bytes 3145732
  297.5 20.6 %collective-permute-start.19 = (bf16[8,32,1024]{2,1,0:T(8,128)(2,1)}, bf16[8,32,1024]{2,1,0:T(8,128)(2,1)S(1)}, u32[]{:S(2)}, u32[]{:S(2)}) collective-permute-start(bf16[8,32,1024]{2,1,0:T(8,128)(2,1)} %add_convert_fusion.2), channel_id=1, source_target_pairs={{1,2},{2,1},{5,6},{6,5},{9,10},{10,9},{13,14},{14,13},{17,18},{18,... | collective-permute-start | bytes 1572872 | tf_op jit(solution)/shard_map/ppermute | solution.py:234
  300.9 12.8 %copy-start.16 = (f32[8,32,1024]{2,1,0:T(8,128)S(1)}, f32[8,32,1024]{2,1,0:T(8,128)}, u32[]{:S(2)}) copy-start(f32[8,32,1024]{2,1,0:T(8,128)} %shard_map.55) | copy-start | bytes 3145732
  300.9 12.8 %copy-start.28 = (f32[8,32,1024]{2,1,0:T(8,128)S(1)}, f32[8,32,1024]{2,1,0:T(8,128)}, u32[]{:S(2)}) copy-start(f32[8,32,1024]{2,1,0:T(8,128)} %copy-done.27) | copy-start | bytes 3145732
  301.0 19.3 %collective-permute-start.24 = (bf16[12,32,1024]{2,1,0:T(8,128)(2,1)S(1)}, bf16[12,32,1024]{2,1,0:T(8,128)(2,1)S(1)}, u32[]{:S(2)}, u32[]{:S(2)}) collective-permute-start(bf16[12,32,1024]{2,1,0:T(8,128)(2,1)S(1)} %pad_maximum_fusion.8), channel_id=1, source_target_pairs={{0,1},{3,2},{4,5},{7,6},{8,9},{11,10},{12,13},{15,14},{16,17},{19,... | collective-permute-start | bytes 2359304 | tf_op jit(solution)/shard_map/ppermute | solution.py:95
  319.6 3.3 collective-permute-start.22
  320.5 3.9 %collective-permute-start.25 = (bf16[8,32,1024]{2,1,0:T(8,128)(2,1)S(1)}, bf16[8,32,1024]{2,1,0:T(8,128)(2,1)S(1)}, u32[]{:S(2)}, u32[]{:S(2)}) collective-permute-start(bf16[8,32,1024]{2,1,0:T(8,128)(2,1)S(1)} %add_convert_fusion), channel_id=1, source_target_pairs={{1,2},{2,1},{5,6},{6,5},{9,10},{10,9},{13,14},{14,13},{17,18},{18,... | collective-permute-start | bytes 1572872 | tf_op jit(solution)/shard_map/ppermute | solution.py:234
  321.4 17.5 %collective-permute-start.20 = (f32[4,32,1024]{2,1,0:T(8,128)S(1)}, f32[4,32,1024]{2,1,0:T(8,128)S(1)}, u32[]{:S(2)}, u32[]{:S(2)}) collective-permute-start(f32[4,32,1024]{2,1,0:T(8,128)S(1)} %slice_add_fusion.5), channel_id=1, source_target_pairs={{1,0},{2,3},{5,4},{6,7},{9,8},{10,11},{13,12},{14,15},{17,16},{18,... | collective-permute-start | bytes 1572872 | tf_op jit(solution)/shard_map/ppermute | solution.py:237
  323.0 21.5 %collective-permute-start.23 = (f32[4,32,1024]{2,1,0:T(8,128)S(1)}, f32[4,32,1024]{2,1,0:T(8,128)S(1)}, u32[]{:S(2)}, u32[]{:S(2)}) collective-permute-start(f32[4,32,1024]{2,1,0:T(8,128)S(1)} %slice_add_fusion.3), channel_id=1, source_target_pairs={{1,0},{2,3},{5,4},{6,7},{9,8},{10,11},{13,12},{14,15},{17,16},{18,... | collective-permute-start | bytes 1572872 | tf_op jit(solution)/shard_map/ppermute | solution.py:237
  324.5 25.6 %collective-permute-start.26 = (f32[4,32,1024]{2,1,0:T(8,128)S(1)}, f32[4,32,1024]{2,1,0:T(8,128)S(1)}, u32[]{:S(2)}, u32[]{:S(2)}) collective-permute-start(f32[4,32,1024]{2,1,0:T(8,128)S(1)} %slice_add_fusion.1), channel_id=1, source_target_pairs={{1,0},{2,3},{5,4},{6,7},{9,8},{10,11},{13,12},{14,15},{17,16},{18,... | collective-permute-start | bytes 1572872 | tf_op jit(solution)/shard_map/ppermute | solution.py:237
  (15 other events, 69.5 us)
where the time goes:
time: 356 us; the launch traced here: 353 us
  Pallas kernels  111 us (31%)
  starting transfers between devices  76.5 us (21%)
  other arithmetic  55.5 us (16%)
  matrix products  34.1 us (10%)
  waiting for transfers between devices  30 us (8%)
  local copies, waits for them, and re-layouts  29.8 us (8%)
  between operations  16.1 us (5%)
    pallas_call x16, Pallas kernels, cross_chunk(): pl.pallas_call(cross_kernel, grid=(width // step_rows,), in_specs=[pl.Blo...  96.2 us
    ppermute x8, starting transfers between devices, edge_first(): return lax.ppermute(values, 'tm', [(0, 1), (groups - 1, groups - 2)])  52.2 us
    dot_general x8, matrix products, on_line(): outs.append(jnp.dot(final, inverse, precision=lax.Precision.HIGHEST))  34.1 us
    ppermute x8, waiting for transfers between devices, on_line(): back = lax.ppermute(low, 'tm', [(1, 0), (2, 3)])  15.7 us
    pallas_call x1, Pallas kernels, whiten_segments(): pl.pallas_call(whiten_kernel, grid=(segments,), in_specs=[pl.BlockSpec((N...  15.2 us
    ppermute x3, waiting for transfers between devices, butterfly_sum(): lax.ppermute(values, axis, [(b, b ^ step) for b in range(count)])  14.1 us
    another operation x9, other arithmetic  12.8 us
    convert_element_type x8, other arithmetic, on_line(): far_total.astype(jnp.bfloat16)  12.6 us
  transfers between devices with their start and end apart: 27, of which 7 were waited for; matrix products, arithmetic and copies ran while one was open for 25% of the time, Pallas kernels for 24%

commit v1 on v0

--- a/solution.py
+++ b/solution.py
@@ -191,7 +191,12 @@
     chunks = 8
     width = channels // chunks
     seg_count = windows_here * segments
-    forward = forward_table(length)
+    sample = jnp.arange(length, dtype=jnp.int32)
+    bin_index = jnp.arange(bins, dtype=jnp.int32)
+    angles = (sample[:, None] * bin_index[None, :] % length).astype(jnp.float32) * (2.0 * math.pi / length)
+    cosine = jnp.cos(angles)
+    sine = jnp.sin(angles)
+    forward = jnp.concatenate([cosine, -sine], axis=1).astype(jnp.bfloat16)
     rows = traces.reshape(channels, seg_count, length).transpose(1, 0, 2)
     mask = valid.reshape(channels, seg_count).transpose(1, 0).astype(jnp.float32)[:, :, None]
     whitened = whiten_segments(rows, mask, forward, chunks)
@@ -214,7 +219,9 @@
     )
     far = jnp.where(first_half, turned, sources[:, :half])
     near = jnp.where(first_half, sources[:, :half], turned)
-    inverse = inverse_table(length, 1.0 / math.sqrt(bins * seg_count * groups))
+    factor = 1.0 / math.sqrt(bins * seg_count * groups)
+    weight = jnp.where(bin_index == 0, 1.0, 2.0).astype(jnp.float32)[:, None] * factor
+    inverse = jnp.concatenate([weight * cosine.T, -weight * sine.T], axis=0)
     is_edge = jnp.logical_or(place == 0, place == groups - 1)
     far_wide, near_wide = widen(far, length), widen(near, length)
     outs = []
@@ -236,7 +243,7 @@
         high = near_part[per_group:] + edge_in[half:].astype(jnp.float32) + got[per_group:]
         back = lax.ppermute(low, "tm", [(1, 0), (2, 3)])
         final = jnp.where(is_edge, near_part[:per_group] + back, high)
-        outs.append(jnp.dot(final, inverse, precision=lax.Precision.HIGHEST))
+        outs.append(jnp.dot(final, inverse, precision=lax.Precision.HIGH))
     return jnp.concatenate(outs, axis=1)
 
 

time: 356 us -> 353 us (level)
  matrix products: 34.1 us -> 26.8 us
  waiting for transfers between devices: 30 us -> 33.9 us
    dot_general x8, matrix products: 34.1 us -> 26.8 us  [on_line(): outs.append(jnp.dot(final, inverse, precision=lax.Precision.HIGH))]
    ppermute x8, waiting for transfers between devices: 15.7 us -> 19.4 us  [on_line(): back = lax.ppermute(low, 'tm', [(1, 0), (2, 3)])]
  transfers between devices with their start and end apart: 27 -> 27, of which waited for: 7 -> 8; matrix products, arithmetic and copies ran while one was open for 25% -> 23% of each run, Pallas kernels for 24% -> 24%
where the time goes in v1:
time: 353 us; the launch traced here: 351 us
  Pallas kernels  111 us (31%)
  starting transfers between devices  77.1 us (22%)
  other arithmetic  55.5 us (16%)
  waiting for transfers between devices  33.9 us (10%)
  local copies, waits for them, and re-layouts  29.8 us (8%)
  matrix products  26.8 us (8%)
  between operations  16 us (5%)
    pallas_call x16, Pallas kernels, cross_chunk(): pl.pallas_call(cross_kernel, grid=(width // step_rows,), in_specs=[pl.Blo...  96.2 us
    ppermute x8, starting transfers between devices, edge_first(): return lax.ppermute(values, 'tm', [(0, 1), (groups - 1, groups - 2)])  52.8 us
    dot_general x8, matrix products, on_line(): outs.append(jnp.dot(final, inverse, precision=lax.Precision.HIGH))  26.8 us
    ppermute x8, waiting for transfers between devices, on_line(): back = lax.ppermute(low, 'tm', [(1, 0), (2, 3)])  19.4 us
    pallas_call x1, Pallas kernels, whiten_segments(): pl.pallas_call(whiten_kernel, grid=(segments,), in_specs=[pl.BlockSpec((N...  15.2 us
    ppermute x3, waiting for transfers between devices, butterfly_sum(): lax.ppermute(values, axis, [(b, b ^ step) for b in range(count)])  14.1 us
    another operation x9, other arithmetic  12.8 us
    convert_element_type x8, other arithmetic, on_line(): far_total.astype(jnp.bfloat16)  12.6 us
  transfers between devices with their start and end apart: 27, of which 8 were waited for; matrix products, arithmetic and copies ran while one was open for 23% of the time, Pallas kernels for 24%

profile of v1, /device:TPU:0, one launch (start us, length us, event | category | flops | bytes accessed | tf_op | source)
XLA Modules:
  0.0 350.7 jit_solution(7916126473195846455)
XLA Ops:
  0.0 8.5 %negate_convert_fusion = (bf16[1024,512]{1,0:T(8,128)(2,1)S(1)}, bf16[1024,512]{1,0:T(8,128)(2,1)S(1)}) fusion(), kind=kLoop, calls=%fused_computation.18 | loop fusion | flops 8912896 | bytes 2097152 | tf_op jit(solution)/shard_map/convert.17
  21.9 7.6 %copy.7 = bf16[256,2,6,1024]{3,0,2,1:T(8,128)(2,1)} copy(bf16[256,2,6,1024]{3,1,2,0:T(2,128)(2,1)} %param.4) | data formatting | bytes 12582912 | tf_op args[0]
  36.1 15.2 %shard_map.46 = bf16[8,12,32,1024]{3,2,1,0:T(8,128)(2,1)} custom-call(bf16[12,256,1024]{2,1,0:T(8,128)(2,1)} %bitcast.50, bf16[1024,1024]{1,0:T(8,128)(2,1)} %pad_maximum_fusion.forward_ref, f32[12,256,1]{2,1,0:T(8,128)} %copy.9.mask_ref), custom_call_target="tpu_custom_call" | custom-call | tf_op jit(solution)/shard_map/pallas_call | solution.py:108
  55.3 2.9 collective-permute-start.1
  58.2 9.4 %collective-permute-done.1 = bf16[12,16,1024]{2,1,0:T(8,128)(2,1)S(1)} collective-permute-done((bf16[12,16,1024]{2,1,0:T(8,128)(2,1)S(1)}, bf16[12,16,1024]{2,1,0:T(8,128)(2,1)S(1)}, u32[]{:S(2)}, u32[]{:S(2)}) %collective-permute-start.1) | collective-permute-done | bytes 393248 | tf_op jit(solution)/shard_map/ppermute | solution.py:176
  69.6 5.6 %slice_bitcast_fusion = (bf16[12,32,1024]{2,1,0:T(8,128)(2,1)}, bf16[12,32,1024]{2,1,0:T(8,128)(2,1)}, bf16[12,32,1024]{2,1,0:T(8,128)(2,1)}, bf16[12,32,1024]{2...) fusion(bf16[8,12,32,1024]{3,2,1,0:T(8,128)(2,1)} %shard_map.46), kind=kLoop, calls=%fused_computation.40 | loop fusion | bytes 12582912 | tf_op jit(solution)/shard_map/squeeze | solution.py:230
  75.2 3.3 collective-permute-done.2
  78.9 2.1 broadcast_in_dim.36.src_ref
  80.9 6.0 %shard_map.48 = f32[8,32,1024]{2,1,0:T(8,128)} custom-call(bf16[12,32,1024]{2,1,0:T(8,128)(2,1)} %get-tuple-element.38.own_ref, f32[12,8,8,1024]{3,2,1,0:T(8,128)} %broadcast_in_dim.36.src_ref), custom_call_target="tpu_custom_call" | custom-call | tf_op jit(solution)/shard_map/pallas_call | solution.py:160
  86.9 2.0 broadcast_in_dim.35.src_ref
  88.9 6.1 %shard_map.47 = f32[8,32,1024]{2,1,0:T(8,128)} custom-call(bf16[12,32,1024]{2,1,0:T(8,128)(2,1)} %get-tuple-element.38.own_ref, f32[12,8,8,1024]{3,2,1,0:T(8,128)} %broadcast_in_dim.35.src_ref), custom_call_target="tpu_custom_call" | custom-call | tf_op jit(solution)/shard_map/pallas_call | solution.py:160
  96.2 4.3 %collective-permute-start.3 = (bf16[12,32,1024]{2,1,0:T(8,128)(2,1)S(1)}, bf16[12,32,1024]{2,1,0:T(8,128)(2,1)}, u32[]{:S(2)}, u32[]{:S(2)}) collective-permute-start(bf16[12,32,1024]{2,1,0:T(8,128)(2,1)S(1)} %pad_maximum_fusion.1), channel_id=1, source_target_pairs={{0,1},{3,2},{4,5},{7,6},{8,9},{11,10},{12,13},{15,14},{16,17},{19,... | collective-permute-start | bytes 2359304 | tf_op jit(solution)/shard_map/ppermute | solution.py:95
  100.6 6.0 %shard_map.50 = f32[8,32,1024]{2,1,0:T(8,128)} custom-call(bf16[12,32,1024]{2,1,0:T(8,128)(2,1)} %get-tuple-element.37.own_ref, f32[12,8,8,1024]{3,2,1,0:T(8,128)} %broadcast_in_dim.36.src_ref), custom_call_target="tpu_custom_call" | custom-call | tf_op jit(solution)/shard_map/pallas_call | solution.py:160
  106.5 6.1 %shard_map.49 = f32[8,32,1024]{2,1,0:T(8,128)} custom-call(bf16[12,32,1024]{2,1,0:T(8,128)(2,1)} %get-tuple-element.37.own_ref, f32[12,8,8,1024]{3,2,1,0:T(8,128)} %broadcast_in_dim.35.src_ref), custom_call_target="tpu_custom_call" | custom-call | tf_op jit(solution)/shard_map/pallas_call | solution.py:160
  115.0 5.4 %collective-permute-start.6 = (bf16[12,32,1024]{2,1,0:T(8,128)(2,1)}, bf16[12,32,1024]{2,1,0:T(8,128)(2,1)}, u32[]{:S(2)}, u32[]{:S(2)}) collective-permute-start(bf16[12,32,1024]{2,1,0:T(8,128)(2,1)} %pad_maximum_fusion.2), channel_id=1, source_target_pairs={{0,1},{3,2},{4,5},{7,6},{8,9},{11,10},{12,13},{15,14},{16,17},{19,... | collective-permute-start | bytes 2359304 | tf_op jit(solution)/shard_map/ppermute | solution.py:95
  120.4 6.0 %shard_map.52 = f32[8,32,1024]{2,1,0:T(8,128)} custom-call(bf16[12,32,1024]{2,1,0:T(8,128)(2,1)} %get-tuple-element.19.own_ref, f32[12,8,8,1024]{3,2,1,0:T(8,128)} %broadcast_in_dim.36.src_ref), custom_call_target="tpu_custom_call" | custom-call | tf_op jit(solution)/shard_map/pallas_call | solution.py:160
  126.4 6.0 %shard_map.51 = f32[8,32,1024]{2,1,0:T(8,128)} custom-call(bf16[12,32,1024]{2,1,0:T(8,128)(2,1)} %get-tuple-element.19.own_ref, f32[12,8,8,1024]{3,2,1,0:T(8,128)} %broadcast_in_dim.35.src_ref), custom_call_target="tpu_custom_call" | custom-call | tf_op jit(solution)/shard_map/pallas_call | solution.py:160
  134.5 4.9 %collective-permute-start.9 = (bf16[12,32,1024]{2,1,0:T(8,128)(2,1)}, bf16[12,32,1024]{2,1,0:T(8,128)(2,1)}, u32[]{:S(2)}, u32[]{:S(2)}) collective-permute-start(bf16[12,32,1024]{2,1,0:T(8,128)(2,1)} %pad_maximum_fusion.3), channel_id=1, source_target_pairs={{0,1},{3,2},{4,5},{7,6},{8,9},{11,10},{12,13},{15,14},{16,17},{19,... | collective-permute-start | bytes 2359304 | tf_op jit(solution)/shard_map/ppermute | solution.py:95
  139.5 2.0 add_convert_fusion.7
  146.4 9.2 %sine_multiply_fusion = (f32[512,1024]{1,0:T(8,128)S(1)}, f32[512,1024]{1,0:T(8,128)}) fusion(f32[512]{0:T(512)S(1)} %fusion.84, f32[512]{0:T(512)S(1)} %select_multiply_fusion), kind=kLoop, calls=%fused_computation.14 | loop fusion | flops 8388608 | bytes 4198400 | tf_op jit(solution)/shard_map/mul | solution.py:224
  155.6 2.2 convert_element_type.144
  157.7 6.0 %shard_map.54 = f32[8,32,1024]{2,1,0:T(8,128)} custom-call(bf16[12,32,1024]{2,1,0:T(8,128)(2,1)} %get-tuple-element.21.own_ref, f32[12,8,8,1024]{3,2,1,0:T(8,128)} %broadcast_in_dim.36.src_ref), custom_call_target="tpu_custom_call" | custom-call | tf_op jit(solution)/shard_map/pallas_call | solution.py:160
  163.8 6.1 %shard_map.53 = f32[8,32,1024]{2,1,0:T(8,128)} custom-call(bf16[12,32,1024]{2,1,0:T(8,128)(2,1)} %get-tuple-element.21.own_ref, f32[12,8,8,1024]{3,2,1,0:T(8,128)} %broadcast_in_dim.35.src_ref), custom_call_target="tpu_custom_call" | custom-call | tf_op jit(solution)/shard_map/pallas_call | solution.py:160
  172.2 4.4 %collective-permute-start.12 = (bf16[12,32,1024]{2,1,0:T(8,128)(2,1)}, bf16[12,32,1024]{2,1,0:T(8,128)(2,1)}, u32[]{:S(2)}, u32[]{:S(2)}) collective-permute-start(bf16[12,32,1024]{2,1,0:T(8,128)(2,1)} %pad_maximum_fusion.4), channel_id=1, source_target_pairs={{0,1},{3,2},{4,5},{7,6},{8,9},{11,10},{12,13},{15,14},{16,17},{19,... | collective-permute-start | bytes 2359304 | tf_op jit(solution)/shard_map/ppermute | solution.py:95
  184.3 6.0 %shard_map.56 = f32[8,32,1024]{2,1,0:T(8,128)} custom-call(bf16[12,32,1024]{2,1,0:T(8,128)(2,1)} %get-tuple-element.23.own_ref, f32[12,8,8,1024]{3,2,1,0:T(8,128)} %broadcast_in_dim.36.src_ref), custom_call_target="tpu_custom_call" | custom-call | tf_op jit(solution)/shard_map/pallas_call | solution.py:160
  190.3 6.0 %shard_map.55 = f32[8,32,1024]{2,1,0:T(8,128)} custom-call(bf16[12,32,1024]{2,1,0:T(8,128)(2,1)} %get-tuple-element.23.own_ref, f32[12,8,8,1024]{3,2,1,0:T(8,128)} %broadcast_in_dim.35.src_ref), custom_call_target="tpu_custom_call" | custom-call | tf_op jit(solution)/shard_map/pallas_call | solution.py:160
  200.6 9.7 %collective-permute-start.15 = (bf16[12,32,1024]{2,1,0:T(8,128)(2,1)}, bf16[12,32,1024]{2,1,0:T(8,128)(2,1)}, u32[]{:S(2)}, u32[]{:S(2)}) collective-permute-start(bf16[12,32,1024]{2,1,0:T(8,128)(2,1)} %pad_maximum_fusion.5), channel_id=1, source_target_pairs={{0,1},{3,2},{4,5},{7,6},{8,9},{11,10},{12,13},{15,14},{16,17},{19,... | collective-permute-start | bytes 2359304 | tf_op jit(solution)/shard_map/ppermute | solution.py:95
  210.3 3.8 %convolution_dynamic-update-slice_fusion.7 = f32[4,256,1024]{2,1,0:T(8,128)} fusion(f32[8,32,1024]{2,1,0:T(8,128)} %convert_element_type.144, f32[4,32,1024]{2,1,0:T(8,128)} %collective-permute-done.5, f32[8,32,1024]{2,1,0:T(8,128)S(1)} %copy-done.21, bf16[12,32,1024]{2,1,0:T(8,128)(2,1)} %collective-permute-done.3, pred[]{:T(512)S(6)} %or.3, ...), kind=kOutput, calls=%fused_computation.31 | convolution fusion | flops 807010304 | bytes 7077889 | tf_op jit(solution)/shard_map/dot_general | solution.py:246
  214.1 3.6 %convolution_dynamic-update-slice_fusion.6 = f32[4,256,1024]{2,1,0:T(8,128)} fusion(f32[4,256,1024]{2,1,0:T(8,128)} %convolution_dynamic-update-slice_fusion.7, f32[8,32,1024]{2,1,0:T(8,128)S(1)} %copy-done.30, f32[4,32,1024]{2,1,0:T(8,128)} %collective-permute-done.8, f32[8,32,1024]{2,1,0:T(8,128)S(1)} %copy-done.23, ...), kind=kOutput, calls=%fused_computation.30 | convolution fusion | flops 807010304 | bytes 7077889 | tf_op jit(solution)/shard_map/dot_general | solution.py:246
  220.3 6.0 %shard_map.58 = f32[8,32,1024]{2,1,0:T(8,128)} custom-call(bf16[12,32,1024]{2,1,0:T(8,128)(2,1)} %get-tuple-element.25.own_ref, f32[12,8,8,1024]{3,2,1,0:T(8,128)} %broadcast_in_dim.36.src_ref), custom_call_target="tpu_custom_call" | custom-call | tf_op jit(solution)/shard_map/pallas_call | solution.py:160
  226.3 6.0 %shard_map.57 = f32[8,32,1024]{2,1,0:T(8,128)} custom-call(bf16[12,32,1024]{2,1,0:T(8,128)(2,1)} %get-tuple-element.25.own_ref, f32[12,8,8,1024]{3,2,1,0:T(8,128)} %broadcast_in_dim.35.src_ref), custom_call_target="tpu_custom_call" | custom-call | tf_op jit(solution)/shard_map/pallas_call | solution.py:160
  235.7 6.5 %collective-permute-start.18 = (bf16[12,32,1024]{2,1,0:T(8,128)(2,1)}, bf16[12,32,1024]{2,1,0:T(8,128)(2,1)}, u32[]{:S(2)}, u32[]{:S(2)}) collective-permute-start(bf16[12,32,1024]{2,1,0:T(8,128)(2,1)} %pad_maximum_fusion.6), channel_id=1, source_target_pairs={{0,1},{3,2},{4,5},{7,6},{8,9},{11,10},{12,13},{15,14},{16,17},{19,... | collective-permute-start | bytes 2359304 | tf_op jit(solution)/shard_map/ppermute | solution.py:95
  244.1 2.0 add_convert_fusion.3
  247.6 3.5 convolution_dynamic-update-slice_fusion.5
  252.2 6.0 %shard_map.60 = f32[8,32,1024]{2,1,0:T(8,128)} custom-call(bf16[12,32,1024]{2,1,0:T(8,128)(2,1)} %get-tuple-element.27.own_ref, f32[12,8,8,1024]{3,2,1,0:T(8,128)} %broadcast_in_dim.36.src_ref), custom_call_target="tpu_custom_call" | custom-call | tf_op jit(solution)/shard_map/pallas_call | solution.py:160
  258.2 6.0 %shard_map.59 = f32[8,32,1024]{2,1,0:T(8,128)} custom-call(bf16[12,32,1024]{2,1,0:T(8,128)(2,1)} %get-tuple-element.27.own_ref, f32[12,8,8,1024]{3,2,1,0:T(8,128)} %broadcast_in_dim.35.src_ref), custom_call_target="tpu_custom_call" | custom-call | tf_op jit(solution)/shard_map/pallas_call | solution.py:160
  266.5 9.6 %collective-permute-start.21 = (bf16[12,32,1024]{2,1,0:T(8,128)(2,1)}, bf16[12,32,1024]{2,1,0:T(8,128)(2,1)}, u32[]{:S(2)}, u32[]{:S(2)}) collective-permute-start(bf16[12,32,1024]{2,1,0:T(8,128)(2,1)} %pad_maximum_fusion.7), channel_id=1, source_target_pairs={{0,1},{3,2},{4,5},{7,6},{8,9},{11,10},{12,13},{15,14},{16,17},{19,... | collective-permute-start | bytes 2359304 | tf_op jit(solution)/shard_map/ppermute | solution.py:95
  283.7 6.0 %shard_map.62 = f32[8,32,1024]{2,1,0:T(8,128)} custom-call(bf16[12,32,1024]{2,1,0:T(8,128)(2,1)} %get-tuple-element.29.own_ref, f32[12,8,8,1024]{3,2,1,0:T(8,128)} %broadcast_in_dim.36.src_ref), custom_call_target="tpu_custom_call" | custom-call | tf_op jit(solution)/shard_map/pallas_call | solution.py:160
  289.7 6.0 %shard_map.61 = f32[8,32,1024]{2,1,0:T(8,128)} custom-call(bf16[12,32,1024]{2,1,0:T(8,128)(2,1)} %get-tuple-element.29.own_ref, f32[12,8,8,1024]{3,2,1,0:T(8,128)} %broadcast_in_dim.35.src_ref), custom_call_target="tpu_custom_call" | custom-call | tf_op jit(solution)/shard_map/pallas_call | solution.py:160
  299.1 8.0 %collective-permute-start.24 = (bf16[12,32,1024]{2,1,0:T(8,128)(2,1)S(1)}, bf16[12,32,1024]{2,1,0:T(8,128)(2,1)S(1)}, u32[]{:S(2)}, u32[]{:S(2)}) collective-permute-start(bf16[12,32,1024]{2,1,0:T(8,128)(2,1)S(1)} %pad_maximum_fusion.8), channel_id=1, source_target_pairs={{0,1},{3,2},{4,5},{7,6},{8,9},{11,10},{12,13},{15,14},{16,17},{19,... | collective-permute-start | bytes 2359304 | tf_op jit(solution)/shard_map/ppermute | solution.py:95
  307.2 3.6 %convolution_dynamic-update-slice_fusion.4 = f32[4,256,1024]{2,1,0:T(8,128)} fusion(f32[4,256,1024]{2,1,0:T(8,128)} %convolution_dynamic-update-slice_fusion.5, f32[8,32,1024]{2,1,0:T(8,128)} %convert_element_type.157, f32[4,32,1024]{2,1,0:T(8,128)} %collective-permute-done.14, f32[8,32,1024]{2,1,0:T(8,128)S(1)} %copy-done.13, ...), kind=kOutput, calls=%fused_computation.28 | convolution fusion | flops 807010304 | bytes 7077889 | tf_op jit(solution)/shard_map/dot_general | solution.py:246
  310.8 3.5 convolution_dynamic-update-slice_fusion.3
  322.4 14.5 %collective-permute-done.20 = f32[4,32,1024]{2,1,0:T(8,128)S(1)} collective-permute-done((f32[4,32,1024]{2,1,0:T(8,128)S(1)}, f32[4,32,1024]{2,1,0:T(8,128)S(1)}, u32[]{:S(2)}, u32[]{:S(2)}) %collective-permute-start.20) | collective-permute-done | bytes 524320 | tf_op jit(solution)/shard_map/ppermute | solution.py:244
  336.8 3.3 convolution_dynamic-update-slice_fusion.2
  340.1 2.6 collective-permute-done.23
  342.8 3.3 convolution_dynamic-update-slice_fusion.1
  346.1 2.3 collective-permute-done.26
  348.4 2.3 convolution_dynamic-update-slice_fusion
  (173 shorter events, 67.3 us)
Async XLA Ops:
  0.0 8.6 %copy-start.34 = (s32[4]{0:T(128)S(1)}, s32[4]{0:T(128)}, u32[]{:S(2)}) copy-start(s32[4]{0:T(128)} %param.7) | copy-start | bytes 52
  21.9 7.6 %copy-start.33 = (s32[256,2,6]{0,1,2:T(2,128)S(1)}, s32[256,2,6]{0,1,2:T(2,128)}, u32[]{:S(2)}) copy-start(s32[256,2,6]{0,1,2:T(2,128)} %param.5) | copy-start | bytes 36868
  21.9 9.3 %copy-start.35 = (s32[4]{0:T(128)S(1)}, s32[4]{0:T(128)}, u32[]{:S(2)}) copy-start(s32[4]{0:T(128)} %param.6) | copy-start | bytes 52
  53.2 1.9 collective-permute-start
  55.3 12.3 %collective-permute-start.1 = (bf16[12,16,1024]{2,1,0:T(8,128)(2,1)S(1)}, bf16[12,16,1024]{2,1,0:T(8,128)(2,1)S(1)}, u32[]{:S(2)}, u32[]{:S(2)}) collective-permute-start(bf16[12,16,1024]{2,1,0:T(8,128)(2,1)S(1)} %fusion.85), channel_id=1, source_target_pairs={{0,8},{4,12},{8,0},{12,4},{16,24},{20,28},{24,16},{28,20},{1,9},{5... | collective-permute-start | bytes 1179656 | tf_op jit(solution)/shard_map/ppermute | solution.py:176
  67.8 10.7 %collective-permute-start.2 = (bf16[12,16,1024]{2,1,0:T(8,128)(2,1)S(1)}, bf16[12,16,1024]{2,1,0:T(8,128)(2,1)S(1)}, u32[]{:S(2)}, u32[]{:S(2)}) collective-permute-start(bf16[12,16,1024]{2,1,0:T(8,128)(2,1)S(1)} %add.198), channel_id=1, source_target_pairs={{0,16},{4,20},{8,24},{12,28},{16,0},{20,4},{24,8},{28,12},{1,17},{... | collective-permute-start | bytes 1179656 | tf_op jit(solution)/shard_map/ppermute | solution.py:176
  96.2 18.8 %collective-permute-start.3 = (bf16[12,32,1024]{2,1,0:T(8,128)(2,1)S(1)}, bf16[12,32,1024]{2,1,0:T(8,128)(2,1)}, u32[]{:S(2)}, u32[]{:S(2)}) collective-permute-start(bf16[12,32,1024]{2,1,0:T(8,128)(2,1)S(1)} %pad_maximum_fusion.1), channel_id=1, source_target_pairs={{0,1},{3,2},{4,5},{7,6},{8,9},{11,10},{12,13},{15,14},{16,17},{19,... | collective-permute-start | bytes 2359304 | tf_op jit(solution)/shard_map/ppermute | solution.py:95
  115.0 19.6 %collective-permute-start.6 = (bf16[12,32,1024]{2,1,0:T(8,128)(2,1)}, bf16[12,32,1024]{2,1,0:T(8,128)(2,1)}, u32[]{:S(2)}, u32[]{:S(2)}) collective-permute-start(bf16[12,32,1024]{2,1,0:T(8,128)(2,1)} %pad_maximum_fusion.2), channel_id=1, source_target_pairs={{0,1},{3,2},{4,5},{7,6},{8,9},{11,10},{12,13},{15,14},{16,17},{19,... | collective-permute-start | bytes 2359304 | tf_op jit(solution)/shard_map/ppermute | solution.py:95
  134.5 37.6 %collective-permute-start.9 = (bf16[12,32,1024]{2,1,0:T(8,128)(2,1)}, bf16[12,32,1024]{2,1,0:T(8,128)(2,1)}, u32[]{:S(2)}, u32[]{:S(2)}) collective-permute-start(bf16[12,32,1024]{2,1,0:T(8,128)(2,1)} %pad_maximum_fusion.3), channel_id=1, source_target_pairs={{0,1},{3,2},{4,5},{7,6},{8,9},{11,10},{12,13},{15,14},{16,17},{19,... | collective-permute-start | bytes 2359304 | tf_op jit(solution)/shard_map/ppermute | solution.py:95
  141.5 14.1 %collective-permute-start.4 = (bf16[8,32,1024]{2,1,0:T(8,128)(2,1)}, bf16[8,32,1024]{2,1,0:T(8,128)(2,1)}, u32[]{:S(2)}, u32[]{:S(2)}) collective-permute-start(bf16[8,32,1024]{2,1,0:T(8,128)(2,1)} %add_convert_fusion.7), channel_id=1, source_target_pairs={{1,2},{2,1},{5,6},{6,5},{9,10},{10,9},{13,14},{14,13},{17,18},{18,... | collective-permute-start | bytes 1572872 | tf_op jit(solution)/shard_map/ppermute | solution.py:241
  144.9 33.8 %collective-permute-start.7 = (bf16[8,32,1024]{2,1,0:T(8,128)(2,1)}, bf16[8,32,1024]{2,1,0:T(8,128)(2,1)}, u32[]{:S(2)}, u32[]{:S(2)}) collective-permute-start(bf16[8,32,1024]{2,1,0:T(8,128)(2,1)} %add_convert_fusion.6), channel_id=1, source_target_pairs={{1,2},{2,1},{5,6},{6,5},{9,10},{10,9},{13,14},{14,13},{17,18},{18,... | collective-permute-start | bytes 1572872 | tf_op jit(solution)/shard_map/ppermute | solution.py:241
  163.8 7.3 %copy-start.3 = (f32[8,32,1024]{2,1,0:T(8,128)S(1)}, f32[8,32,1024]{2,1,0:T(8,128)}, u32[]{:S(2)}) copy-start(f32[8,32,1024]{2,1,0:T(8,128)} %shard_map.54) | copy-start | bytes 3145732
  171.1 8.8 %copy-start.22 = (f32[8,32,1024]{2,1,0:T(8,128)S(1)}, f32[8,32,1024]{2,1,0:T(8,128)}, u32[]{:S(2)}) copy-start(f32[8,32,1024]{2,1,0:T(8,128)} %shard_map.49) | copy-start | bytes 3145732
  172.2 10.2 %copy-start.6 = (f32[8,32,1024]{2,1,0:T(8,128)S(1)}, f32[8,32,1024]{2,1,0:T(8,128)}, u32[]{:S(2)}) copy-start(f32[8,32,1024]{2,1,0:T(8,128)} %shard_map.52) | copy-start | bytes 3145732
  172.2 28.4 %collective-permute-start.12 = (bf16[12,32,1024]{2,1,0:T(8,128)(2,1)}, bf16[12,32,1024]{2,1,0:T(8,128)(2,1)}, u32[]{:S(2)}, u32[]{:S(2)}) collective-permute-start(bf16[12,32,1024]{2,1,0:T(8,128)(2,1)} %pad_maximum_fusion.4), channel_id=1, source_target_pairs={{0,1},{3,2},{4,5},{7,6},{8,9},{11,10},{12,13},{15,14},{16,17},{19,... | collective-permute-start | bytes 2359304 | tf_op jit(solution)/shard_map/ppermute | solution.py:95
  177.4 32.8 %collective-permute-start.5 = (f32[4,32,1024]{2,1,0:T(8,128)}, f32[4,32,1024]{2,1,0:T(8,128)}, u32[]{:S(2)}, u32[]{:S(2)}) collective-permute-start(f32[4,32,1024]{2,1,0:T(8,128)} %slice_add_fusion.15), channel_id=1, source_target_pairs={{1,0},{2,3},{5,4},{6,7},{9,8},{10,11},{13,12},{14,15},{17,16},{18,... | collective-permute-start | bytes 1572872 | tf_op jit(solution)/shard_map/ppermute | solution.py:244
  180.9 33.2 %collective-permute-start.8 = (f32[4,32,1024]{2,1,0:T(8,128)}, f32[4,32,1024]{2,1,0:T(8,128)}, u32[]{:S(2)}, u32[]{:S(2)}) collective-permute-start(f32[4,32,1024]{2,1,0:T(8,128)} %slice_add_fusion.13), channel_id=1, source_target_pairs={{1,0},{2,3},{5,4},{6,7},{9,8},{10,11},{13,12},{14,15},{17,16},{18,... | collective-permute-start | bytes 1572872 | tf_op jit(solution)/shard_map/ppermute | solution.py:244
  196.3 14.0 %copy-start = (f32[512,1024]{1,0:T(8,128)S(1)}, f32[512,1024]{1,0:T(8,128)}, u32[]{:S(2)}) copy-start(f32[512,1024]{1,0:T(8,128)} %get-tuple-element.58) | copy-start | bytes 6291460
  196.3 14.0 %copy-start.21 = (f32[8,32,1024]{2,1,0:T(8,128)S(1)}, f32[8,32,1024]{2,1,0:T(8,128)}, u32[]{:S(2)}) copy-start(f32[8,32,1024]{2,1,0:T(8,128)} %shard_map.47) | copy-start | bytes 3145732
  196.3 21.3 %collective-permute-start.10 = (bf16[8,32,1024]{2,1,0:T(8,128)(2,1)}, bf16[8,32,1024]{2,1,0:T(8,128)(2,1)S(1)}, u32[]{:S(2)}, u32[]{:S(2)}) collective-permute-start(bf16[8,32,1024]{2,1,0:T(8,128)(2,1)} %add_convert_fusion.5), channel_id=1, source_target_pairs={{1,2},{2,1},{5,6},{6,5},{9,10},{10,9},{13,14},{14,13},{17,18},{18,... | collective-permute-start | bytes 1572872 | tf_op jit(solution)/shard_map/ppermute | solution.py:241
  200.6 35.1 %collective-permute-start.15 = (bf16[12,32,1024]{2,1,0:T(8,128)(2,1)}, bf16[12,32,1024]{2,1,0:T(8,128)(2,1)}, u32[]{:S(2)}, u32[]{:S(2)}) collective-permute-start(bf16[12,32,1024]{2,1,0:T(8,128)(2,1)} %pad_maximum_fusion.5), channel_id=1, source_target_pairs={{0,1},{3,2},{4,5},{7,6},{8,9},{11,10},{12,13},{15,14},{16,17},{19,... | collective-permute-start | bytes 2359304 | tf_op jit(solution)/shard_map/ppermute | solution.py:95
  219.0 28.6 %collective-permute-start.11 = (f32[4,32,1024]{2,1,0:T(8,128)}, f32[4,32,1024]{2,1,0:T(8,128)}, u32[]{:S(2)}, u32[]{:S(2)}) collective-permute-start(f32[4,32,1024]{2,1,0:T(8,128)} %slice_add_fusion.11), channel_id=1, source_target_pairs={{1,0},{2,3},{5,4},{6,7},{9,8},{10,11},{13,12},{14,15},{17,16},{18,... | collective-permute-start | bytes 1572872 | tf_op jit(solution)/shard_map/ppermute | solution.py:244
  234.7 9.4 %copy-start.8 = (f32[8,32,1024]{2,1,0:T(8,128)S(1)}, f32[8,32,1024]{2,1,0:T(8,128)}, u32[]{:S(2)}) copy-start(f32[8,32,1024]{2,1,0:T(8,128)} %shard_map.56) | copy-start | bytes 3145732
  235.7 11.9 %copy-start.1 = (f32[512,1024]{1,0:T(8,128)S(1)}, f32[512,1024]{1,0:T(8,128)}, u32[]{:S(2)}) copy-start(f32[512,1024]{1,0:T(8,128)} %get-tuple-element.58) | copy-start | bytes 6291460
  235.7 11.9 %copy-start.18 = (f32[8,32,1024]{2,1,0:T(8,128)S(1)}, f32[8,32,1024]{2,1,0:T(8,128)}, u32[]{:S(2)}) copy-start(f32[8,32,1024]{2,1,0:T(8,128)} %shard_map.51) | copy-start | bytes 3145732
  235.7 11.9 %copy-start.32 = (f32[8,32,1024]{2,1,0:T(8,128)S(1)}, f32[8,32,1024]{2,1,0:T(8,128)}, u32[]{:S(2)}) copy-start(f32[8,32,1024]{2,1,0:T(8,128)} %copy-done.31) | copy-start | bytes 3145732
  235.7 30.8 %collective-permute-start.18 = (bf16[12,32,1024]{2,1,0:T(8,128)(2,1)}, bf16[12,32,1024]{2,1,0:T(8,128)(2,1)}, u32[]{:S(2)}, u32[]{:S(2)}) collective-permute-start(bf16[12,32,1024]{2,1,0:T(8,128)(2,1)} %pad_maximum_fusion.6), channel_id=1, source_target_pairs={{0,1},{3,2},{4,5},{7,6},{8,9},{11,10},{12,13},{15,14},{16,17},{19,... | collective-permute-start | bytes 2359304 | tf_op jit(solution)/shard_map/ppermute | solution.py:95
  243.4 7.7 %collective-permute-start.13 = (bf16[8,32,1024]{2,1,0:T(8,128)(2,1)S(1)}, bf16[8,32,1024]{2,1,0:T(8,128)(2,1)S(1)}, u32[]{:S(2)}, u32[]{:S(2)}) collective-permute-start(bf16[8,32,1024]{2,1,0:T(8,128)(2,1)S(1)} %add_convert_fusion.4), channel_id=1, source_target_pairs={{1,2},{2,1},{5,6},{6,5},{9,10},{10,9},{13,14},{14,13},{17,18},{18,... | collective-permute-start | bytes 1572872 | tf_op jit(solution)/shard_map/ppermute | solution.py:241
  246.1 32.3 %collective-permute-start.16 = (bf16[8,32,1024]{2,1,0:T(8,128)(2,1)}, bf16[8,32,1024]{2,1,0:T(8,128)(2,1)}, u32[]{:S(2)}, u32[]{:S(2)}) collective-permute-start(bf16[8,32,1024]{2,1,0:T(8,128)(2,1)} %add_convert_fusion.3), channel_id=1, source_target_pairs={{1,2},{2,1},{5,6},{6,5},{9,10},{10,9},{13,14},{14,13},{17,18},{18,... | collective-permute-start | bytes 1572872 | tf_op jit(solution)/shard_map/ppermute | solution.py:241
  258.2 7.3 %copy-start.4 = (f32[8,32,1024]{2,1,0:T(8,128)S(1)}, f32[8,32,1024]{2,1,0:T(8,128)}, u32[]{:S(2)}) copy-start(f32[8,32,1024]{2,1,0:T(8,128)} %shard_map.60) | copy-start | bytes 3145732
  264.2 11.9 %copy-start.12 = (f32[8,32,1024]{2,1,0:T(8,128)S(1)}, f32[8,32,1024]{2,1,0:T(8,128)}, u32[]{:S(2)}) copy-start(f32[8,32,1024]{2,1,0:T(8,128)} %shard_map.53) | copy-start | bytes 3145732
  264.2 11.9 %copy-start.25 = (f32[8,32,1024]{2,1,0:T(8,128)S(1)}, f32[8,32,1024]{2,1,0:T(8,128)}, u32[]{:S(2)}) copy-start(f32[8,32,1024]{2,1,0:T(8,128)} %convert_element_type.157) | copy-start | bytes 3145732
  265.5 14.0 %copy-start.15 = (f32[8,32,1024]{2,1,0:T(8,128)S(1)}, f32[8,32,1024]{2,1,0:T(8,128)}, u32[]{:S(2)}) copy-start(f32[8,32,1024]{2,1,0:T(8,128)} %shard_map.55) | copy-start | bytes 3145732
  266.5 15.2 %copy-start.7 = (f32[8,32,1024]{2,1,0:T(8,128)S(1)}, f32[8,32,1024]{2,1,0:T(8,128)}, u32[]{:S(2)}) copy-start(f32[8,32,1024]{2,1,0:T(8,128)} %shard_map.58) | copy-start | bytes 3145732
  266.5 32.6 %collective-permute-start.21 = (bf16[12,32,1024]{2,1,0:T(8,128)(2,1)}, bf16[12,32,1024]{2,1,0:T(8,128)(2,1)}, u32[]{:S(2)}, u32[]{:S(2)}) collective-permute-start(bf16[12,32,1024]{2,1,0:T(8,128)(2,1)} %pad_maximum_fusion.7), channel_id=1, source_target_pairs={{0,1},{3,2},{4,5},{7,6},{8,9},{11,10},{12,13},{15,14},{16,17},{19,... | collective-permute-start | bytes 2359304 | tf_op jit(solution)/shard_map/ppermute | solution.py:95
  277.1 30.1 %collective-permute-start.14 = (f32[4,32,1024]{2,1,0:T(8,128)}, f32[4,32,1024]{2,1,0:T(8,128)}, u32[]{:S(2)}, u32[]{:S(2)}) collective-permute-start(f32[4,32,1024]{2,1,0:T(8,128)} %slice_add_fusion.9), channel_id=1, source_target_pairs={{1,0},{2,3},{5,4},{6,7},{9,8},{10,11},{13,12},{14,15},{17,16},{18,... | collective-permute-start | bytes 1572872 | tf_op jit(solution)/shard_map/ppermute | solution.py:244
  280.4 30.4 %collective-permute-start.17 = (f32[4,32,1024]{2,1,0:T(8,128)}, f32[4,32,1024]{2,1,0:T(8,128)}, u32[]{:S(2)}, u32[]{:S(2)}) collective-permute-start(f32[4,32,1024]{2,1,0:T(8,128)} %slice_add_fusion.7), channel_id=1, source_target_pairs={{1,0},{2,3},{5,4},{6,7},{9,8},{10,11},{13,12},{14,15},{17,16},{18,... | collective-permute-start | bytes 1572872 | tf_op jit(solution)/shard_map/ppermute | solution.py:244
  295.7 11.5 %copy-start.2 = (f32[512,1024]{1,0:T(8,128)S(1)}, f32[512,1024]{1,0:T(8,128)}, u32[]{:S(2)}) copy-start(f32[512,1024]{1,0:T(8,128)} %get-tuple-element.58) | copy-start | bytes 6291460
  295.7 11.5 %copy-start.13 = (f32[8,32,1024]{2,1,0:T(8,128)S(1)}, f32[8,32,1024]{2,1,0:T(8,128)}, u32[]{:S(2)}) copy-start(f32[8,32,1024]{2,1,0:T(8,128)} %shard_map.53) | copy-start | bytes 3145732
  295.7 18.6 %collective-permute-start.19 = (bf16[8,32,1024]{2,1,0:T(8,128)(2,1)}, bf16[8,32,1024]{2,1,0:T(8,128)(2,1)S(1)}, u32[]{:S(2)}, u32[]{:S(2)}) collective-permute-start(bf16[8,32,1024]{2,1,0:T(8,128)(2,1)} %add_convert_fusion.2), channel_id=1, source_target_pairs={{1,2},{2,1},{5,6},{6,5},{9,10},{10,9},{13,14},{14,13},{17,18},{18,... | collective-permute-start | bytes 1572872 | tf_op jit(solution)/shard_map/ppermute | solution.py:241
  299.1 11.7 %copy-start.16 = (f32[8,32,1024]{2,1,0:T(8,128)S(1)}, f32[8,32,1024]{2,1,0:T(8,128)}, u32[]{:S(2)}) copy-start(f32[8,32,1024]{2,1,0:T(8,128)} %shard_map.55) | copy-start | bytes 3145732
  299.1 11.7 %copy-start.28 = (f32[8,32,1024]{2,1,0:T(8,128)S(1)}, f32[8,32,1024]{2,1,0:T(8,128)}, u32[]{:S(2)}) copy-start(f32[8,32,1024]{2,1,0:T(8,128)} %copy-done.27) | copy-start | bytes 3145732
  299.1 17.5 %collective-permute-start.24 = (bf16[12,32,1024]{2,1,0:T(8,128)(2,1)S(1)}, bf16[12,32,1024]{2,1,0:T(8,128)(2,1)S(1)}, u32[]{:S(2)}, u32[]{:S(2)}) collective-permute-start(bf16[12,32,1024]{2,1,0:T(8,128)(2,1)S(1)} %pad_maximum_fusion.8), channel_id=1, source_target_pairs={{0,1},{3,2},{4,5},{7,6},{8,9},{11,10},{12,13},{15,14},{16,17},{19,... | collective-permute-start | bytes 2359304 | tf_op jit(solution)/shard_map/ppermute | solution.py:95
  315.7 3.6 %collective-permute-start.22 = (bf16[8,32,1024]{2,1,0:T(8,128)(2,1)S(1)}, bf16[8,32,1024]{2,1,0:T(8,128)(2,1)S(1)}, u32[]{:S(2)}, u32[]{:S(2)}) collective-permute-start(bf16[8,32,1024]{2,1,0:T(8,128)(2,1)S(1)} %add_convert_fusion.1), channel_id=1, source_target_pairs={{1,2},{2,1},{5,6},{6,5},{9,10},{10,9},{13,14},{14,13},{17,18},{18,... | collective-permute-start | bytes 1572872 | tf_op jit(solution)/shard_map/ppermute | solution.py:241
  316.8 4.1 %collective-permute-start.25 = (bf16[8,32,1024]{2,1,0:T(8,128)(2,1)S(1)}, bf16[8,32,1024]{2,1,0:T(8,128)(2,1)S(1)}, u32[]{:S(2)}, u32[]{:S(2)}) collective-permute-start(bf16[8,32,1024]{2,1,0:T(8,128)(2,1)S(1)} %add_convert_fusion), channel_id=1, source_target_pairs={{1,2},{2,1},{5,6},{6,5},{9,10},{10,9},{13,14},{14,13},{17,18},{18,... | collective-permute-start | bytes 1572872 | tf_op jit(solution)/shard_map/ppermute | solution.py:241
  317.7 19.1 %collective-permute-start.20 = (f32[4,32,1024]{2,1,0:T(8,128)S(1)}, f32[4,32,1024]{2,1,0:T(8,128)S(1)}, u32[]{:S(2)}, u32[]{:S(2)}) collective-permute-start(f32[4,32,1024]{2,1,0:T(8,128)S(1)} %slice_add_fusion.5), channel_id=1, source_target_pairs={{1,0},{2,3},{5,4},{6,7},{9,8},{10,11},{13,12},{14,15},{17,16},{18,... | collective-permute-start | bytes 1572872 | tf_op jit(solution)/shard_map/ppermute | solution.py:244
  319.6 23.2 %collective-permute-start.23 = (f32[4,32,1024]{2,1,0:T(8,128)S(1)}, f32[4,32,1024]{2,1,0:T(8,128)S(1)}, u32[]{:S(2)}, u32[]{:S(2)}) collective-permute-start(f32[4,32,1024]{2,1,0:T(8,128)S(1)} %slice_add_fusion.3), channel_id=1, source_target_pairs={{1,0},{2,3},{5,4},{6,7},{9,8},{10,11},{13,12},{14,15},{17,16},{18,... | collective-permute-start | bytes 1572872 | tf_op jit(solution)/shard_map/ppermute | solution.py:244
  321.1 27.3 %collective-permute-start.26 = (f32[4,32,1024]{2,1,0:T(8,128)S(1)}, f32[4,32,1024]{2,1,0:T(8,128)S(1)}, u32[]{:S(2)}, u32[]{:S(2)}) collective-permute-start(f32[4,32,1024]{2,1,0:T(8,128)S(1)} %slice_add_fusion.1), channel_id=1, source_target_pairs={{1,0},{2,3},{5,4},{6,7},{9,8},{10,11},{13,12},{14,15},{17,16},{18,... | collective-permute-start | bytes 1572872 | tf_op jit(solution)/shard_map/ppermute | solution.py:244
  (15 other events, 67.5 us)

commit v2 on v1

--- a/solution.py
+++ b/solution.py
@@ -125,32 +125,34 @@
 def cross_kernel(own_ref, src_ref, out_ref):
     segments = own_ref.shape[0]
     sources = src_ref.shape[1]
-    rows = own_ref.shape[1]
     bins = own_ref.shape[-1] // 2
 
-    def tile_body(tile, carry):
+    def tile_body(index, carry):
+        half = index // (bins // LANES)
+        tile = index % (bins // LANES)
+        rows = pl.ds(pl.multiple_of(half * ROWS, ROWS), ROWS)
         re_lanes = pl.ds(pl.multiple_of(tile * LANES, LANES), LANES)
         im_lanes = pl.ds(pl.multiple_of(bins + tile * LANES, LANES), LANES)
 
         def step(m, acc):
-            wr = own_ref[m, :, re_lanes].astype(jnp.float32)
-            wi = own_ref[m, :, im_lanes].astype(jnp.float32)
+            wr = own_ref[m, rows, re_lanes].astype(jnp.float32)
+            wi = own_ref[m, rows, im_lanes].astype(jnp.float32)
             out = []
             for j in range(sources):
-                sr = jnp.concatenate([src_ref[m, j, :, re_lanes]] * (rows // ROWS), axis=0)
-                si = jnp.concatenate([src_ref[m, j, :, im_lanes]] * (rows // ROWS), axis=0)
+                sr = src_ref[m, j, :, re_lanes]
+                si = src_ref[m, j, :, im_lanes]
                 out.append(acc[2 * j] + (wr * sr + wi * si))
                 out.append(acc[2 * j + 1] + (wi * sr - wr * si))
             return tuple(out)
 
-        acc = tuple(jnp.zeros((rows, LANES), jnp.float32) for _ in range(2 * sources))
+        acc = tuple(jnp.zeros((ROWS, LANES), jnp.float32) for _ in range(2 * sources))
         acc = lax.fori_loop(0, segments, step, acc)
         for j in range(sources):
-            out_ref[j, :, re_lanes] = acc[2 * j]
-            out_ref[j, :, im_lanes] = acc[2 * j + 1]
+            out_ref[j, rows, re_lanes] = acc[2 * j]
+            out_ref[j, rows, im_lanes] = acc[2 * j + 1]
         return carry
 
-    lax.fori_loop(0, bins // LANES, tile_body, 0)
+    lax.fori_loop(0, (own_ref.shape[1] // ROWS) * (bins // LANES), tile_body, 0)
 
 
 def cross_chunk(own, src):
@@ -194,8 +196,7 @@
     sample = jnp.arange(length, dtype=jnp.int32)
     bin_index = jnp.arange(bins, dtype=jnp.int32)
     angles = (sample[:, None] * bin_index[None, :] % length).astype(jnp.float32) * (2.0 * math.pi / length)
-    cosine = jnp.cos(angles)
-    sine = jnp.sin(angles)
+    cosine, sine = lax.optimization_barrier((jnp.cos(angles), jnp.sin(angles)))
     forward = jnp.concatenate([cosine, -sine], axis=1).astype(jnp.bfloat16)
     rows = traces.reshape(channels, seg_count, length).transpose(1, 0, 2)
     mask = valid.reshape(channels, seg_count).transpose(1, 0).astype(jnp.float32)[:, :, None]
@@ -223,16 +224,18 @@
     weight = jnp.where(bin_index == 0, 1.0, 2.0).astype(jnp.float32)[:, None] * factor
     inverse = jnp.concatenate([weight * cosine.T, -weight * sine.T], axis=0)
     is_edge = jnp.logical_or(place == 0, place == groups - 1)
-    far_wide, near_wide = widen(far, length), widen(near, length)
+    order = jnp.concatenate([far, near[:, per_group:], near[:, :per_group]], axis=1)
+    order_wide = widen(order, length)
     outs = []
     arrived = []
     for chunk in range(chunks):
         own = whitened[chunk]
         if chunk >= 2:
             own, _ = lax.optimization_barrier((own, arrived[chunk - 2]))
-        far_part = cross_chunk(own, far_wide)
-        near_part = cross_chunk(own, near_wide)
-        edge_out = jnp.concatenate([far_part, near_part[per_group:]], axis=0).astype(jnp.bfloat16)
+        part = cross_chunk(own, order_wide)
+        far_part = part[:half]
+        near_part = jnp.concatenate([part[source_count - per_group:], part[half:source_count - per_group]], axis=0)
+        edge_out = part[:source_count - per_group].astype(jnp.bfloat16)
         if arrived:
             edge_out, _ = lax.optimization_barrier((edge_out, arrived[-1]))
         edge_in = edge_first(edge_out, groups)

time: 353 us -> 353 us (level)
  local copies, waits for them, and re-layouts: 29.8 us -> 39.9 us
  other arithmetic: 55.5 us -> 45.6 us
  Pallas kernels: 111 us -> 102 us
  matrix products: 26.8 us -> 35.2 us
  starting transfers between devices: 77.1 us -> 81.5 us
    another operation x9 -> x0, other arithmetic: 12.8 us -> none
    pallas_call x16 -> x8, Pallas kernels: 96.2 us -> 86.4 us  [cross_chunk(): pl.pallas_call(cross_kernel, grid=(width // step_rows,), in_specs=[pl.Blo...]
    sin x0 -> x1, other arithmetic: none -> 9.12 us  [on_line(): cosine, sine = lax.optimization_barrier((jnp.cos(angles), jnp.sin(angles)))]
    slice x8 -> x9, local copies, waits for them, and re-layouts: 9.1 us -> 18.1 us  [the longest x8 18.1 us: on_line(): edge_out = part[:source_count - per_group].astype(jnp.bfloat16)]
    dot_general x8, matrix products: 26.8 us -> 35.2 us  [on_line(): outs.append(jnp.dot(final, inverse, precision=lax.Precision.HIGH))]
    concatenate x8 -> x0, other arithmetic: 5.97 us -> none  [on_line(): jnp.concatenate([far_part, near_part[per_group:]], axis=0)]
    mul x1 -> x2, other arithmetic: 9.23 us -> 3.74 us  [on_line(): inverse = jnp.concatenate([weight * cosine.T, -weight * sine.T], axis=0)]
    add x8, other arithmetic: 4.79 us -> 9.72 us  [on_line(): low = near_part[:per_group] + got[:per_group]]
  transfers between devices with their start and end apart: 27 -> 27, of which waited for: 8 -> 8; matrix products, arithmetic and copies ran while one was open for 23% -> 23% of each run, Pallas kernels for 24% -> 22%
where the time goes in v2:
time: 353 us; the launch traced here: 351 us
  Pallas kernels  102 us (29%)
  starting transfers between devices  81.5 us (23%)
  other arithmetic  45.6 us (13%)
  local copies, waits for them, and re-layouts  39.9 us (11%)
  matrix products  35.2 us (10%)
  waiting for transfers between devices  31.5 us (9%)
  between operations  16 us (5%)
    pallas_call x8, Pallas kernels, cross_chunk(): pl.pallas_call(cross_kernel, grid=(width // step_rows,), in_specs=[pl.Blo...  86.4 us
    ppermute x8, starting transfers between devices, edge_first(): return lax.ppermute(values, 'tm', [(0, 1), (groups - 1, groups - 2)])  56.3 us
    dot_general x8, matrix products, on_line(): outs.append(jnp.dot(final, inverse, precision=lax.Precision.HIGH))  35.2 us
    slice x8, local copies, waits for them, and re-layouts, on_line(): edge_out = part[:source_count - per_group].astype(jnp.bfloat16)  18.1 us
    pallas_call x1, Pallas kernels, whiten_segments(): pl.pallas_call(whiten_kernel, grid=(segments,), in_specs=[pl.BlockSpec((N...  15.3 us
    ppermute x8, waiting for transfers between devices, on_line(): back = lax.ppermute(low, 'tm', [(1, 0), (2, 3)])  14.9 us
    ppermute x3, waiting for transfers between devices, butterfly_sum(): lax.ppermute(values, axis, [(b, b ^ step) for b in range(count)])  14.1 us
    convert_element_type x8, other arithmetic, on_line(): far_total.astype(jnp.bfloat16)  12.5 us
  transfers between devices with their start and end apart: 27, of which 8 were waited for; matrix products, arithmetic and copies ran while one was open for 23% of the time, Pallas kernels for 22%

profile of v2, /device:TPU:0, one launch (start us, length us, event | category | flops | bytes accessed | tf_op | source)
XLA Modules:
  0.0 351.3 jit_solution(8867179326720087444)
XLA Ops:
  0.0 9.1 %fusion.14 = (f32[1024,512]{1,0:T(8,128)}, f32[1024,512]{1,0:T(8,128)}) fusion(), kind=kLoop, calls=%fused_computation.46 | loop fusion | flops 7340032 | bytes 4194304 | tf_op jit(solution)/shard_map/sin | solution.py:199
  22.8 7.6 %copy.15 = bf16[256,2,6,1024]{3,0,2,1:T(8,128)(2,1)} copy(bf16[256,2,6,1024]{3,1,2,0:T(2,128)(2,1)} %param.4) | data formatting | bytes 12582912 | tf_op args[0]
  35.2 2.1 multiply_bitcast_fusion
  40.6 15.3 %shard_map.46 = bf16[8,12,32,1024]{3,2,1,0:T(8,128)(2,1)} custom-call(bf16[12,256,1024]{2,1,0:T(8,128)(2,1)} %bitcast.61, bf16[1024,1024]{1,0:T(8,128)(2,1)} %pad_maximum_fusion.forward_ref, f32[12,256,1]{2,1,0:T(8,128)} %copy.17.mask_ref), custom_call_target="tpu_custom_call" | custom-call | tf_op jit(solution)/shard_map/pallas_call | solution.py:108
  59.9 2.9 collective-permute-start.1
  62.8 9.4 %collective-permute-done.1 = bf16[12,16,1024]{2,1,0:T(8,128)(2,1)S(1)} collective-permute-done((bf16[12,16,1024]{2,1,0:T(8,128)(2,1)S(1)}, bf16[12,16,1024]{2,1,0:T(8,128)(2,1)S(1)}, u32[]{:S(2)}, u32[]{:S(2)}) %collective-permute-start.1) | collective-permute-done | bytes 393248 | tf_op jit(solution)/shard_map/ppermute | solution.py:178
  74.2 5.6 %slice_bitcast_fusion = (bf16[12,32,1024]{2,1,0:T(8,128)(2,1)}, bf16[12,32,1024]{2,1,0:T(8,128)(2,1)}, bf16[12,32,1024]{2,1,0:T(8,128)(2,1)}, bf16[12,32,1024]{2...) fusion(bf16[8,12,32,1024]{3,2,1,0:T(8,128)(2,1)} %shard_map.46), kind=kLoop, calls=%fused_computation.48 | loop fusion | bytes 12582912 | tf_op jit(solution)/shard_map/squeeze | solution.py:232
  79.8 3.3 collective-permute-done.2
  83.7 3.5 broadcast_in_dim.29.src_ref
  87.2 10.8 %shard_map.47 = f32[16,32,1024]{2,1,0:T(8,128)} custom-call(bf16[12,32,1024]{2,1,0:T(8,128)(2,1)} %get-tuple-element.42.own_ref, f32[12,16,8,1024]{3,2,1,0:T(8,128)} %broadcast_in_dim.29.src_ref), custom_call_target="tpu_custom_call" | custom-call | tf_op jit(solution)/shard_map/pallas_call | solution.py:162
  98.0 2.5 slice.627
  100.5 4.3 %collective-permute-start.3 = (bf16[12,32,1024]{2,1,0:T(8,128)(2,1)}, bf16[12,32,1024]{2,1,0:T(8,128)(2,1)}, u32[]{:S(2)}, u32[]{:S(2)}) collective-permute-start(bf16[12,32,1024]{2,1,0:T(8,128)(2,1)} %slice.627), channel_id=1, source_target_pairs={{0,1},{3,2},{4,5},{7,6},{8,9},{11,10},{12,13},{15,14},{16,17},{19,... | collective-permute-start | bytes 2359304 | tf_op jit(solution)/shard_map/ppermute | solution.py:95
  104.8 10.8 %shard_map.48 = f32[16,32,1024]{2,1,0:T(8,128)} custom-call(bf16[12,32,1024]{2,1,0:T(8,128)(2,1)} %get-tuple-element.41.own_ref, f32[12,16,8,1024]{3,2,1,0:T(8,128)} %broadcast_in_dim.29.src_ref), custom_call_target="tpu_custom_call" | custom-call | tf_op jit(solution)/shard_map/pallas_call | solution.py:162
  117.1 2.5 collective-permute-done.3
  119.6 5.3 %collective-permute-start.6 = (bf16[12,32,1024]{2,1,0:T(8,128)(2,1)S(1)}, bf16[12,32,1024]{2,1,0:T(8,128)(2,1)}, u32[]{:S(2)}, u32[]{:S(2)}) collective-permute-start(bf16[12,32,1024]{2,1,0:T(8,128)(2,1)S(1)} %slice.626), channel_id=1, source_target_pairs={{0,1},{3,2},{4,5},{7,6},{8,9},{11,10},{12,13},{15,14},{16,17},{19,... | collective-permute-start | bytes 2359304 | tf_op jit(solution)/shard_map/ppermute | solution.py:95
  124.9 10.8 %shard_map.49 = f32[16,32,1024]{2,1,0:T(8,128)} custom-call(bf16[12,32,1024]{2,1,0:T(8,128)(2,1)} %get-tuple-element.23.own_ref, f32[12,16,8,1024]{3,2,1,0:T(8,128)} %broadcast_in_dim.29.src_ref), custom_call_target="tpu_custom_call" | custom-call | tf_op jit(solution)/shard_map/pallas_call | solution.py:162
  135.7 2.6 slice.625
  138.3 5.4 %collective-permute-start.9 = (bf16[12,32,1024]{2,1,0:T(8,128)(2,1)}, bf16[12,32,1024]{2,1,0:T(8,128)(2,1)}, u32[]{:S(2)}, u32[]{:S(2)}) collective-permute-start(bf16[12,32,1024]{2,1,0:T(8,128)(2,1)} %slice.625), channel_id=1, source_target_pairs={{0,1},{3,2},{4,5},{7,6},{8,9},{11,10},{12,13},{15,14},{16,17},{19,... | collective-permute-start | bytes 2359304 | tf_op jit(solution)/shard_map/ppermute | solution.py:95
  146.8 2.0 fusion.12
  151.4 10.8 %shard_map.50 = f32[16,32,1024]{2,1,0:T(8,128)} custom-call(bf16[12,32,1024]{2,1,0:T(8,128)(2,1)} %get-tuple-element.25.own_ref, f32[12,16,8,1024]{3,2,1,0:T(8,128)} %broadcast_in_dim.29.src_ref), custom_call_target="tpu_custom_call" | custom-call | tf_op jit(solution)/shard_map/pallas_call | solution.py:162
  162.2 2.4 slice.624
  164.6 13.3 %collective-permute-start.12 = (bf16[12,32,1024]{2,1,0:T(8,128)(2,1)}, bf16[12,32,1024]{2,1,0:T(8,128)(2,1)}, u32[]{:S(2)}, u32[]{:S(2)}) collective-permute-start(bf16[12,32,1024]{2,1,0:T(8,128)(2,1)} %slice.624), channel_id=1, source_target_pairs={{0,1},{3,2},{4,5},{7,6},{8,9},{11,10},{12,13},{15,14},{16,17},{19,... | collective-permute-start | bytes 2359304 | tf_op jit(solution)/shard_map/ppermute | solution.py:95
  177.9 1.9 slice_add_fusion.39
  183.2 1.9 slice_add_fusion.35
  186.4 2.0 fusion.11
  189.9 10.8 %shard_map.51 = f32[16,32,1024]{2,1,0:T(8,128)} custom-call(bf16[12,32,1024]{2,1,0:T(8,128)(2,1)} %get-tuple-element.27.own_ref, f32[12,16,8,1024]{3,2,1,0:T(8,128)} %broadcast_in_dim.29.src_ref), custom_call_target="tpu_custom_call" | custom-call | tf_op jit(solution)/shard_map/pallas_call | solution.py:162
  200.7 2.4 slice.623
  203.1 9.0 %collective-permute-start.15 = (bf16[12,32,1024]{2,1,0:T(8,128)(2,1)}, bf16[12,32,1024]{2,1,0:T(8,128)(2,1)}, u32[]{:S(2)}, u32[]{:S(2)}) collective-permute-start(bf16[12,32,1024]{2,1,0:T(8,128)(2,1)} %slice.623), channel_id=1, source_target_pairs={{0,1},{3,2},{4,5},{7,6},{8,9},{11,10},{12,13},{15,14},{16,17},{19,... | collective-permute-start | bytes 2359304 | tf_op jit(solution)/shard_map/ppermute | solution.py:95
  212.1 5.3 %convolution_dynamic-update-slice_fusion.7 = f32[4,256,1024]{2,1,0:T(8,128)} fusion(f32[8,32,1024]{2,1,0:T(8,128)S(1)} %convert_element_type.138, f32[16,32,1024]{2,1,0:T(8,128)} %shard_map.47, f32[4,32,1024]{2,1,0:T(8,128)} %collective-permute-done.5, bf16[12,32,1024]{2,1,0:T(8,128)(2,1)} %collective-permute-done.3, pred[]{:T(512)S(6)} %or.3, ...), kind=kOutput, calls=%fused_computation.29 | convolution fusion | flops 807010304 | bytes 7077889 | tf_op jit(solution)/shard_map/dot_general | solution.py:249
  217.5 4.5 %convolution_dynamic-update-slice_fusion.6 = f32[4,256,1024]{2,1,0:T(8,128)} fusion(f32[4,256,1024]{2,1,0:T(8,128)} %convolution_dynamic-update-slice_fusion.7, f32[8,32,1024]{2,1,0:T(8,128)S(1)} %copy-done.14, f32[16,32,1024]{2,1,0:T(8,128)} %shard_map.48, f32[4,32,1024]{2,1,0:T(8,128)} %collective-permute-done.8, ...), kind=kOutput, calls=%fused_computation.28 | convolution fusion | flops 807010304 | bytes 7077889 | tf_op jit(solution)/shard_map/dot_general | solution.py:249
  226.3 10.8 %shard_map.52 = f32[16,32,1024]{2,1,0:T(8,128)} custom-call(bf16[12,32,1024]{2,1,0:T(8,128)(2,1)} %get-tuple-element.29.own_ref, f32[12,16,8,1024]{3,2,1,0:T(8,128)} %broadcast_in_dim.29.src_ref), custom_call_target="tpu_custom_call" | custom-call | tf_op jit(solution)/shard_map/pallas_call | solution.py:162
  237.1 2.6 slice.622
  239.8 6.3 %collective-permute-start.18 = (bf16[12,32,1024]{2,1,0:T(8,128)(2,1)}, bf16[12,32,1024]{2,1,0:T(8,128)(2,1)}, u32[]{:S(2)}, u32[]{:S(2)}) collective-permute-start(bf16[12,32,1024]{2,1,0:T(8,128)(2,1)} %slice.622), channel_id=1, source_target_pairs={{0,1},{3,2},{4,5},{7,6},{8,9},{11,10},{12,13},{15,14},{16,17},{19,... | collective-permute-start | bytes 2359304 | tf_op jit(solution)/shard_map/ppermute | solution.py:95
  248.3 2.0 fusion.9
  251.8 4.5 %convolution_dynamic-update-slice_fusion.5 = f32[4,256,1024]{2,1,0:T(8,128)} fusion(f32[4,256,1024]{2,1,0:T(8,128)} %convolution_dynamic-update-slice_fusion.6, f32[8,32,1024]{2,1,0:T(8,128)S(1)} %convert_element_type.146, f32[16,32,1024]{2,1,0:T(8,128)} %shard_map.49, f32[4,32,1024]{2,1,0:T(8,128)} %collective-permute-done.11, ...), kind=kOutput, calls=%fused_computation.27 | convolution fusion | flops 807010304 | bytes 7077889 | tf_op jit(solution)/shard_map/dot_general | solution.py:249
  256.4 10.8 %shard_map.53 = f32[16,32,1024]{2,1,0:T(8,128)} custom-call(bf16[12,32,1024]{2,1,0:T(8,128)(2,1)} %get-tuple-element.31.own_ref, f32[12,16,8,1024]{3,2,1,0:T(8,128)} %broadcast_in_dim.29.src_ref), custom_call_target="tpu_custom_call" | custom-call | tf_op jit(solution)/shard_map/pallas_call | solution.py:162
  267.2 2.5 slice.621
  269.7 5.2 %collective-permute-start.21 = (bf16[12,32,1024]{2,1,0:T(8,128)(2,1)}, bf16[12,32,1024]{2,1,0:T(8,128)(2,1)}, u32[]{:S(2)}, u32[]{:S(2)}) collective-permute-start(bf16[12,32,1024]{2,1,0:T(8,128)(2,1)} %slice.621), channel_id=1, source_target_pairs={{0,1},{3,2},{4,5},{7,6},{8,9},{11,10},{12,13},{15,14},{16,17},{19,... | collective-permute-start | bytes 2359304 | tf_op jit(solution)/shard_map/ppermute | solution.py:95
  280.2 1.9 slice_add_fusion.23
  283.4 2.0 fusion.8
  286.8 10.8 %shard_map.54 = f32[16,32,1024]{2,1,0:T(8,128)} custom-call(bf16[12,32,1024]{2,1,0:T(8,128)(2,1)} %get-tuple-element.33.own_ref, f32[12,16,8,1024]{3,2,1,0:T(8,128)} %broadcast_in_dim.29.src_ref), custom_call_target="tpu_custom_call" | custom-call | tf_op jit(solution)/shard_map/pallas_call | solution.py:162
  299.2 7.4 %collective-permute-start.24 = (bf16[12,32,1024]{2,1,0:T(8,128)(2,1)S(1)}, bf16[12,32,1024]{2,1,0:T(8,128)(2,1)S(1)}, u32[]{:S(2)}, u32[]{:S(2)}) collective-permute-start(bf16[12,32,1024]{2,1,0:T(8,128)(2,1)S(1)} %slice.620), channel_id=1, source_target_pairs={{0,1},{3,2},{4,5},{7,6},{8,9},{11,10},{12,13},{15,14},{16,17},{19,... | collective-permute-start | bytes 2359304 | tf_op jit(solution)/shard_map/ppermute | solution.py:95
  306.7 5.2 %convolution_dynamic-update-slice_fusion.4 = f32[4,256,1024]{2,1,0:T(8,128)} fusion(f32[4,256,1024]{2,1,0:T(8,128)} %convolution_dynamic-update-slice_fusion.5, f32[8,32,1024]{2,1,0:T(8,128)S(1)} %convert_element_type.150, f32[16,32,1024]{2,1,0:T(8,128)} %shard_map.50, f32[4,32,1024]{2,1,0:T(8,128)} %collective-permute-done.14, ...), kind=kOutput, calls=%fused_computation.26 | convolution fusion | flops 807010304 | bytes 7077889 | tf_op jit(solution)/shard_map/dot_general | solution.py:249
  311.9 4.6 %convolution_dynamic-update-slice_fusion.3 = f32[4,256,1024]{2,1,0:T(8,128)} fusion(f32[4,256,1024]{2,1,0:T(8,128)} %convolution_dynamic-update-slice_fusion.4, f32[8,32,1024]{2,1,0:T(8,128)S(1)} %copy-done.12, f32[16,32,1024]{2,1,0:T(8,128)} %shard_map.51, f32[4,32,1024]{2,1,0:T(8,128)} %collective-permute-done.17, ...), kind=kOutput, calls=%fused_computation.25 | convolution fusion | flops 807010304 | bytes 7077889 | tf_op jit(solution)/shard_map/dot_general | solution.py:249
  325.4 11.7 %collective-permute-done.20 = f32[4,32,1024]{2,1,0:T(8,128)S(1)} collective-permute-done((f32[4,32,1024]{2,1,0:T(8,128)S(1)}, f32[4,32,1024]{2,1,0:T(8,128)S(1)}, u32[]{:S(2)}, u32[]{:S(2)}) %collective-permute-start.20) | collective-permute-done | bytes 524320 | tf_op jit(solution)/shard_map/ppermute | solution.py:247
  337.0 4.0 %convolution_dynamic-update-slice_fusion.2 = f32[4,256,1024]{2,1,0:T(8,128)} fusion(f32[4,256,1024]{2,1,0:T(8,128)} %convolution_dynamic-update-slice_fusion.3, f32[8,32,1024]{2,1,0:T(8,128)S(1)} %convert_element_type.158, f32[16,32,1024]{2,1,0:T(8,128)S(1)} %copy-done.4, f32[4,32,1024]{2,1,0:T(8,128)S(1)} %collective-permute-done.20, ...), kind=kOutput, calls=%fused_computation.24 | convolution fusion | flops 807010304 | bytes 7077889 | tf_op jit(solution)/shard_map/dot_general | solution.py:249
  342.6 4.0 %convolution_dynamic-update-slice_fusion.1 = f32[4,256,1024]{2,1,0:T(8,128)} fusion(f32[4,256,1024]{2,1,0:T(8,128)} %convolution_dynamic-update-slice_fusion.2, f32[8,32,1024]{2,1,0:T(8,128)S(1)} %convert_element_type.162, f32[16,32,1024]{2,1,0:T(8,128)S(1)} %copy-done.7, f32[4,32,1024]{2,1,0:T(8,128)S(1)} %collective-permute-done.23, ...), kind=kOutput, calls=%fused_computation.23 | convolution fusion | flops 807010304 | bytes 7077889 | tf_op jit(solution)/shard_map/dot_general | solution.py:249
  348.3 3.1 convolution_dynamic-update-slice_fusion
  (115 shorter events, 55.7 us)
Async XLA Ops:
  0.0 9.1 %copy-start.16 = (s32[4]{0:T(128)S(1)}, s32[4]{0:T(128)}, u32[]{:S(2)}) copy-start(s32[4]{0:T(128)} %param.7) | copy-start | bytes 52
  22.7 7.6 %copy-start.15 = (s32[256,2,6]{0,1,2:T(2,128)S(1)}, s32[256,2,6]{0,1,2:T(2,128)}, u32[]{:S(2)}) copy-start(s32[256,2,6]{0,1,2:T(2,128)} %param.5) | copy-start | bytes 36868
  22.8 9.3 %copy-start.17 = (s32[4]{0:T(128)S(1)}, s32[4]{0:T(128)}, u32[]{:S(2)}) copy-start(s32[4]{0:T(128)} %param.6) | copy-start | bytes 52
  35.2 2.2 copy-start.10
  57.8 1.9 collective-permute-start
  59.9 12.3 %collective-permute-start.1 = (bf16[12,16,1024]{2,1,0:T(8,128)(2,1)S(1)}, bf16[12,16,1024]{2,1,0:T(8,128)(2,1)S(1)}, u32[]{:S(2)}, u32[]{:S(2)}) collective-permute-start(bf16[12,16,1024]{2,1,0:T(8,128)(2,1)S(1)} %fusion.73), channel_id=1, source_target_pairs={{0,8},{4,12},{8,0},{12,4},{16,24},{20,28},{24,16},{28,20},{1,9},{5... | collective-permute-start | bytes 1179656 | tf_op jit(solution)/shard_map/ppermute | solution.py:178
  72.4 10.7 %collective-permute-start.2 = (bf16[12,16,1024]{2,1,0:T(8,128)(2,1)S(1)}, bf16[12,16,1024]{2,1,0:T(8,128)(2,1)S(1)}, u32[]{:S(2)}, u32[]{:S(2)}) collective-permute-start(bf16[12,16,1024]{2,1,0:T(8,128)(2,1)S(1)} %add.192), channel_id=1, source_target_pairs={{0,16},{4,20},{8,24},{12,28},{16,0},{20,4},{24,8},{28,12},{1,17},{... | collective-permute-start | bytes 1179656 | tf_op jit(solution)/shard_map/ppermute | solution.py:178
  100.5 19.1 %collective-permute-start.3 = (bf16[12,32,1024]{2,1,0:T(8,128)(2,1)}, bf16[12,32,1024]{2,1,0:T(8,128)(2,1)}, u32[]{:S(2)}, u32[]{:S(2)}) collective-permute-start(bf16[12,32,1024]{2,1,0:T(8,128)(2,1)} %slice.627), channel_id=1, source_target_pairs={{0,1},{3,2},{4,5},{7,6},{8,9},{11,10},{12,13},{15,14},{16,17},{19,... | collective-permute-start | bytes 2359304 | tf_op jit(solution)/shard_map/ppermute | solution.py:95
  119.6 18.8 %collective-permute-start.6 = (bf16[12,32,1024]{2,1,0:T(8,128)(2,1)S(1)}, bf16[12,32,1024]{2,1,0:T(8,128)(2,1)}, u32[]{:S(2)}, u32[]{:S(2)}) collective-permute-start(bf16[12,32,1024]{2,1,0:T(8,128)(2,1)S(1)} %slice.626), channel_id=1, source_target_pairs={{0,1},{3,2},{4,5},{7,6},{8,9},{11,10},{12,13},{15,14},{16,17},{19,... | collective-permute-start | bytes 2359304 | tf_op jit(solution)/shard_map/ppermute | solution.py:95
  135.7 11.1 %copy-start.9 = (f32[16,32,1024]{2,1,0:T(8,128)S(1)}, f32[16,32,1024]{2,1,0:T(8,128)}, u32[]{:S(2)}) copy-start(f32[16,32,1024]{2,1,0:T(8,128)} %shard_map.48) | copy-start | bytes 6291460
  138.3 26.2 %collective-permute-start.9 = (bf16[12,32,1024]{2,1,0:T(8,128)(2,1)}, bf16[12,32,1024]{2,1,0:T(8,128)(2,1)}, u32[]{:S(2)}, u32[]{:S(2)}) collective-permute-start(bf16[12,32,1024]{2,1,0:T(8,128)(2,1)} %slice.625), channel_id=1, source_target_pairs={{0,1},{3,2},{4,5},{7,6},{8,9},{11,10},{12,13},{15,14},{16,17},{19,... | collective-permute-start | bytes 2359304 | tf_op jit(solution)/shard_map/ppermute | solution.py:95
  145.3 4.9 %collective-permute-start.4 = (bf16[8,32,1024]{2,1,0:T(8,128)(2,1)S(1)}, bf16[8,32,1024]{2,1,0:T(8,128)(2,1)}, u32[]{:S(2)}, u32[]{:S(2)}) collective-permute-start(bf16[8,32,1024]{2,1,0:T(8,128)(2,1)S(1)} %fusion.13), channel_id=1, source_target_pairs={{1,2},{2,1},{5,6},{6,5},{9,10},{10,9},{13,14},{14,13},{17,18},{18,... | collective-permute-start | bytes 1572872 | tf_op jit(solution)/shard_map/ppermute | solution.py:244
  148.8 32.3 %collective-permute-start.7 = (bf16[8,32,1024]{2,1,0:T(8,128)(2,1)}, bf16[8,32,1024]{2,1,0:T(8,128)(2,1)}, u32[]{:S(2)}, u32[]{:S(2)}) collective-permute-start(bf16[8,32,1024]{2,1,0:T(8,128)(2,1)} %fusion.12), channel_id=1, source_target_pairs={{1,2},{2,1},{5,6},{6,5},{9,10},{10,9},{13,14},{14,13},{17,18},{18,... | collective-permute-start | bytes 1572872 | tf_op jit(solution)/shard_map/ppermute | solution.py:244
  164.6 21.8 %copy-start.6 = (f32[16,32,1024]{2,1,0:T(8,128)S(1)}, f32[16,32,1024]{2,1,0:T(8,128)}, u32[]{:S(2)}) copy-start(f32[16,32,1024]{2,1,0:T(8,128)} %shard_map.49) | copy-start | bytes 6291460
  164.6 38.5 %collective-permute-start.12 = (bf16[12,32,1024]{2,1,0:T(8,128)(2,1)}, bf16[12,32,1024]{2,1,0:T(8,128)(2,1)}, u32[]{:S(2)}, u32[]{:S(2)}) collective-permute-start(bf16[12,32,1024]{2,1,0:T(8,128)(2,1)} %slice.624), channel_id=1, source_target_pairs={{0,1},{3,2},{4,5},{7,6},{8,9},{11,10},{12,13},{15,14},{16,17},{19,... | collective-permute-start | bytes 2359304 | tf_op jit(solution)/shard_map/ppermute | solution.py:95
  179.8 32.4 %collective-permute-start.5 = (f32[4,32,1024]{2,1,0:T(8,128)}, f32[4,32,1024]{2,1,0:T(8,128)}, u32[]{:S(2)}, u32[]{:S(2)}) collective-permute-start(f32[4,32,1024]{2,1,0:T(8,128)} %slice_add_fusion.39), channel_id=1, source_target_pairs={{1,0},{2,3},{5,4},{6,7},{9,8},{10,11},{13,12},{14,15},{17,16},{18,... | collective-permute-start | bytes 1572872 | tf_op jit(solution)/shard_map/ppermute | solution.py:247
  182.2 1.0 copy-start.13
  185.1 32.4 %collective-permute-start.8 = (f32[4,32,1024]{2,1,0:T(8,128)}, f32[4,32,1024]{2,1,0:T(8,128)}, u32[]{:S(2)}, u32[]{:S(2)}) collective-permute-start(f32[4,32,1024]{2,1,0:T(8,128)} %slice_add_fusion.35), channel_id=1, source_target_pairs={{1,0},{2,3},{5,4},{6,7},{9,8},{10,11},{13,12},{14,15},{17,16},{18,... | collective-permute-start | bytes 1572872 | tf_op jit(solution)/shard_map/ppermute | solution.py:247
  188.4 33.6 %collective-permute-start.10 = (bf16[8,32,1024]{2,1,0:T(8,128)(2,1)}, bf16[8,32,1024]{2,1,0:T(8,128)(2,1)}, u32[]{:S(2)}, u32[]{:S(2)}) collective-permute-start(bf16[8,32,1024]{2,1,0:T(8,128)(2,1)} %fusion.11), channel_id=1, source_target_pairs={{1,2},{2,1},{5,6},{6,5},{9,10},{10,9},{13,14},{14,13},{17,18},{18,... | collective-permute-start | bytes 1572872 | tf_op jit(solution)/shard_map/ppermute | solution.py:244
  203.1 36.6 %collective-permute-start.15 = (bf16[12,32,1024]{2,1,0:T(8,128)(2,1)}, bf16[12,32,1024]{2,1,0:T(8,128)(2,1)}, u32[]{:S(2)}, u32[]{:S(2)}) collective-permute-start(bf16[12,32,1024]{2,1,0:T(8,128)(2,1)} %slice.623), channel_id=1, source_target_pairs={{0,1},{3,2},{4,5},{7,6},{8,9},{11,10},{12,13},{15,14},{16,17},{19,... | collective-permute-start | bytes 2359304 | tf_op jit(solution)/shard_map/ppermute | solution.py:95
  212.1 5.3 %copy-start = (f32[512,1024]{0,1:T(8,128)S(1)}, f32[512,1024]{0,1:T(8,128)}, u32[]{:S(2)}) copy-start(f32[512,1024]{0,1:T(8,128)} %get-tuple-element.47) | copy-start | bytes 6291460
  212.1 5.3 %copy-start.14 = (f32[8,32,1024]{2,1,0:T(8,128)S(1)}, f32[8,32,1024]{2,1,0:T(8,128)}, u32[]{:S(2)}) copy-start(f32[8,32,1024]{2,1,0:T(8,128)} %copy-done.13) | copy-start | bytes 3145732
  225.0 26.7 %collective-permute-start.11 = (f32[4,32,1024]{2,1,0:T(8,128)}, f32[4,32,1024]{2,1,0:T(8,128)}, u32[]{:S(2)}, u32[]{:S(2)}) collective-permute-start(f32[4,32,1024]{2,1,0:T(8,128)} %slice_add_fusion.31), channel_id=1, source_target_pairs={{1,0},{2,3},{5,4},{6,7},{9,8},{10,11},{13,12},{14,15},{17,16},{18,... | collective-permute-start | bytes 1572872 | tf_op jit(solution)/shard_map/ppermute | solution.py:247
  237.1 11.2 %copy-start.5 = (f32[16,32,1024]{2,1,0:T(8,128)S(1)}, f32[16,32,1024]{2,1,0:T(8,128)}, u32[]{:S(2)}) copy-start(f32[16,32,1024]{2,1,0:T(8,128)} %shard_map.51) | copy-start | bytes 6291460
  239.7 12.0 %copy-start.1 = (f32[512,1024]{0,1:T(8,128)S(1)}, f32[512,1024]{0,1:T(8,128)}, u32[]{:S(2)}) copy-start(f32[512,1024]{0,1:T(8,128)} %get-tuple-element.47) | copy-start | bytes 6291460
  239.8 29.9 %collective-permute-start.18 = (bf16[12,32,1024]{2,1,0:T(8,128)(2,1)}, bf16[12,32,1024]{2,1,0:T(8,128)(2,1)}, u32[]{:S(2)}, u32[]{:S(2)}) collective-permute-start(bf16[12,32,1024]{2,1,0:T(8,128)(2,1)} %slice.622), channel_id=1, source_target_pairs={{0,1},{3,2},{4,5},{7,6},{8,9},{11,10},{12,13},{15,14},{16,17},{19,... | collective-permute-start | bytes 2359304 | tf_op jit(solution)/shard_map/ppermute | solution.py:95
  247.6 8.7 %collective-permute-start.13 = (bf16[8,32,1024]{2,1,0:T(8,128)(2,1)S(1)}, bf16[8,32,1024]{2,1,0:T(8,128)(2,1)S(1)}, u32[]{:S(2)}, u32[]{:S(2)}) collective-permute-start(bf16[8,32,1024]{2,1,0:T(8,128)(2,1)S(1)} %fusion.10), channel_id=1, source_target_pairs={{1,2},{2,1},{5,6},{6,5},{9,10},{10,9},{13,14},{14,13},{17,18},{18,... | collective-permute-start | bytes 1572872 | tf_op jit(solution)/shard_map/ppermute | solution.py:244
  250.3 27.7 %collective-permute-start.16 = (bf16[8,32,1024]{2,1,0:T(8,128)(2,1)}, bf16[8,32,1024]{2,1,0:T(8,128)(2,1)}, u32[]{:S(2)}, u32[]{:S(2)}) collective-permute-start(bf16[8,32,1024]{2,1,0:T(8,128)(2,1)} %fusion.9), channel_id=1, source_target_pairs={{1,2},{2,1},{5,6},{6,5},{9,10},{10,9},{13,14},{14,13},{17,18},{18,... | collective-permute-start | bytes 1572872 | tf_op jit(solution)/shard_map/ppermute | solution.py:244
  269.7 13.7 %copy-start.3 = (f32[16,32,1024]{2,1,0:T(8,128)S(1)}, f32[16,32,1024]{2,1,0:T(8,128)}, u32[]{:S(2)}) copy-start(f32[16,32,1024]{2,1,0:T(8,128)} %shard_map.52) | copy-start | bytes 6291460
  269.7 29.5 %collective-permute-start.21 = (bf16[12,32,1024]{2,1,0:T(8,128)(2,1)}, bf16[12,32,1024]{2,1,0:T(8,128)(2,1)}, u32[]{:S(2)}, u32[]{:S(2)}) collective-permute-start(bf16[12,32,1024]{2,1,0:T(8,128)(2,1)} %slice.621), channel_id=1, source_target_pairs={{0,1},{3,2},{4,5},{7,6},{8,9},{11,10},{12,13},{15,14},{16,17},{19,... | collective-permute-start | bytes 2359304 | tf_op jit(solution)/shard_map/ppermute | solution.py:95
  276.7 29.9 %collective-permute-start.14 = (f32[4,32,1024]{2,1,0:T(8,128)}, f32[4,32,1024]{2,1,0:T(8,128)}, u32[]{:S(2)}, u32[]{:S(2)}) collective-permute-start(f32[4,32,1024]{2,1,0:T(8,128)} %slice_add_fusion.27), channel_id=1, source_target_pairs={{1,0},{2,3},{5,4},{6,7},{9,8},{10,11},{13,12},{14,15},{17,16},{18,... | collective-permute-start | bytes 1572872 | tf_op jit(solution)/shard_map/ppermute | solution.py:247
  279.2 1.0 copy-start.11
  282.1 29.8 %collective-permute-start.17 = (f32[4,32,1024]{2,1,0:T(8,128)}, f32[4,32,1024]{2,1,0:T(8,128)}, u32[]{:S(2)}, u32[]{:S(2)}) collective-permute-start(f32[4,32,1024]{2,1,0:T(8,128)} %slice_add_fusion.23), channel_id=1, source_target_pairs={{1,0},{2,3},{5,4},{6,7},{9,8},{10,11},{13,12},{14,15},{17,16},{18,... | collective-permute-start | bytes 1572872 | tf_op jit(solution)/shard_map/ppermute | solution.py:247
  285.4 31.2 %collective-permute-start.19 = (bf16[8,32,1024]{2,1,0:T(8,128)(2,1)}, bf16[8,32,1024]{2,1,0:T(8,128)(2,1)}, u32[]{:S(2)}, u32[]{:S(2)}) collective-permute-start(bf16[8,32,1024]{2,1,0:T(8,128)(2,1)} %fusion.8), channel_id=1, source_target_pairs={{1,2},{2,1},{5,6},{6,5},{9,10},{10,9},{13,14},{14,13},{17,18},{18,... | collective-permute-start | bytes 1572872 | tf_op jit(solution)/shard_map/ppermute | solution.py:244
  299.2 12.7 %copy-start.2 = (f32[512,1024]{0,1:T(8,128)S(1)}, f32[512,1024]{0,1:T(8,128)}, u32[]{:S(2)}) copy-start(f32[512,1024]{0,1:T(8,128)} %get-tuple-element.47) | copy-start | bytes 6291460
  299.2 12.7 %copy-start.12 = (f32[8,32,1024]{2,1,0:T(8,128)S(1)}, f32[8,32,1024]{2,1,0:T(8,128)}, u32[]{:S(2)}) copy-start(f32[8,32,1024]{2,1,0:T(8,128)} %copy-done.11) | copy-start | bytes 3145732
  299.2 20.7 %collective-permute-start.24 = (bf16[12,32,1024]{2,1,0:T(8,128)(2,1)S(1)}, bf16[12,32,1024]{2,1,0:T(8,128)(2,1)S(1)}, u32[]{:S(2)}, u32[]{:S(2)}) collective-permute-start(bf16[12,32,1024]{2,1,0:T(8,128)(2,1)S(1)} %slice.620), channel_id=1, source_target_pairs={{0,1},{3,2},{4,5},{7,6},{8,9},{11,10},{12,13},{15,14},{16,17},{19,... | collective-permute-start | bytes 2359304 | tf_op jit(solution)/shard_map/ppermute | solution.py:95
  311.9 6.0 %copy-start.7 = (f32[16,32,1024]{2,1,0:T(8,128)S(1)}, f32[16,32,1024]{2,1,0:T(8,128)}, u32[]{:S(2)}) copy-start(f32[16,32,1024]{2,1,0:T(8,128)} %shard_map.53) | copy-start | bytes 6291460
  316.5 3.4 copy-start.8
  317.8 2.9 copy-start.4
  319.2 3.2 collective-permute-start.22
  320.1 3.8 %collective-permute-start.25 = (bf16[8,32,1024]{2,1,0:T(8,128)(2,1)S(1)}, bf16[8,32,1024]{2,1,0:T(8,128)(2,1)S(1)}, u32[]{:S(2)}, u32[]{:S(2)}) collective-permute-start(bf16[8,32,1024]{2,1,0:T(8,128)(2,1)S(1)} %fusion.6), channel_id=1, source_target_pairs={{1,2},{2,1},{5,6},{6,5},{9,10},{10,9},{13,14},{14,13},{17,18},{18,... | collective-permute-start | bytes 1572872 | tf_op jit(solution)/shard_map/ppermute | solution.py:244
  320.9 16.2 %collective-permute-start.20 = (f32[4,32,1024]{2,1,0:T(8,128)S(1)}, f32[4,32,1024]{2,1,0:T(8,128)S(1)}, u32[]{:S(2)}, u32[]{:S(2)}) collective-permute-start(f32[4,32,1024]{2,1,0:T(8,128)S(1)} %slice_add_fusion.19), channel_id=1, source_target_pairs={{1,0},{2,3},{5,4},{6,7},{9,8},{10,11},{13,12},{14,15},{17,16},{18,... | collective-permute-start | bytes 1572872 | tf_op jit(solution)/shard_map/ppermute | solution.py:247
  322.6 20.1 %collective-permute-start.23 = (f32[4,32,1024]{2,1,0:T(8,128)S(1)}, f32[4,32,1024]{2,1,0:T(8,128)S(1)}, u32[]{:S(2)}, u32[]{:S(2)}) collective-permute-start(f32[4,32,1024]{2,1,0:T(8,128)S(1)} %slice_add_fusion.15), channel_id=1, source_target_pairs={{1,0},{2,3},{5,4},{6,7},{9,8},{10,11},{13,12},{14,15},{17,16},{18,... | collective-permute-start | bytes 1572872 | tf_op jit(solution)/shard_map/ppermute | solution.py:247
  324.1 24.2 %collective-permute-start.26 = (f32[4,32,1024]{2,1,0:T(8,128)S(1)}, f32[4,32,1024]{2,1,0:T(8,128)S(1)}, u32[]{:S(2)}, u32[]{:S(2)}) collective-permute-start(f32[4,32,1024]{2,1,0:T(8,128)S(1)} %slice_add_fusion.11), channel_id=1, source_target_pairs={{1,0},{2,3},{5,4},{6,7},{9,8},{10,11},{13,12},{14,15},{17,16},{18,... | collective-permute-start | bytes 1572872 | tf_op jit(solution)/shard_map/ppermute | solution.py:247

commit v3 on v2

--- a/solution.py
+++ b/solution.py
@@ -190,7 +190,7 @@
     bins = length // 2
     groups = lax.axis_size("tm")
     place = lax.axis_index("tm")
-    chunks = 8
+    chunks = 4
     width = channels // chunks
     seg_count = windows_here * segments
     sample = jnp.arange(length, dtype=jnp.int32)

time: 353 us -> 354 us (level)
  waiting for transfers between devices: 31.5 us -> 129 us
  starting transfers between devices: 81.5 us -> 35.8 us
  matrix products: 35.2 us -> 14.4 us
  Pallas kernels: 102 us -> 85.8 us
  other arithmetic: 45.6 us -> 38.7 us
  local copies, waits for them, and re-layouts: 39.9 us -> 33.4 us
    ppermute x8 -> x4, waiting for transfers between devices: 14.9 us -> 67.3 us  [on_line(): back = lax.ppermute(low, 'tm', [(1, 0), (2, 3)])]
    ppermute x8 -> x4, waiting for transfers between devices: 2.59 us -> 48.3 us  [edge_first(): return lax.ppermute(values, 'tm', [(0, 1), (groups - 1, groups - 2)])]
    ppermute x8 -> x4, starting transfers between devices: 56.3 us -> 20.1 us  [edge_first(): return lax.ppermute(values, 'tm', [(0, 1), (groups - 1, groups - 2)])]
    dot_general x8 -> x4, matrix products: 35.2 us -> 14.4 us  [on_line(): outs.append(jnp.dot(final, inverse, precision=lax.Precision.HIGH))]
    pallas_call x8 -> x4, Pallas kernels: 86.4 us -> 70.6 us  [cross_chunk(): pl.pallas_call(cross_kernel, grid=(width // step_rows,), in_specs=[pl.Blo...]
    slice x8 -> x4, local copies, waits for them, and re-layouts: 18.1 us -> 12 us  [on_line(): edge_out = part[:source_count - per_group].astype(jnp.bfloat16)]
    ppermute x8 -> x4, starting transfers between devices: 10.5 us -> 5.41 us  [on_line(): back = lax.ppermute(low, 'tm', [(1, 0), (2, 3)])]
    another operation x0 -> x2, other arithmetic: none -> 4.47 us
  transfers between devices with their start and end apart: 27 -> 15, of which waited for: 8 -> 11; matrix products, arithmetic and copies ran while one was open for 23% -> 13% of each run, Pallas kernels for 22% -> 15%
where the time goes in v3:
time: 354 us; the launch traced here: 353 us
  waiting for transfers between devices  129 us (36%)
  Pallas kernels  85.8 us (24%)
  other arithmetic  38.7 us (11%)
  starting transfers between devices  35.8 us (10%)
  local copies, waits for them, and re-layouts  33.4 us (9%)
  between operations  15.6 us (4%)
  matrix products  14.4 us (4%)
    pallas_call x4, Pallas kernels, cross_chunk(): pl.pallas_call(cross_kernel, grid=(width // step_rows,), in_specs=[pl.Blo...  70.6 us
    ppermute x4, waiting for transfers between devices, on_line(): back = lax.ppermute(low, 'tm', [(1, 0), (2, 3)])  67.3 us
    ppermute x4, waiting for transfers between devices, edge_first(): return lax.ppermute(values, 'tm', [(0, 1), (groups - 1, groups - 2)])  48.3 us
    ppermute x4, starting transfers between devices, edge_first(): return lax.ppermute(values, 'tm', [(0, 1), (groups - 1, groups - 2)])  20.1 us
    pallas_call x1, Pallas kernels, whiten_segments(): pl.pallas_call(whiten_kernel, grid=(segments,), in_specs=[pl.BlockSpec((N...  15.2 us
    dot_general x4, matrix products, on_line(): outs.append(jnp.dot(final, inverse, precision=lax.Precision.HIGH))  14.4 us
    ppermute x3, waiting for transfers between devices, butterfly_sum(): lax.ppermute(values, axis, [(b, b ^ step) for b in range(count)])  13.7 us
    slice x4, local copies, waits for them, and re-layouts, on_line(): edge_out = part[:source_count - per_group].astype(jnp.bfloat16)  12 us
  transfers between devices with their start and end apart: 15, of which 11 were waited for; matrix products, arithmetic and copies ran while one was open for 13% of the time, Pallas kernels for 15%

profile of v3, /device:TPU:0, one launch (start us, length us, event | category | flops | bytes accessed | tf_op | source)
XLA Modules:
  0.0 353.0 jit_solution(17325535473853414168)
XLA Ops:
  14.1 9.1 %fusion.30 = (f32[1024,512]{1,0:T(8,128)}, f32[1024,512]{1,0:T(8,128)}) fusion(), kind=kLoop, calls=%fused_computation.59 | loop fusion | flops 7340032 | bytes 4194304 | tf_op jit(solution)/shard_map/sin | solution.py:199
  23.3 7.5 %copy.11 = bf16[256,2,6,1024]{3,0,2,1:T(8,128)(2,1)} copy(bf16[256,2,6,1024]{3,1,2,0:T(2,128)(2,1)} %param.4) | data formatting | bytes 12582912 | tf_op args[0]
  30.9 1.7 copy.13.mask_ref
  35.8 2.8 fusion.50
  38.6 1.7 negate_convert_fusion
  40.3 1.6 pad_maximum_fusion.1.forward_ref
  41.9 15.2 %shard_map.46 = bf16[4,12,64,1024]{3,2,1,0:T(8,128)(2,1)} custom-call(bf16[12,256,1024]{2,1,0:T(8,128)(2,1)} %bitcast.45, bf16[1024,1024]{1,0:T(8,128)(2,1)} %pad_maximum_fusion.1.forward_ref, f32[12,256,1]{2,1,0:T(8,128)} %copy.13.mask_ref), custom_call_target="tpu_custom_call" | custom-call | tf_op jit(solution)/shard_map/pallas_call | solution.py:108
  57.1 1.7 select_bitcast_fusion.3
  61.2 2.9 collective-permute-start.1
  64.1 9.4 %collective-permute-done.1 = bf16[12,16,1024]{2,1,0:T(8,128)(2,1)S(1)} collective-permute-done((bf16[12,16,1024]{2,1,0:T(8,128)(2,1)S(1)}, bf16[12,16,1024]{2,1,0:T(8,128)(2,1)S(1)}, u32[]{:S(2)}, u32[]{:S(2)}) %collective-permute-start.1) | collective-permute-done | bytes 393248 | tf_op jit(solution)/shard_map/ppermute | solution.py:178
  73.7 1.8 collective-permute-start.2
  75.5 6.0 %slice_bitcast_fusion.1 = (bf16[12,64,1024]{2,1,0:T(8,128)(2,1)}, bf16[12,64,1024]{2,1,0:T(8,128)(2,1)}, bf16[12,64,1024]{2,1,0:T(8,128)(2,1)}, bf16[12,64,1024]{2,1,0:T(8,128)(2,1)}) fusion(bf16[4,12,64,1024]{3,2,1,0:T(8,128)(2,1)} %shard_map.46), kind=kLoop, calls=%fused_computation.32 | loop fusion | bytes 12582912 | tf_op jit(solution)/shard_map/squeeze | solution.py:232
  81.5 2.9 collective-permute-done.2
  85.0 3.5 broadcast_in_dim.29.src_ref
  88.4 17.6 %shard_map.47 = f32[16,64,1024]{2,1,0:T(8,128)} custom-call(bf16[12,64,1024]{2,1,0:T(8,128)(2,1)} %get-tuple-element.22.own_ref, f32[12,16,8,1024]{3,2,1,0:T(8,128)} %broadcast_in_dim.29.src_ref), custom_call_target="tpu_custom_call" | custom-call | tf_op jit(solution)/shard_map/pallas_call | solution.py:162
  106.1 3.3 slice.343
  109.4 4.6 %collective-permute-start.3 = (bf16[12,64,1024]{2,1,0:T(8,128)(2,1)}, bf16[12,64,1024]{2,1,0:T(8,128)(2,1)}, u32[]{:S(2)}, u32[]{:S(2)}) collective-permute-start(bf16[12,64,1024]{2,1,0:T(8,128)(2,1)} %slice.343), channel_id=1, source_target_pairs={{0,1},{3,2},{4,5},{7,6},{8,9},{11,10},{12,13},{15,14},{16,17},{19,... | collective-permute-start | bytes 4718600 | tf_op jit(solution)/shard_map/ppermute | solution.py:95
  114.0 17.6 %shard_map.48 = f32[16,64,1024]{2,1,0:T(8,128)} custom-call(bf16[12,64,1024]{2,1,0:T(8,128)(2,1)} %get-tuple-element.21.own_ref, f32[12,16,8,1024]{3,2,1,0:T(8,128)} %broadcast_in_dim.29.src_ref), custom_call_target="tpu_custom_call" | custom-call | tf_op jit(solution)/shard_map/pallas_call | solution.py:162
  131.6 3.3 slice.342
  134.9 10.4 %collective-permute-done.3 = bf16[12,64,1024]{2,1,0:T(8,128)(2,1)} collective-permute-done((bf16[12,64,1024]{2,1,0:T(8,128)(2,1)}, bf16[12,64,1024]{2,1,0:T(8,128)(2,1)}, u32[]{:S(2)}, u32[]{:S(2)}) %collective-permute-start.3) | collective-permute-done | bytes 1572896 | tf_op jit(solution)/shard_map/ppermute | solution.py:95
  145.3 5.5 %collective-permute-start.6 = (bf16[12,64,1024]{2,1,0:T(8,128)(2,1)}, bf16[12,64,1024]{2,1,0:T(8,128)(2,1)}, u32[]{:S(2)}, u32[]{:S(2)}) collective-permute-start(bf16[12,64,1024]{2,1,0:T(8,128)(2,1)} %slice.342), channel_id=1, source_target_pairs={{0,1},{3,2},{4,5},{7,6},{8,9},{11,10},{12,13},{15,14},{16,17},{19,... | collective-permute-start | bytes 4718600 | tf_op jit(solution)/shard_map/ppermute | solution.py:95
  150.9 17.6 %shard_map.49 = f32[16,64,1024]{2,1,0:T(8,128)} custom-call(bf16[12,64,1024]{2,1,0:T(8,128)(2,1)} %get-tuple-element.15.own_ref, f32[12,16,8,1024]{3,2,1,0:T(8,128)} %broadcast_in_dim.29.src_ref), custom_call_target="tpu_custom_call" | custom-call | tf_op jit(solution)/shard_map/pallas_call | solution.py:162
  168.5 3.3 slice.341
  171.8 9.5 %collective-permute-done.6 = bf16[12,64,1024]{2,1,0:T(8,128)(2,1)} collective-permute-done((bf16[12,64,1024]{2,1,0:T(8,128)(2,1)}, bf16[12,64,1024]{2,1,0:T(8,128)(2,1)}, u32[]{:S(2)}, u32[]{:S(2)}) %collective-permute-start.6) | collective-permute-done | bytes 1572896 | tf_op jit(solution)/shard_map/ppermute | solution.py:95
  181.3 5.5 %collective-permute-start.9 = (bf16[12,64,1024]{2,1,0:T(8,128)(2,1)}, bf16[12,64,1024]{2,1,0:T(8,128)(2,1)}, u32[]{:S(2)}, u32[]{:S(2)}) collective-permute-start(bf16[12,64,1024]{2,1,0:T(8,128)(2,1)} %slice.341), channel_id=1, source_target_pairs={{0,1},{3,2},{4,5},{7,6},{8,9},{11,10},{12,13},{15,14},{16,17},{19,... | collective-permute-start | bytes 4718600 | tf_op jit(solution)/shard_map/ppermute | solution.py:95
  186.8 17.6 %shard_map.50 = f32[16,64,1024]{2,1,0:T(8,128)} custom-call(bf16[12,64,1024]{2,1,0:T(8,128)(2,1)} %get-tuple-element.17.own_ref, f32[12,16,8,1024]{3,2,1,0:T(8,128)} %broadcast_in_dim.29.src_ref), custom_call_target="tpu_custom_call" | custom-call | tf_op jit(solution)/shard_map/pallas_call | solution.py:162
  204.4 2.1 slice.340
  206.6 9.7 %collective-permute-done.9 = bf16[12,64,1024]{2,1,0:T(8,128)(2,1)} collective-permute-done((bf16[12,64,1024]{2,1,0:T(8,128)(2,1)}, bf16[12,64,1024]{2,1,0:T(8,128)(2,1)}, u32[]{:S(2)}, u32[]{:S(2)}) %collective-permute-start.9) | collective-permute-done | bytes 1572896 | tf_op jit(solution)/shard_map/ppermute | solution.py:95
  216.3 4.5 %collective-permute-start.12 = (bf16[12,64,1024]{2,1,0:T(8,128)(2,1)S(1)}, bf16[12,64,1024]{2,1,0:T(8,128)(2,1)S(1)}, u32[]{:S(2)}, u32[]{:S(2)}) collective-permute-start(bf16[12,64,1024]{2,1,0:T(8,128)(2,1)S(1)} %slice.340), channel_id=1, source_target_pairs={{0,1},{3,2},{4,5},{7,6},{8,9},{11,10},{12,13},{15,14},{16,17},{19,... | collective-permute-start | bytes 4718600 | tf_op jit(solution)/shard_map/ppermute | solution.py:95
  220.8 2.2 fusion.6
  223.9 2.0 fusion.5
  226.8 3.0 fusion.4
  229.7 1.7 collective-permute-start.10
  231.4 18.7 %collective-permute-done.12 = bf16[12,64,1024]{2,1,0:T(8,128)(2,1)S(1)} collective-permute-done((bf16[12,64,1024]{2,1,0:T(8,128)(2,1)S(1)}, bf16[12,64,1024]{2,1,0:T(8,128)(2,1)S(1)}, u32[]{:S(2)}, u32[]{:S(2)}) %collective-permute-start.12) | collective-permute-done | bytes 1572896 | tf_op jit(solution)/shard_map/ppermute | solution.py:95
  250.1 1.5 fusion.3
  251.6 1.6 collective-permute-start.13
  253.5 3.1 slice_add_fusion.19
  262.6 1.5 slice_add_fusion.11
  265.6 1.6 convert_element_type.98
  268.8 17.7 %collective-permute-done.5 = f32[4,64,1024]{2,1,0:T(8,128)S(1)} collective-permute-done((f32[4,64,1024]{2,1,0:T(8,128)}, f32[4,64,1024]{2,1,0:T(8,128)S(1)}, u32[]{:S(2)}, u32[]{:S(2)}) %collective-permute-start.5) | collective-permute-done | bytes 1048608 | tf_op jit(solution)/shard_map/ppermute | solution.py:247
  286.5 3.8 %fusion.13 = f32[4,64,1024]{2,1,0:T(8,128)S(1)} fusion(f32[512,1024]{0,1:T(8,128)S(1)} %copy-done, f32[512,1024]{0,1:T(8,128)S(1)} %get-tuple-element.28, f32[8,64,1024]{2,1,0:T(8,128)S(1)} %copy-done.7, f32[16,64,1024]{2,1,0:T(8,128)} %shard_map.47, f32[4,64,1024]{2,1,0:T(8,128)S(1)} %collective-permute-done.5, ...), kind=kOutput, calls=%fused_computation.30 | convolution fusion | flops 1612972032 | bytes 9961473 | tf_op jit(solution)/shard_map/dot_general | solution.py:249
  290.3 18.8 %collective-permute-done.8 = f32[4,64,1024]{2,1,0:T(8,128)} collective-permute-done((f32[4,64,1024]{2,1,0:T(8,128)}, f32[4,64,1024]{2,1,0:T(8,128)}, u32[]{:S(2)}, u32[]{:S(2)}) %collective-permute-start.8) | collective-permute-done | bytes 1048608 | tf_op jit(solution)/shard_map/ppermute | solution.py:247
  309.1 3.9 %fusion.12 = f32[4,64,1024]{2,1,0:T(8,128)S(1)} fusion(f32[512,1024]{0,1:T(8,128)S(1)} %copy-done, f32[512,1024]{0,1:T(8,128)S(1)} %get-tuple-element.28, f32[8,64,1024]{2,1,0:T(8,128)S(1)} %copy-done.9, f32[16,64,1024]{2,1,0:T(8,128)} %shard_map.48, f32[4,64,1024]{2,1,0:T(8,128)} %collective-permute-done.8, ...), kind=kOutput, calls=%fused_computation.29 | convolution fusion | flops 1612972032 | bytes 9961473 | tf_op jit(solution)/shard_map/dot_general | solution.py:249
  313.0 18.4 %collective-permute-done.11 = f32[4,64,1024]{2,1,0:T(8,128)S(1)} collective-permute-done((f32[4,64,1024]{2,1,0:T(8,128)S(1)}, f32[4,64,1024]{2,1,0:T(8,128)S(1)}, u32[]{:S(2)}, u32[]{:S(2)}) %collective-permute-start.11) | collective-permute-done | bytes 1048608 | tf_op jit(solution)/shard_map/ppermute | solution.py:247
  331.4 3.6 %fusion.11 = f32[4,64,1024]{2,1,0:T(8,128)S(1)} fusion(f32[512,1024]{0,1:T(8,128)S(1)} %copy-done, f32[512,1024]{0,1:T(8,128)S(1)} %get-tuple-element.28, f32[8,64,1024]{2,1,0:T(8,128)S(1)} %convert_element_type.94, f32[16,64,1024]{2,1,0:T(8,128)} %shard_map.49, f32[4,64,1024]{2,1,0:T(8,128)S(1)} %collective-permute-done.11, ...), kind=kOutput, calls=%fused_computation.28 | convolution fusion | flops 1612972032 | bytes 9961473 | tf_op jit(solution)/shard_map/dot_general | solution.py:249
  335.1 12.5 %collective-permute-done.14 = f32[4,64,1024]{2,1,0:T(8,128)S(1)} collective-permute-done((f32[4,64,1024]{2,1,0:T(8,128)S(1)}, f32[4,64,1024]{2,1,0:T(8,128)S(1)}, u32[]{:S(2)}, u32[]{:S(2)}) %collective-permute-start.14) | collective-permute-done | bytes 1048608 | tf_op jit(solution)/shard_map/ppermute | solution.py:247
  347.6 3.0 fusion.10
  350.6 2.4 pad_maximum_fusion
  (58 shorter events, 16.2 us)
Async XLA Ops:
  23.3 7.6 %copy-start.11 = (s32[256,2,6]{0,1,2:T(2,128)S(1)}, s32[256,2,6]{0,1,2:T(2,128)}, u32[]{:S(2)}) copy-start(s32[256,2,6]{0,1,2:T(2,128)} %param.5) | copy-start | bytes 36868
  23.3 9.3 %copy-start.12 = (s32[4]{0:T(128)S(1)}, s32[4]{0:T(128)}, u32[]{:S(2)}) copy-start(s32[4]{0:T(128)} %param.6) | copy-start | bytes 52
  35.7 2.9 copy-start.5
  59.0 1.9 collective-permute-start
  61.2 12.3 %collective-permute-start.1 = (bf16[12,16,1024]{2,1,0:T(8,128)(2,1)S(1)}, bf16[12,16,1024]{2,1,0:T(8,128)(2,1)S(1)}, u32[]{:S(2)}, u32[]{:S(2)}) collective-permute-start(bf16[12,16,1024]{2,1,0:T(8,128)(2,1)S(1)} %fusion.49), channel_id=1, source_target_pairs={{0,8},{4,12},{8,0},{12,4},{16,24},{20,28},{24,16},{28,20},{1,9},{5... | collective-permute-start | bytes 1179656 | tf_op jit(solution)/shard_map/ppermute | solution.py:178
  73.7 10.7 %collective-permute-start.2 = (bf16[12,16,1024]{2,1,0:T(8,128)(2,1)S(1)}, bf16[12,16,1024]{2,1,0:T(8,128)(2,1)S(1)}, u32[]{:S(2)}, u32[]{:S(2)}) collective-permute-start(bf16[12,16,1024]{2,1,0:T(8,128)(2,1)S(1)} %add.132), channel_id=1, source_target_pairs={{0,16},{4,20},{8,24},{12,28},{16,0},{20,4},{24,8},{28,12},{1,17},{... | collective-permute-start | bytes 1179656 | tf_op jit(solution)/shard_map/ppermute | solution.py:178
  109.4 35.9 %collective-permute-start.3 = (bf16[12,64,1024]{2,1,0:T(8,128)(2,1)}, bf16[12,64,1024]{2,1,0:T(8,128)(2,1)}, u32[]{:S(2)}, u32[]{:S(2)}) collective-permute-start(bf16[12,64,1024]{2,1,0:T(8,128)(2,1)} %slice.343), channel_id=1, source_target_pairs={{0,1},{3,2},{4,5},{7,6},{8,9},{11,10},{12,13},{15,14},{16,17},{19,... | collective-permute-start | bytes 4718600 | tf_op jit(solution)/shard_map/ppermute | solution.py:95
  145.3 36.0 %collective-permute-start.6 = (bf16[12,64,1024]{2,1,0:T(8,128)(2,1)}, bf16[12,64,1024]{2,1,0:T(8,128)(2,1)}, u32[]{:S(2)}, u32[]{:S(2)}) collective-permute-start(bf16[12,64,1024]{2,1,0:T(8,128)(2,1)} %slice.342), channel_id=1, source_target_pairs={{0,1},{3,2},{4,5},{7,6},{8,9},{11,10},{12,13},{15,14},{16,17},{19,... | collective-permute-start | bytes 4718600 | tf_op jit(solution)/shard_map/ppermute | solution.py:95
  181.3 35.0 %collective-permute-start.9 = (bf16[12,64,1024]{2,1,0:T(8,128)(2,1)}, bf16[12,64,1024]{2,1,0:T(8,128)(2,1)}, u32[]{:S(2)}, u32[]{:S(2)}) collective-permute-start(bf16[12,64,1024]{2,1,0:T(8,128)(2,1)} %slice.341), channel_id=1, source_target_pairs={{0,1},{3,2},{4,5},{7,6},{8,9},{11,10},{12,13},{15,14},{16,17},{19,... | collective-permute-start | bytes 4718600 | tf_op jit(solution)/shard_map/ppermute | solution.py:95
  206.6 17.3 %copy-start.1 = (f32[16,64,1024]{2,1,0:T(8,128)S(1)}, f32[16,64,1024]{2,1,0:T(8,128)}, u32[]{:S(2)}) copy-start(f32[16,64,1024]{2,1,0:T(8,128)} %shard_map.48) | copy-start | bytes 12582916
  216.3 33.8 %collective-permute-start.12 = (bf16[12,64,1024]{2,1,0:T(8,128)(2,1)S(1)}, bf16[12,64,1024]{2,1,0:T(8,128)(2,1)S(1)}, u32[]{:S(2)}, u32[]{:S(2)}) collective-permute-start(bf16[12,64,1024]{2,1,0:T(8,128)(2,1)S(1)} %slice.340), channel_id=1, source_target_pairs={{0,1},{3,2},{4,5},{7,6},{8,9},{11,10},{12,13},{15,14},{16,17},{19,... | collective-permute-start | bytes 4718600 | tf_op jit(solution)/shard_map/ppermute | solution.py:95
  223.0 3.8 %copy-start.2 = (f32[16,64,1024]{2,1,0:T(8,128)S(1)}, f32[16,64,1024]{2,1,0:T(8,128)}, u32[]{:S(2)}) copy-start(f32[16,64,1024]{2,1,0:T(8,128)} %shard_map.49) | copy-start | bytes 12582916
  223.0 30.2 %collective-permute-start.4 = (bf16[8,64,1024]{2,1,0:T(8,128)(2,1)S(1)}, bf16[8,64,1024]{2,1,0:T(8,128)(2,1)S(1)}, u32[]{:S(2)}, u32[]{:S(2)}) collective-permute-start(bf16[8,64,1024]{2,1,0:T(8,128)(2,1)S(1)} %fusion.6), channel_id=1, source_target_pairs={{1,2},{2,1},{5,6},{6,5},{9,10},{10,9},{13,14},{14,13},{17,18},{18,... | collective-permute-start | bytes 3145736 | tf_op jit(solution)/shard_map/ppermute | solution.py:244
  225.9 24.2 %copy-start.3 = (f32[16,64,1024]{2,1,0:T(8,128)S(1)}, f32[16,64,1024]{2,1,0:T(8,128)}, u32[]{:S(2)}) copy-start(f32[16,64,1024]{2,1,0:T(8,128)} %shard_map.50) | copy-start | bytes 12582916
  225.9 32.0 %collective-permute-start.7 = (bf16[8,64,1024]{2,1,0:T(8,128)(2,1)S(1)}, bf16[8,64,1024]{2,1,0:T(8,128)(2,1)S(1)}, u32[]{:S(2)}, u32[]{:S(2)}) collective-permute-start(bf16[8,64,1024]{2,1,0:T(8,128)(2,1)S(1)} %fusion.5), channel_id=1, source_target_pairs={{1,2},{2,1},{5,6},{6,5},{9,10},{10,9},{13,14},{14,13},{17,18},{18,... | collective-permute-start | bytes 3145736 | tf_op jit(solution)/shard_map/ppermute | solution.py:244
  229.7 31.4 %collective-permute-start.10 = (bf16[8,64,1024]{2,1,0:T(8,128)(2,1)}, bf16[8,64,1024]{2,1,0:T(8,128)(2,1)}, u32[]{:S(2)}, u32[]{:S(2)}) collective-permute-start(bf16[8,64,1024]{2,1,0:T(8,128)(2,1)} %fusion.4), channel_id=1, source_target_pairs={{1,2},{2,1},{5,6},{6,5},{9,10},{10,9},{13,14},{14,13},{17,18},{18,... | collective-permute-start | bytes 3145736 | tf_op jit(solution)/shard_map/ppermute | solution.py:244
  250.1 1.5 copy-start.10
  251.6 14.0 %collective-permute-start.13 = (bf16[8,64,1024]{2,1,0:T(8,128)(2,1)}, bf16[8,64,1024]{2,1,0:T(8,128)(2,1)}, u32[]{:S(2)}, u32[]{:S(2)}) collective-permute-start(bf16[8,64,1024]{2,1,0:T(8,128)(2,1)} %fusion.3), channel_id=1, source_target_pairs={{1,2},{2,1},{5,6},{6,5},{9,10},{10,9},{13,14},{14,13},{17,18},{18,... | collective-permute-start | bytes 3145736 | tf_op jit(solution)/shard_map/ppermute | solution.py:244
  253.5 4.7 %copy-start.6 = (f32[8,64,1024]{2,1,0:T(8,128)}, f32[8,64,1024]{2,1,0:T(8,128)S(1)}, u32[]{:S(2)}) copy-start(f32[8,64,1024]{2,1,0:T(8,128)S(1)} %convert_element_type.86) | copy-start | bytes 6291460
  256.6 29.9 %collective-permute-start.5 = (f32[4,64,1024]{2,1,0:T(8,128)}, f32[4,64,1024]{2,1,0:T(8,128)S(1)}, u32[]{:S(2)}, u32[]{:S(2)}) collective-permute-start(f32[4,64,1024]{2,1,0:T(8,128)} %slice_add_fusion.19), channel_id=1, source_target_pairs={{1,0},{2,3},{5,4},{6,7},{9,8},{10,11},{13,12},{14,15},{17,16},{18,... | collective-permute-start | bytes 3145736 | tf_op jit(solution)/shard_map/ppermute | solution.py:247
  258.1 1.7 copy-start.8
  259.8 49.2 %collective-permute-start.8 = (f32[4,64,1024]{2,1,0:T(8,128)}, f32[4,64,1024]{2,1,0:T(8,128)}, u32[]{:S(2)}, u32[]{:S(2)}) collective-permute-start(f32[4,64,1024]{2,1,0:T(8,128)} %slice_add_fusion.15), channel_id=1, source_target_pairs={{1,0},{2,3},{5,4},{6,7},{9,8},{10,11},{13,12},{14,15},{17,16},{18,... | collective-permute-start | bytes 3145736 | tf_op jit(solution)/shard_map/ppermute | solution.py:247
  262.6 4.6 %copy-start.4 = (f32[16,64,1024]{2,1,0:T(8,128)S(1)}, f32[16,64,1024]{2,1,0:T(8,128)}, u32[]{:S(2)}) copy-start(f32[16,64,1024]{2,1,0:T(8,128)} %shard_map.50) | copy-start | bytes 12582916
  264.1 67.3 %collective-permute-start.11 = (f32[4,64,1024]{2,1,0:T(8,128)S(1)}, f32[4,64,1024]{2,1,0:T(8,128)S(1)}, u32[]{:S(2)}, u32[]{:S(2)}) collective-permute-start(f32[4,64,1024]{2,1,0:T(8,128)S(1)} %slice_add_fusion.11), channel_id=1, source_target_pairs={{1,0},{2,3},{5,4},{6,7},{9,8},{10,11},{13,12},{14,15},{17,16},{18,... | collective-permute-start | bytes 3145736 | tf_op jit(solution)/shard_map/ppermute | solution.py:247
  265.6 20.9 %copy-start.7 = (f32[8,64,1024]{2,1,0:T(8,128)S(1)}, f32[8,64,1024]{2,1,0:T(8,128)}, u32[]{:S(2)}) copy-start(f32[8,64,1024]{2,1,0:T(8,128)} %copy-done.6) | copy-start | bytes 6291460
  267.2 19.3 %copy-start = (f32[512,1024]{0,1:T(8,128)S(1)}, f32[512,1024]{0,1:T(8,128)}, u32[]{:S(2)}) copy-start(f32[512,1024]{0,1:T(8,128)} %get-tuple-element.30) | copy-start | bytes 6291460
  267.4 80.2 %collective-permute-start.14 = (f32[4,64,1024]{2,1,0:T(8,128)S(1)}, f32[4,64,1024]{2,1,0:T(8,128)S(1)}, u32[]{:S(2)}, u32[]{:S(2)}) collective-permute-start(f32[4,64,1024]{2,1,0:T(8,128)S(1)} %slice_add_fusion.7), channel_id=1, source_target_pairs={{1,0},{2,3},{5,4},{6,7},{9,8},{10,11},{13,12},{14,15},{17,16},{18,... | collective-permute-start | bytes 3145736 | tf_op jit(solution)/shard_map/ppermute | solution.py:247
  286.5 22.6 %copy-start.9 = (f32[8,64,1024]{2,1,0:T(8,128)S(1)}, f32[8,64,1024]{2,1,0:T(8,128)}, u32[]{:S(2)}) copy-start(f32[8,64,1024]{2,1,0:T(8,128)} %copy-done.8) | copy-start | bytes 6291460

commit v4 on v2

--- a/solution.py
+++ b/solution.py
@@ -228,9 +228,12 @@
     order_wide = widen(order, length)
     outs = []
     arrived = []
+    returned = []
     for chunk in range(chunks):
         own = whitened[chunk]
-        if chunk >= 2:
+        if chunk >= 3:
+            own, _, _ = lax.optimization_barrier((own, arrived[chunk - 2], returned[chunk - 3]))
+        elif chunk >= 2:
             own, _ = lax.optimization_barrier((own, arrived[chunk - 2]))
         part = cross_chunk(own, order_wide)
         far_part = part[:half]
@@ -245,6 +248,7 @@
         low = near_part[:per_group] + got[:per_group]
         high = near_part[per_group:] + edge_in[half:].astype(jnp.float32) + got[per_group:]
         back = lax.ppermute(low, "tm", [(1, 0), (2, 3)])
+        returned.append(back)
         final = jnp.where(is_edge, near_part[:per_group] + back, high)
         outs.append(jnp.dot(final, inverse, precision=lax.Precision.HIGH))
     return jnp.concatenate(outs, axis=1)

time: 353 us -> 350 us (level)
  starting transfers between devices: 81.5 us -> 60 us
  waiting for transfers between devices: 31.5 us -> 51.7 us
  other arithmetic: 45.6 us -> 41.1 us
    ppermute x8, starting transfers between devices: 56.3 us -> 33.8 us  [edge_first(): return lax.ppermute(values, 'tm', [(0, 1), (groups - 1, groups - 2)])]
    ppermute x8, waiting for transfers between devices: 14.9 us -> 25.6 us  [on_line(): back = lax.ppermute(low, 'tm', [(1, 0), (2, 3)])]
    ppermute x8, waiting for transfers between devices: 2.59 us -> 12.1 us  [edge_first(): return lax.ppermute(values, 'tm', [(0, 1), (groups - 1, groups - 2)])]
    unnamed x37 -> x65, local copies, waits for them, and re-layouts: 9.65 us -> 14.3 us
  transfers between devices with their start and end apart: 27 -> 27, of which waited for: 8 -> 11; matrix products, arithmetic and copies ran while one was open for 23% -> 22% of each run, Pallas kernels for 22% -> 22%
where the time goes in v4:
time: 350 us; the launch traced here: 348 us
  Pallas kernels  102 us (29%)
  starting transfers between devices  60 us (17%)
  waiting for transfers between devices  51.7 us (15%)
  local copies, waits for them, and re-layouts  43.4 us (12%)
  other arithmetic  41.1 us (12%)
  matrix products  34.2 us (10%)
  between operations  16.2 us (5%)
    pallas_call x8, Pallas kernels, cross_chunk(): pl.pallas_call(cross_kernel, grid=(width // step_rows,), in_specs=[pl.Blo...  86.4 us
    dot_general x8, matrix products, on_line(): outs.append(jnp.dot(final, inverse, precision=lax.Precision.HIGH))  34.2 us
    ppermute x8, starting transfers between devices, edge_first(): return lax.ppermute(values, 'tm', [(0, 1), (groups - 1, groups - 2)])  33.8 us
    ppermute x8, waiting for transfers between devices, on_line(): back = lax.ppermute(low, 'tm', [(1, 0), (2, 3)])  25.6 us
    slice x8, local copies, waits for them, and re-layouts, on_line(): edge_out = part[:source_count - per_group].astype(jnp.bfloat16)  16.2 us
    pallas_call x1, Pallas kernels, whiten_segments(): pl.pallas_call(whiten_kernel, grid=(segments,), in_specs=[pl.BlockSpec((N...  15.3 us
    unnamed x65, local copies, waits for them, and re-layouts  14.3 us
    ppermute x3, waiting for transfers between devices, butterfly_sum(): lax.ppermute(values, axis, [(b, b ^ step) for b in range(count)])  14 us
  transfers between devices with their start and end apart: 27, of which 11 were waited for; matrix products, arithmetic and copies ran while one was open for 22% of the time, Pallas kernels for 22%

profile of v4, /device:TPU:0, one launch (start us, length us, event | category | flops | bytes accessed | tf_op | source)
XLA Modules:
  0.0 348.3 jit_solution(6308940617946314178)
XLA Ops:
  14.5 9.1 %fusion.14 = (f32[1024,512]{1,0:T(8,128)}, f32[1024,512]{1,0:T(8,128)}) fusion(), kind=kLoop, calls=%fused_computation.46 | loop fusion | flops 7340032 | bytes 4194304 | tf_op jit(solution)/shard_map/sin | solution.py:199
  28.5 7.7 %copy.15 = bf16[256,2,6,1024]{3,0,2,1:T(8,128)(2,1)} copy(bf16[256,2,6,1024]{3,1,2,0:T(2,128)(2,1)} %param.4) | data formatting | bytes 12582912 | tf_op args[0]
  41.2 15.3 %shard_map.46 = bf16[8,12,32,1024]{3,2,1,0:T(8,128)(2,1)} custom-call(bf16[12,256,1024]{2,1,0:T(8,128)(2,1)} %bitcast.61, bf16[1024,1024]{1,0:T(8,128)(2,1)} %pad_maximum_fusion.forward_ref, f32[12,256,1]{2,1,0:T(8,128)} %copy.17.mask_ref), custom_call_target="tpu_custom_call" | custom-call | tf_op jit(solution)/shard_map/pallas_call | solution.py:108
  60.5 2.9 collective-permute-start.1
  63.4 9.4 %collective-permute-done.1 = bf16[12,16,1024]{2,1,0:T(8,128)(2,1)S(1)} collective-permute-done((bf16[12,16,1024]{2,1,0:T(8,128)(2,1)S(1)}, bf16[12,16,1024]{2,1,0:T(8,128)(2,1)S(1)}, u32[]{:S(2)}, u32[]{:S(2)}) %collective-permute-start.1) | collective-permute-done | bytes 393248 | tf_op jit(solution)/shard_map/ppermute | solution.py:178
  72.9 1.8 collective-permute-start.2
  74.8 5.6 %slice_bitcast_fusion = (bf16[12,32,1024]{2,1,0:T(8,128)(2,1)}, bf16[12,32,1024]{2,1,0:T(8,128)(2,1)}, bf16[12,32,1024]{2,1,0:T(8,128)(2,1)}, bf16[12,32,1024]{2...) fusion(bf16[8,12,32,1024]{3,2,1,0:T(8,128)(2,1)} %shard_map.46), kind=kLoop, calls=%fused_computation.48 | loop fusion | bytes 12582912 | tf_op jit(solution)/shard_map/squeeze | solution.py:233
  80.4 3.3 collective-permute-done.2
  84.2 3.4 broadcast_in_dim.29.src_ref
  87.6 10.8 %shard_map.47 = f32[16,32,1024]{2,1,0:T(8,128)} custom-call(bf16[12,32,1024]{2,1,0:T(8,128)(2,1)} %get-tuple-element.42.own_ref, f32[12,16,8,1024]{3,2,1,0:T(8,128)} %broadcast_in_dim.29.src_ref), custom_call_target="tpu_custom_call" | custom-call | tf_op jit(solution)/shard_map/pallas_call | solution.py:162
  98.4 2.4 slice.627
  100.8 4.3 %collective-permute-start.3 = (bf16[12,32,1024]{2,1,0:T(8,128)(2,1)}, bf16[12,32,1024]{2,1,0:T(8,128)(2,1)}, u32[]{:S(2)}, u32[]{:S(2)}) collective-permute-start(bf16[12,32,1024]{2,1,0:T(8,128)(2,1)} %slice.627), channel_id=1, source_target_pairs={{0,1},{3,2},{4,5},{7,6},{8,9},{11,10},{12,13},{15,14},{16,17},{19,... | collective-permute-start | bytes 2359304 | tf_op jit(solution)/shard_map/ppermute | solution.py:95
  105.2 10.8 %shard_map.48 = f32[16,32,1024]{2,1,0:T(8,128)} custom-call(bf16[12,32,1024]{2,1,0:T(8,128)(2,1)} %get-tuple-element.41.own_ref, f32[12,16,8,1024]{3,2,1,0:T(8,128)} %broadcast_in_dim.29.src_ref), custom_call_target="tpu_custom_call" | custom-call | tf_op jit(solution)/shard_map/pallas_call | solution.py:162
  117.5 2.4 collective-permute-done.3
  119.9 5.3 %collective-permute-start.6 = (bf16[12,32,1024]{2,1,0:T(8,128)(2,1)S(1)}, bf16[12,32,1024]{2,1,0:T(8,128)(2,1)}, u32[]{:S(2)}, u32[]{:S(2)}) collective-permute-start(bf16[12,32,1024]{2,1,0:T(8,128)(2,1)S(1)} %slice.626), channel_id=1, source_target_pairs={{0,1},{3,2},{4,5},{7,6},{8,9},{11,10},{12,13},{15,14},{16,17},{19,... | collective-permute-start | bytes 2359304 | tf_op jit(solution)/shard_map/ppermute | solution.py:95
  128.1 10.8 %shard_map.49 = f32[16,32,1024]{2,1,0:T(8,128)} custom-call(bf16[12,32,1024]{2,1,0:T(8,128)(2,1)} %get-tuple-element.23.own_ref, f32[12,16,8,1024]{3,2,1,0:T(8,128)} %broadcast_in_dim.29.src_ref), custom_call_target="tpu_custom_call" | custom-call | tf_op jit(solution)/shard_map/pallas_call | solution.py:162
  140.6 2.6 collective-permute-start.9
  147.0 2.0 fusion.12
  150.4 6.8 %collective-permute-done.9 = bf16[12,32,1024]{2,1,0:T(8,128)(2,1)S(1)} collective-permute-done((bf16[12,32,1024]{2,1,0:T(8,128)(2,1)S(1)}, bf16[12,32,1024]{2,1,0:T(8,128)(2,1)S(1)}, u32[]{:S(2)}, u32[]{:S(2)}) %collective-permute-start.9) | collective-permute-done | bytes 786464 | tf_op jit(solution)/shard_map/ppermute | solution.py:95
  160.6 10.8 %shard_map.50 = f32[16,32,1024]{2,1,0:T(8,128)} custom-call(bf16[12,32,1024]{2,1,0:T(8,128)(2,1)} %get-tuple-element.25.own_ref, f32[12,16,8,1024]{3,2,1,0:T(8,128)} %broadcast_in_dim.29.src_ref), custom_call_target="tpu_custom_call" | custom-call | tf_op jit(solution)/shard_map/pallas_call | solution.py:162
  172.9 5.9 %collective-permute-start.12 = (bf16[12,32,1024]{2,1,0:T(8,128)(2,1)S(1)}, bf16[12,32,1024]{2,1,0:T(8,128)(2,1)S(1)}, u32[]{:S(2)}, u32[]{:S(2)}) collective-permute-start(bf16[12,32,1024]{2,1,0:T(8,128)(2,1)S(1)} %slice.624), channel_id=1, source_target_pairs={{0,1},{3,2},{4,5},{7,6},{8,9},{11,10},{12,13},{15,14},{16,17},{19,... | collective-permute-start | bytes 2359304 | tf_op jit(solution)/shard_map/ppermute | solution.py:95
  185.0 1.9 slice_add_fusion.31
  188.2 2.8 collective-permute-done.12
  193.6 4.3 %collective-permute-done.8 = f32[4,32,1024]{2,1,0:T(8,128)S(1)} collective-permute-done((f32[4,32,1024]{2,1,0:T(8,128)S(1)}, f32[4,32,1024]{2,1,0:T(8,128)S(1)}, u32[]{:S(2)}, u32[]{:S(2)}) %collective-permute-start.8) | collective-permute-done | bytes 524320 | tf_op jit(solution)/shard_map/ppermute | solution.py:250
  198.8 10.8 %shard_map.51 = f32[16,32,1024]{2,1,0:T(8,128)} custom-call(bf16[12,32,1024]{2,1,0:T(8,128)(2,1)} %get-tuple-element.27.own_ref, f32[12,16,8,1024]{3,2,1,0:T(8,128)} %broadcast_in_dim.29.src_ref), custom_call_target="tpu_custom_call" | custom-call | tf_op jit(solution)/shard_map/pallas_call | solution.py:162
  209.6 2.4 slice.623
  212.0 2.9 collective-permute-start.15
  214.9 10.8 %shard_map.52 = f32[16,32,1024]{2,1,0:T(8,128)} custom-call(bf16[12,32,1024]{2,1,0:T(8,128)(2,1)} %get-tuple-element.29.own_ref, f32[12,16,8,1024]{3,2,1,0:T(8,128)} %broadcast_in_dim.29.src_ref), custom_call_target="tpu_custom_call" | custom-call | tf_op jit(solution)/shard_map/pallas_call | solution.py:162
  225.7 2.6 slice.622
  233.0 5.5 %collective-permute-start.18 = (bf16[12,32,1024]{2,1,0:T(8,128)(2,1)}, bf16[12,32,1024]{2,1,0:T(8,128)(2,1)}, u32[]{:S(2)}, u32[]{:S(2)}) collective-permute-start(bf16[12,32,1024]{2,1,0:T(8,128)(2,1)} %slice.622), channel_id=1, source_target_pairs={{0,1},{3,2},{4,5},{7,6},{8,9},{11,10},{12,13},{15,14},{16,17},{19,... | collective-permute-start | bytes 2359304 | tf_op jit(solution)/shard_map/ppermute | solution.py:95
  238.5 2.0 fusion.9
  242.0 4.5 %convolution_dynamic-update-slice_fusion.7 = f32[4,256,1024]{2,1,0:T(8,128)} fusion(f32[8,32,1024]{2,1,0:T(8,128)S(1)} %convert_element_type.138, f32[16,32,1024]{2,1,0:T(8,128)} %shard_map.47, f32[4,32,1024]{2,1,0:T(8,128)S(1)} %copy-done.24, bf16[12,32,1024]{2,1,0:T(8,128)(2,1)} %collective-permute-done.3, pred[]{:T(512)S(6)} %or.3, ...), kind=kOutput, calls=%fused_computation.29 | convolution fusion | flops 807010304 | bytes 7077889 | tf_op jit(solution)/shard_map/dot_general | solution.py:253
  246.5 4.4 %convolution_dynamic-update-slice_fusion.6 = f32[4,256,1024]{2,1,0:T(8,128)} fusion(f32[4,256,1024]{2,1,0:T(8,128)} %convolution_dynamic-update-slice_fusion.7, f32[8,32,1024]{2,1,0:T(8,128)S(1)} %copy-done.18, f32[16,32,1024]{2,1,0:T(8,128)} %shard_map.48, f32[4,32,1024]{2,1,0:T(8,128)S(1)} %copy-done.27, ...), kind=kOutput, calls=%fused_computation.28 | convolution fusion | flops 807010304 | bytes 7077889 | tf_op jit(solution)/shard_map/dot_general | solution.py:253
  251.6 10.8 %shard_map.53 = f32[16,32,1024]{2,1,0:T(8,128)} custom-call(bf16[12,32,1024]{2,1,0:T(8,128)(2,1)} %get-tuple-element.31.own_ref, f32[12,16,8,1024]{3,2,1,0:T(8,128)} %broadcast_in_dim.29.src_ref), custom_call_target="tpu_custom_call" | custom-call | tf_op jit(solution)/shard_map/pallas_call | solution.py:162
  262.4 2.6 slice.621
  266.1 2.5 collective-permute-start.21
  271.2 4.5 %convolution_dynamic-update-slice_fusion.5 = f32[4,256,1024]{2,1,0:T(8,128)} fusion(f32[4,256,1024]{2,1,0:T(8,128)} %convolution_dynamic-update-slice_fusion.6, f32[8,32,1024]{2,1,0:T(8,128)S(1)} %copy-done.14, f32[16,32,1024]{2,1,0:T(8,128)} %shard_map.49, f32[4,32,1024]{2,1,0:T(8,128)} %collective-permute-done.11, bf16[12,32,1024]{2,1,0:T(8,128)(2,1)} %copy-done.21, ...), kind=kOutput, calls=%fused_computation.27 | convolution fusion | flops 807010304 | bytes 7077889 | tf_op jit(solution)/shard_map/dot_general | solution.py:253
  275.7 2.0 fusion.8
  279.2 1.8 collective-permute-done.17
  281.8 10.8 %shard_map.54 = f32[16,32,1024]{2,1,0:T(8,128)} custom-call(bf16[12,32,1024]{2,1,0:T(8,128)(2,1)} %get-tuple-element.33.own_ref, f32[12,16,8,1024]{3,2,1,0:T(8,128)} %broadcast_in_dim.29.src_ref), custom_call_target="tpu_custom_call" | custom-call | tf_op jit(solution)/shard_map/pallas_call | solution.py:162
  294.2 4.9 %collective-permute-start.24 = (bf16[12,32,1024]{2,1,0:T(8,128)(2,1)S(1)}, bf16[12,32,1024]{2,1,0:T(8,128)(2,1)S(1)}, u32[]{:S(2)}, u32[]{:S(2)}) collective-permute-start(bf16[12,32,1024]{2,1,0:T(8,128)(2,1)S(1)} %slice.620), channel_id=1, source_target_pairs={{0,1},{3,2},{4,5},{7,6},{8,9},{11,10},{12,13},{15,14},{16,17},{19,... | collective-permute-start | bytes 2359304 | tf_op jit(solution)/shard_map/ppermute | solution.py:95
  299.1 5.2 %convolution_dynamic-update-slice_fusion.4 = f32[4,256,1024]{2,1,0:T(8,128)} fusion(f32[4,256,1024]{2,1,0:T(8,128)} %convolution_dynamic-update-slice_fusion.5, f32[8,32,1024]{2,1,0:T(8,128)S(1)} %copy-done.16, f32[16,32,1024]{2,1,0:T(8,128)} %shard_map.50, f32[4,32,1024]{2,1,0:T(8,128)} %copy-done.25, bf16[12,32,1024]{2,1,0:T(8,128)(2,1)} %copy-done.22, ...), kind=kOutput, calls=%fused_computation.26 | convolution fusion | flops 807010304 | bytes 7077889 | tf_op jit(solution)/shard_map/dot_general | solution.py:253
  304.3 4.5 %convolution_dynamic-update-slice_fusion.3 = f32[4,256,1024]{2,1,0:T(8,128)} fusion(f32[4,256,1024]{2,1,0:T(8,128)} %convolution_dynamic-update-slice_fusion.4, f32[8,32,1024]{2,1,0:T(8,128)S(1)} %copy-done.20, f32[16,32,1024]{2,1,0:T(8,128)} %shard_map.51, f32[4,32,1024]{2,1,0:T(8,128)S(1)} %copy-done.29, ...), kind=kOutput, calls=%fused_computation.25 | convolution fusion | flops 807010304 | bytes 7077889 | tf_op jit(solution)/shard_map/dot_general | solution.py:253
  317.7 13.4 %collective-permute-done.20 = f32[4,32,1024]{2,1,0:T(8,128)S(1)} collective-permute-done((f32[4,32,1024]{2,1,0:T(8,128)S(1)}, f32[4,32,1024]{2,1,0:T(8,128)S(1)}, u32[]{:S(2)}, u32[]{:S(2)}) %collective-permute-start.20) | collective-permute-done | bytes 524320 | tf_op jit(solution)/shard_map/ppermute | solution.py:250
  331.1 4.0 %convolution_dynamic-update-slice_fusion.2 = f32[4,256,1024]{2,1,0:T(8,128)} fusion(f32[4,256,1024]{2,1,0:T(8,128)} %convolution_dynamic-update-slice_fusion.3, f32[8,32,1024]{2,1,0:T(8,128)S(1)} %convert_element_type.158, f32[16,32,1024]{2,1,0:T(8,128)S(1)} %copy-done.5, f32[4,32,1024]{2,1,0:T(8,128)S(1)} %collective-permute-done.20, ...), kind=kOutput, calls=%fused_computation.24 | convolution fusion | flops 807010304 | bytes 7077889 | tf_op jit(solution)/shard_map/dot_general | solution.py:253
  335.1 4.5 %collective-permute-done.23 = f32[4,32,1024]{2,1,0:T(8,128)S(1)} collective-permute-done((f32[4,32,1024]{2,1,0:T(8,128)S(1)}, f32[4,32,1024]{2,1,0:T(8,128)S(1)}, u32[]{:S(2)}, u32[]{:S(2)}) %collective-permute-start.23) | collective-permute-done | bytes 524320 | tf_op jit(solution)/shard_map/ppermute | solution.py:250
  339.6 4.0 %convolution_dynamic-update-slice_fusion.1 = f32[4,256,1024]{2,1,0:T(8,128)} fusion(f32[4,256,1024]{2,1,0:T(8,128)} %convolution_dynamic-update-slice_fusion.2, f32[8,32,1024]{2,1,0:T(8,128)S(1)} %convert_element_type.162, f32[16,32,1024]{2,1,0:T(8,128)S(1)} %copy-done.8, f32[4,32,1024]{2,1,0:T(8,128)S(1)} %collective-permute-done.23, ...), kind=kOutput, calls=%fused_computation.23 | convolution fusion | flops 807010304 | bytes 7077889 | tf_op jit(solution)/shard_map/dot_general | solution.py:253
  345.2 3.1 convolution_dynamic-update-slice_fusion
  (143 shorter events, 65.1 us)
Async XLA Ops:
  14.5 9.2 %copy-start.31 = (s32[4]{0:T(128)S(1)}, s32[4]{0:T(128)}, u32[]{:S(2)}) copy-start(s32[4]{0:T(128)} %param.6) | copy-start | bytes 52
  14.5 12.3 %copy-start.30 = (s32[256,2,6]{0,1,2:T(2,128)S(1)}, s32[256,2,6]{0,1,2:T(2,128)}, u32[]{:S(2)}) copy-start(s32[256,2,6]{0,1,2:T(2,128)} %param.5) | copy-start | bytes 36868
  28.5 7.7 %copy-start.12 = (f32[1024,512]{1,0:T(8,128)S(1)}, f32[1024,512]{1,0:T(8,128)}, u32[]{:S(2)}) copy-start(f32[1024,512]{1,0:T(8,128)} %get-tuple-element.20) | copy-start | bytes 6291460
  58.3 1.9 collective-permute-start
  60.5 12.3 %collective-permute-start.1 = (bf16[12,16,1024]{2,1,0:T(8,128)(2,1)S(1)}, bf16[12,16,1024]{2,1,0:T(8,128)(2,1)S(1)}, u32[]{:S(2)}, u32[]{:S(2)}) collective-permute-start(bf16[12,16,1024]{2,1,0:T(8,128)(2,1)S(1)} %fusion.73), channel_id=1, source_target_pairs={{0,8},{4,12},{8,0},{12,4},{16,24},{20,28},{24,16},{28,20},{1,9},{5... | collective-permute-start | bytes 1179656 | tf_op jit(solution)/shard_map/ppermute | solution.py:178
  72.9 10.7 %collective-permute-start.2 = (bf16[12,16,1024]{2,1,0:T(8,128)(2,1)S(1)}, bf16[12,16,1024]{2,1,0:T(8,128)(2,1)S(1)}, u32[]{:S(2)}, u32[]{:S(2)}) collective-permute-start(bf16[12,16,1024]{2,1,0:T(8,128)(2,1)S(1)} %add.192), channel_id=1, source_target_pairs={{0,16},{4,20},{8,24},{12,28},{16,0},{20,4},{24,8},{28,12},{1,17},{... | collective-permute-start | bytes 1179656 | tf_op jit(solution)/shard_map/ppermute | solution.py:178
  100.8 19.1 %collective-permute-start.3 = (bf16[12,32,1024]{2,1,0:T(8,128)(2,1)}, bf16[12,32,1024]{2,1,0:T(8,128)(2,1)}, u32[]{:S(2)}, u32[]{:S(2)}) collective-permute-start(bf16[12,32,1024]{2,1,0:T(8,128)(2,1)} %slice.627), channel_id=1, source_target_pairs={{0,1},{3,2},{4,5},{7,6},{8,9},{11,10},{12,13},{15,14},{16,17},{19,... | collective-permute-start | bytes 2359304 | tf_op jit(solution)/shard_map/ppermute | solution.py:95
  119.9 20.7 %collective-permute-start.6 = (bf16[12,32,1024]{2,1,0:T(8,128)(2,1)S(1)}, bf16[12,32,1024]{2,1,0:T(8,128)(2,1)}, u32[]{:S(2)}, u32[]{:S(2)}) collective-permute-start(bf16[12,32,1024]{2,1,0:T(8,128)(2,1)S(1)} %slice.626), channel_id=1, source_target_pairs={{0,1},{3,2},{4,5},{7,6},{8,9},{11,10},{12,13},{15,14},{16,17},{19,... | collective-permute-start | bytes 2359304 | tf_op jit(solution)/shard_map/ppermute | solution.py:95
  126.7 16.5 %collective-permute-start.4 = (bf16[8,32,1024]{2,1,0:T(8,128)(2,1)S(1)}, bf16[8,32,1024]{2,1,0:T(8,128)(2,1)}, u32[]{:S(2)}, u32[]{:S(2)}) collective-permute-start(bf16[8,32,1024]{2,1,0:T(8,128)(2,1)S(1)} %fusion.13), channel_id=1, source_target_pairs={{1,2},{2,1},{5,6},{6,5},{9,10},{10,9},{13,14},{14,13},{17,18},{18,... | collective-permute-start | bytes 1572872 | tf_op jit(solution)/shard_map/ppermute | solution.py:247
  138.9 8.0 %copy-start.7 = (f32[16,32,1024]{2,1,0:T(8,128)S(1)}, f32[16,32,1024]{2,1,0:T(8,128)}, u32[]{:S(2)}) copy-start(f32[16,32,1024]{2,1,0:T(8,128)} %shard_map.48) | copy-start | bytes 6291460
  140.6 16.6 %collective-permute-start.9 = (bf16[12,32,1024]{2,1,0:T(8,128)(2,1)S(1)}, bf16[12,32,1024]{2,1,0:T(8,128)(2,1)S(1)}, u32[]{:S(2)}, u32[]{:S(2)}) collective-permute-start(bf16[12,32,1024]{2,1,0:T(8,128)(2,1)S(1)} %slice.625), channel_id=1, source_target_pairs={{0,1},{3,2},{4,5},{7,6},{8,9},{11,10},{12,13},{15,14},{16,17},{19,... | collective-permute-start | bytes 2359304 | tf_op jit(solution)/shard_map/ppermute | solution.py:95
  144.4 12.8 %copy-start.3 = (f32[16,32,1024]{2,1,0:T(8,128)S(1)}, f32[16,32,1024]{2,1,0:T(8,128)}, u32[]{:S(2)}) copy-start(f32[16,32,1024]{2,1,0:T(8,128)} %shard_map.49) | copy-start | bytes 6291460
  145.7 14.1 %collective-permute-start.5 = (f32[4,32,1024]{2,1,0:T(8,128)S(1)}, f32[4,32,1024]{2,1,0:T(8,128)S(1)}, u32[]{:S(2)}, u32[]{:S(2)}) collective-permute-start(f32[4,32,1024]{2,1,0:T(8,128)S(1)} %slice_add_fusion.39), channel_id=1, source_target_pairs={{1,0},{2,3},{5,4},{6,7},{9,8},{10,11},{13,12},{14,15},{17,16},{18,... | collective-permute-start | bytes 1572872 | tf_op jit(solution)/shard_map/ppermute | solution.py:250
  148.9 29.9 %collective-permute-start.7 = (bf16[8,32,1024]{2,1,0:T(8,128)(2,1)}, bf16[8,32,1024]{2,1,0:T(8,128)(2,1)}, u32[]{:S(2)}, u32[]{:S(2)}) collective-permute-start(bf16[8,32,1024]{2,1,0:T(8,128)(2,1)} %fusion.12), channel_id=1, source_target_pairs={{1,2},{2,1},{5,6},{6,5},{9,10},{10,9},{13,14},{14,13},{17,18},{18,... | collective-permute-start | bytes 1572872 | tf_op jit(solution)/shard_map/ppermute | solution.py:247
  158.3 24.6 %collective-permute-start.10 = (bf16[8,32,1024]{2,1,0:T(8,128)(2,1)}, bf16[8,32,1024]{2,1,0:T(8,128)(2,1)}, u32[]{:S(2)}, u32[]{:S(2)}) collective-permute-start(bf16[8,32,1024]{2,1,0:T(8,128)(2,1)} %fusion.11), channel_id=1, source_target_pairs={{1,2},{2,1},{5,6},{6,5},{9,10},{10,9},{13,14},{14,13},{17,18},{18,... | collective-permute-start | bytes 1572872 | tf_op jit(solution)/shard_map/ppermute | solution.py:247
  172.9 18.1 %collective-permute-start.12 = (bf16[12,32,1024]{2,1,0:T(8,128)(2,1)S(1)}, bf16[12,32,1024]{2,1,0:T(8,128)(2,1)S(1)}, u32[]{:S(2)}, u32[]{:S(2)}) collective-permute-start(bf16[12,32,1024]{2,1,0:T(8,128)(2,1)S(1)} %slice.624), channel_id=1, source_target_pairs={{0,1},{3,2},{4,5},{7,6},{8,9},{11,10},{12,13},{15,14},{16,17},{19,... | collective-permute-start | bytes 2359304 | tf_op jit(solution)/shard_map/ppermute | solution.py:95
  180.0 11.1 %copy-start.6 = (f32[16,32,1024]{2,1,0:T(8,128)S(1)}, f32[16,32,1024]{2,1,0:T(8,128)}, u32[]{:S(2)}) copy-start(f32[16,32,1024]{2,1,0:T(8,128)} %shard_map.50) | copy-start | bytes 6291460
  181.5 16.4 %collective-permute-start.8 = (f32[4,32,1024]{2,1,0:T(8,128)S(1)}, f32[4,32,1024]{2,1,0:T(8,128)S(1)}, u32[]{:S(2)}, u32[]{:S(2)}) collective-permute-start(f32[4,32,1024]{2,1,0:T(8,128)S(1)} %slice_add_fusion.35), channel_id=1, source_target_pairs={{1,0},{2,3},{5,4},{6,7},{9,8},{10,11},{13,12},{14,15},{17,16},{18,... | collective-permute-start | bytes 1572872 | tf_op jit(solution)/shard_map/ppermute | solution.py:250
  187.0 27.9 %collective-permute-start.11 = (f32[4,32,1024]{2,1,0:T(8,128)}, f32[4,32,1024]{2,1,0:T(8,128)}, u32[]{:S(2)}, u32[]{:S(2)}) collective-permute-start(f32[4,32,1024]{2,1,0:T(8,128)} %slice_add_fusion.31), channel_id=1, source_target_pairs={{1,0},{2,3},{5,4},{6,7},{9,8},{10,11},{13,12},{14,15},{17,16},{18,... | collective-permute-start | bytes 1572872 | tf_op jit(solution)/shard_map/ppermute | solution.py:250
  192.2 36.2 %collective-permute-start.13 = (bf16[8,32,1024]{2,1,0:T(8,128)(2,1)}, bf16[8,32,1024]{2,1,0:T(8,128)(2,1)}, u32[]{:S(2)}, u32[]{:S(2)}) collective-permute-start(bf16[8,32,1024]{2,1,0:T(8,128)(2,1)} %fusion.10), channel_id=1, source_target_pairs={{1,2},{2,1},{5,6},{6,5},{9,10},{10,9},{13,14},{14,13},{17,18},{18,... | collective-permute-start | bytes 1572872 | tf_op jit(solution)/shard_map/ppermute | solution.py:247
  212.0 21.0 %collective-permute-start.15 = (bf16[12,32,1024]{2,1,0:T(8,128)(2,1)}, bf16[12,32,1024]{2,1,0:T(8,128)(2,1)}, u32[]{:S(2)}, u32[]{:S(2)}) collective-permute-start(bf16[12,32,1024]{2,1,0:T(8,128)(2,1)} %slice.623), channel_id=1, source_target_pairs={{0,1},{3,2},{4,5},{7,6},{8,9},{11,10},{12,13},{15,14},{16,17},{19,... | collective-permute-start | bytes 2359304 | tf_op jit(solution)/shard_map/ppermute | solution.py:95
  225.7 12.8 %copy-start.9 = (f32[16,32,1024]{2,1,0:T(8,128)S(1)}, f32[16,32,1024]{2,1,0:T(8,128)}, u32[]{:S(2)}) copy-start(f32[16,32,1024]{2,1,0:T(8,128)} %shard_map.51) | copy-start | bytes 6291460
  230.5 11.5 %copy-start = (f32[512,1024]{0,1:T(8,128)S(1)}, f32[512,1024]{0,1:T(8,128)}, u32[]{:S(2)}) copy-start(f32[512,1024]{0,1:T(8,128)} %get-tuple-element.49) | copy-start | bytes 6291460
  230.5 11.5 %copy-start.24 = (f32[4,32,1024]{2,1,0:T(8,128)S(1)}, f32[4,32,1024]{2,1,0:T(8,128)}, u32[]{:S(2)}) copy-start(f32[4,32,1024]{2,1,0:T(8,128)} %copy-done.23) | copy-start | bytes 1572868
  231.7 19.1 %collective-permute-start.14 = (f32[4,32,1024]{2,1,0:T(8,128)S(1)}, f32[4,32,1024]{2,1,0:T(8,128)S(1)}, u32[]{:S(2)}, u32[]{:S(2)}) collective-permute-start(f32[4,32,1024]{2,1,0:T(8,128)S(1)} %slice_add_fusion.27), channel_id=1, source_target_pairs={{1,0},{2,3},{5,4},{6,7},{9,8},{10,11},{13,12},{14,15},{17,16},{18,... | collective-permute-start | bytes 1572872 | tf_op jit(solution)/shard_map/ppermute | solution.py:250
  233.0 33.1 %collective-permute-start.18 = (bf16[12,32,1024]{2,1,0:T(8,128)(2,1)}, bf16[12,32,1024]{2,1,0:T(8,128)(2,1)}, u32[]{:S(2)}, u32[]{:S(2)}) collective-permute-start(bf16[12,32,1024]{2,1,0:T(8,128)(2,1)} %slice.622), channel_id=1, source_target_pairs={{0,1},{3,2},{4,5},{7,6},{8,9},{11,10},{12,13},{15,14},{16,17},{19,... | collective-permute-start | bytes 2359304 | tf_op jit(solution)/shard_map/ppermute | solution.py:95
  240.5 24.5 %collective-permute-start.16 = (bf16[8,32,1024]{2,1,0:T(8,128)(2,1)}, bf16[8,32,1024]{2,1,0:T(8,128)(2,1)}, u32[]{:S(2)}, u32[]{:S(2)}) collective-permute-start(bf16[8,32,1024]{2,1,0:T(8,128)(2,1)} %fusion.9), channel_id=1, source_target_pairs={{1,2},{2,1},{5,6},{6,5},{9,10},{10,9},{13,14},{14,13},{17,18},{18,... | collective-permute-start | bytes 1572872 | tf_op jit(solution)/shard_map/ppermute | solution.py:247
  242.0 4.5 %copy-start.18 = (f32[8,32,1024]{2,1,0:T(8,128)S(1)}, f32[8,32,1024]{2,1,0:T(8,128)}, u32[]{:S(2)}) copy-start(f32[8,32,1024]{2,1,0:T(8,128)} %copy-done.17) | copy-start | bytes 3145732
  242.0 4.5 %copy-start.27 = (f32[4,32,1024]{2,1,0:T(8,128)S(1)}, f32[4,32,1024]{2,1,0:T(8,128)}, u32[]{:S(2)}) copy-start(f32[4,32,1024]{2,1,0:T(8,128)} %copy-done.26) | copy-start | bytes 1572868
  262.4 8.8 %copy-start.1 = (f32[512,1024]{0,1:T(8,128)S(1)}, f32[512,1024]{0,1:T(8,128)}, u32[]{:S(2)}) copy-start(f32[512,1024]{0,1:T(8,128)} %get-tuple-element.49) | copy-start | bytes 6291460
  262.4 8.8 %copy-start.14 = (f32[8,32,1024]{2,1,0:T(8,128)S(1)}, f32[8,32,1024]{2,1,0:T(8,128)}, u32[]{:S(2)}) copy-start(f32[8,32,1024]{2,1,0:T(8,128)} %copy-done.13) | copy-start | bytes 3145732
  266.1 28.0 %collective-permute-start.21 = (bf16[12,32,1024]{2,1,0:T(8,128)(2,1)}, bf16[12,32,1024]{2,1,0:T(8,128)(2,1)}, u32[]{:S(2)}, u32[]{:S(2)}) collective-permute-start(bf16[12,32,1024]{2,1,0:T(8,128)(2,1)} %slice.621), channel_id=1, source_target_pairs={{0,1},{3,2},{4,5},{7,6},{8,9},{11,10},{12,13},{15,14},{16,17},{19,... | collective-permute-start | bytes 2359304 | tf_op jit(solution)/shard_map/ppermute | solution.py:95
  269.7 6.0 %copy-start.4 = (f32[16,32,1024]{2,1,0:T(8,128)S(1)}, f32[16,32,1024]{2,1,0:T(8,128)}, u32[]{:S(2)}) copy-start(f32[16,32,1024]{2,1,0:T(8,128)} %shard_map.52) | copy-start | bytes 6291460
  269.8 11.2 %collective-permute-start.17 = (f32[4,32,1024]{2,1,0:T(8,128)S(1)}, f32[4,32,1024]{2,1,0:T(8,128)S(1)}, u32[]{:S(2)}, u32[]{:S(2)}) collective-permute-start(f32[4,32,1024]{2,1,0:T(8,128)S(1)} %slice_add_fusion.23), channel_id=1, source_target_pairs={{1,0},{2,3},{5,4},{6,7},{9,8},{10,11},{13,12},{14,15},{17,16},{18,... | collective-permute-start | bytes 1572872 | tf_op jit(solution)/shard_map/ppermute | solution.py:250
  277.8 31.1 %collective-permute-start.19 = (bf16[8,32,1024]{2,1,0:T(8,128)(2,1)}, bf16[8,32,1024]{2,1,0:T(8,128)(2,1)}, u32[]{:S(2)}, u32[]{:S(2)}) collective-permute-start(bf16[8,32,1024]{2,1,0:T(8,128)(2,1)} %fusion.8), channel_id=1, source_target_pairs={{1,2},{2,1},{5,6},{6,5},{9,10},{10,9},{13,14},{14,13},{17,18},{18,... | collective-permute-start | bytes 1572872 | tf_op jit(solution)/shard_map/ppermute | solution.py:247
  281.8 17.3 %copy-start.16 = (f32[8,32,1024]{2,1,0:T(8,128)S(1)}, f32[8,32,1024]{2,1,0:T(8,128)}, u32[]{:S(2)}) copy-start(f32[8,32,1024]{2,1,0:T(8,128)} %copy-done.15) | copy-start | bytes 3145732
  294.1 10.2 %copy-start.2 = (f32[512,1024]{0,1:T(8,128)S(1)}, f32[512,1024]{0,1:T(8,128)}, u32[]{:S(2)}) copy-start(f32[512,1024]{0,1:T(8,128)} %get-tuple-element.49) | copy-start | bytes 6291460
  294.1 10.2 %copy-start.20 = (f32[8,32,1024]{2,1,0:T(8,128)S(1)}, f32[8,32,1024]{2,1,0:T(8,128)}, u32[]{:S(2)}) copy-start(f32[8,32,1024]{2,1,0:T(8,128)} %copy-done.19) | copy-start | bytes 3145732
  294.1 10.1 %copy-start.29 = (f32[4,32,1024]{2,1,0:T(8,128)S(1)}, f32[4,32,1024]{2,1,0:T(8,128)}, u32[]{:S(2)}) copy-start(f32[4,32,1024]{2,1,0:T(8,128)} %copy-done.28) | copy-start | bytes 1572868
  294.2 18.0 %collective-permute-start.24 = (bf16[12,32,1024]{2,1,0:T(8,128)(2,1)S(1)}, bf16[12,32,1024]{2,1,0:T(8,128)(2,1)S(1)}, u32[]{:S(2)}, u32[]{:S(2)}) collective-permute-start(bf16[12,32,1024]{2,1,0:T(8,128)(2,1)S(1)} %slice.620), channel_id=1, source_target_pairs={{0,1},{3,2},{4,5},{7,6},{8,9},{11,10},{12,13},{15,14},{16,17},{19,... | collective-permute-start | bytes 2359304 | tf_op jit(solution)/shard_map/ppermute | solution.py:95
  304.3 5.8 %copy-start.8 = (f32[16,32,1024]{2,1,0:T(8,128)S(1)}, f32[16,32,1024]{2,1,0:T(8,128)}, u32[]{:S(2)}) copy-start(f32[16,32,1024]{2,1,0:T(8,128)} %shard_map.53) | copy-start | bytes 6291460
  308.8 3.4 copy-start.10
  310.1 2.9 copy-start.5
  311.5 3.0 collective-permute-start.22
  312.4 3.8 %collective-permute-start.25 = (bf16[8,32,1024]{2,1,0:T(8,128)(2,1)S(1)}, bf16[8,32,1024]{2,1,0:T(8,128)(2,1)S(1)}, u32[]{:S(2)}, u32[]{:S(2)}) collective-permute-start(bf16[8,32,1024]{2,1,0:T(8,128)(2,1)S(1)} %fusion.6), channel_id=1, source_target_pairs={{1,2},{2,1},{5,6},{6,5},{9,10},{10,9},{13,14},{14,13},{17,18},{18,... | collective-permute-start | bytes 1572872 | tf_op jit(solution)/shard_map/ppermute | solution.py:247
  313.2 17.9 %collective-permute-start.20 = (f32[4,32,1024]{2,1,0:T(8,128)S(1)}, f32[4,32,1024]{2,1,0:T(8,128)S(1)}, u32[]{:S(2)}, u32[]{:S(2)}) collective-permute-start(f32[4,32,1024]{2,1,0:T(8,128)S(1)} %slice_add_fusion.19), channel_id=1, source_target_pairs={{1,0},{2,3},{5,4},{6,7},{9,8},{10,11},{13,12},{14,15},{17,16},{18,... | collective-permute-start | bytes 1572872 | tf_op jit(solution)/shard_map/ppermute | solution.py:250
  314.7 24.9 %collective-permute-start.23 = (f32[4,32,1024]{2,1,0:T(8,128)S(1)}, f32[4,32,1024]{2,1,0:T(8,128)S(1)}, u32[]{:S(2)}, u32[]{:S(2)}) collective-permute-start(f32[4,32,1024]{2,1,0:T(8,128)S(1)} %slice_add_fusion.15), channel_id=1, source_target_pairs={{1,0},{2,3},{5,4},{6,7},{9,8},{10,11},{13,12},{14,15},{17,16},{18,... | collective-permute-start | bytes 1572872 | tf_op jit(solution)/shard_map/ppermute | solution.py:250
  316.4 28.8 %collective-permute-start.26 = (f32[4,32,1024]{2,1,0:T(8,128)S(1)}, f32[4,32,1024]{2,1,0:T(8,128)S(1)}, u32[]{:S(2)}, u32[]{:S(2)}) collective-permute-start(f32[4,32,1024]{2,1,0:T(8,128)S(1)} %slice_add_fusion.11), channel_id=1, source_target_pairs={{1,0},{2,3},{5,4},{6,7},{9,8},{10,11},{13,12},{14,15},{17,16},{18,... | collective-permute-start | bytes 1572872 | tf_op jit(solution)/shard_map/ppermute | solution.py:250
  (11 other events, 14.3 us)

commit v5 on v4

--- a/solution.py
+++ b/solution.py
@@ -250,7 +250,7 @@
         back = lax.ppermute(low, "tm", [(1, 0), (2, 3)])
         returned.append(back)
         final = jnp.where(is_edge, near_part[:per_group] + back, high)
-        outs.append(jnp.dot(final, inverse, precision=lax.Precision.HIGH))
+        outs.append(jnp.dot(final, inverse, preferred_element_type=jnp.float32))
     return jnp.concatenate(outs, axis=1)
 
 

time: 350 us -> 350 us (level)
  matrix products: 34.2 us -> 22.4 us
  waiting for transfers between devices: 51.7 us -> 60.6 us
    dot_general x8, matrix products: 34.2 us -> 22.4 us  [on_line(): outs.append(jnp.dot(final, inverse, preferred_element_type=jnp.float32))]
    ppermute x8, waiting for transfers between devices: 12.1 us -> 17.6 us  [edge_first(): return lax.ppermute(values, 'tm', [(0, 1), (groups - 1, groups - 2)])]
    ppermute x8, waiting for transfers between devices: 25.6 us -> 29.1 us  [on_line(): back = lax.ppermute(low, 'tm', [(1, 0), (2, 3)])]
    unnamed x65 -> x67, local copies, waits for them, and re-layouts: 14.3 us -> 13 us
  transfers between devices with their start and end apart: 27 -> 27, of which waited for: 11 -> 11; matrix products, arithmetic and copies ran while one was open for 22% -> 20% of each run, Pallas kernels for 22% -> 22%
where the time goes in v5:
time: 350 us; the launch traced here: 348 us
  Pallas kernels  101 us (29%)
  starting transfers between devices  62.8 us (18%)
  waiting for transfers between devices  60.6 us (17%)
  local copies, waits for them, and re-layouts  42.4 us (12%)
  other arithmetic  42.2 us (12%)
  matrix products  22.4 us (6%)
  between operations  15.9 us (5%)
    pallas_call x8, Pallas kernels, cross_chunk(): pl.pallas_call(cross_kernel, grid=(width // step_rows,), in_specs=[pl.Blo...  86.1 us
    ppermute x8, starting transfers between devices, edge_first(): return lax.ppermute(values, 'tm', [(0, 1), (groups - 1, groups - 2)])  36.8 us
    ppermute x8, waiting for transfers between devices, on_line(): back = lax.ppermute(low, 'tm', [(1, 0), (2, 3)])  29.1 us
    dot_general x8, matrix products, on_line(): outs.append(jnp.dot(final, inverse, preferred_element_type=jnp.float32))  22.4 us
    ppermute x8, waiting for transfers between devices, edge_first(): return lax.ppermute(values, 'tm', [(0, 1), (groups - 1, groups - 2)])  17.6 us
    slice x8, local copies, waits for them, and re-layouts, on_line(): edge_out = part[:source_count - per_group].astype(jnp.bfloat16)  16.4 us
    pallas_call x1, Pallas kernels, whiten_segments(): pl.pallas_call(whiten_kernel, grid=(segments,), in_specs=[pl.BlockSpec((N...  15.2 us
    ppermute x3, waiting for transfers between devices, butterfly_sum(): lax.ppermute(values, axis, [(b, b ^ step) for b in range(count)])  13.9 us
  transfers between devices with their start and end apart: 27, of which 11 were waited for; matrix products, arithmetic and copies ran while one was open for 20% of the time, Pallas kernels for 22%

profile of v5, /device:TPU:0, one launch (start us, length us, event | category | flops | bytes accessed | tf_op | source)
XLA Modules:
  0.0 347.6 jit_solution(16472588664969544658)
XLA Ops:
  14.2 9.0 %fusion.14 = (f32[1024,512]{1,0:T(8,128)S(1)}, f32[1024,512]{1,0:T(8,128)}) fusion(), kind=kLoop, calls=%fused_computation.46 | loop fusion | flops 7340032 | bytes 4194304 | tf_op jit(solution)/shard_map/sin | solution.py:199
  30.1 7.6 %copy.15 = bf16[256,2,6,1024]{3,0,2,1:T(8,128)(2,1)} copy(bf16[256,2,6,1024]{3,1,2,0:T(2,128)(2,1)} %param.4) | data formatting | bytes 12582912 | tf_op args[0]
  39.3 15.2 %shard_map.46 = bf16[8,12,32,1024]{3,2,1,0:T(8,128)(2,1)} custom-call(bf16[12,256,1024]{2,1,0:T(8,128)(2,1)} %bitcast.61, bf16[1024,1024]{1,0:T(8,128)(2,1)} %pad_maximum_fusion.forward_ref, f32[12,256,1]{2,1,0:T(8,128)} %copy.17.mask_ref), custom_call_target="tpu_custom_call" | custom-call | tf_op jit(solution)/shard_map/pallas_call | solution.py:108
  58.5 2.9 collective-permute-start.1
  61.4 9.4 %collective-permute-done.1 = bf16[12,16,1024]{2,1,0:T(8,128)(2,1)S(1)} collective-permute-done((bf16[12,16,1024]{2,1,0:T(8,128)(2,1)S(1)}, bf16[12,16,1024]{2,1,0:T(8,128)(2,1)S(1)}, u32[]{:S(2)}, u32[]{:S(2)}) %collective-permute-start.1) | collective-permute-done | bytes 393248 | tf_op jit(solution)/shard_map/ppermute | solution.py:178
  71.0 1.8 collective-permute-start.2
  72.8 5.7 %slice_bitcast_fusion = (bf16[12,32,1024]{2,1,0:T(8,128)(2,1)}, bf16[12,32,1024]{2,1,0:T(8,128)(2,1)}, bf16[12,32,1024]{2,1,0:T(8,128)(2,1)}, bf16[12,32,1024]{2...) fusion(bf16[8,12,32,1024]{3,2,1,0:T(8,128)(2,1)} %shard_map.46), kind=kLoop, calls=%fused_computation.48 | loop fusion | bytes 12582912 | tf_op jit(solution)/shard_map/squeeze | solution.py:233
  78.5 3.2 collective-permute-done.2
  82.3 3.4 broadcast_in_dim.29.src_ref
  85.7 10.7 %shard_map.47 = f32[16,32,1024]{2,1,0:T(8,128)} custom-call(bf16[12,32,1024]{2,1,0:T(8,128)(2,1)} %get-tuple-element.42.own_ref, f32[12,16,8,1024]{3,2,1,0:T(8,128)} %broadcast_in_dim.29.src_ref), custom_call_target="tpu_custom_call" | custom-call | tf_op jit(solution)/shard_map/pallas_call | solution.py:162
  97.9 4.3 %collective-permute-start.3 = (bf16[12,32,1024]{2,1,0:T(8,128)(2,1)S(1)}, bf16[12,32,1024]{2,1,0:T(8,128)(2,1)}, u32[]{:S(2)}, u32[]{:S(2)}) collective-permute-start(bf16[12,32,1024]{2,1,0:T(8,128)(2,1)S(1)} %slice.627), channel_id=1, source_target_pairs={{0,1},{3,2},{4,5},{7,6},{8,9},{11,10},{12,13},{15,14},{16,17},{19,... | collective-permute-start | bytes 2359304 | tf_op jit(solution)/shard_map/ppermute | solution.py:95
  102.3 10.7 %shard_map.48 = f32[16,32,1024]{2,1,0:T(8,128)} custom-call(bf16[12,32,1024]{2,1,0:T(8,128)(2,1)} %get-tuple-element.41.own_ref, f32[12,16,8,1024]{3,2,1,0:T(8,128)} %broadcast_in_dim.29.src_ref), custom_call_target="tpu_custom_call" | custom-call | tf_op jit(solution)/shard_map/pallas_call | solution.py:162
  114.7 2.0 collective-permute-done.3
  116.7 4.5 %collective-permute-start.6 = (bf16[12,32,1024]{2,1,0:T(8,128)(2,1)S(1)}, bf16[12,32,1024]{2,1,0:T(8,128)(2,1)S(1)}, u32[]{:S(2)}, u32[]{:S(2)}) collective-permute-start(bf16[12,32,1024]{2,1,0:T(8,128)(2,1)S(1)} %slice.626), channel_id=1, source_target_pairs={{0,1},{3,2},{4,5},{7,6},{8,9},{11,10},{12,13},{15,14},{16,17},{19,... | collective-permute-start | bytes 2359304 | tf_op jit(solution)/shard_map/ppermute | solution.py:95
  124.2 11.4 %collective-permute-done.6 = bf16[12,32,1024]{2,1,0:T(8,128)(2,1)S(1)} collective-permute-done((bf16[12,32,1024]{2,1,0:T(8,128)(2,1)S(1)}, bf16[12,32,1024]{2,1,0:T(8,128)(2,1)S(1)}, u32[]{:S(2)}, u32[]{:S(2)}) %collective-permute-start.6) | collective-permute-done | bytes 786464 | tf_op jit(solution)/shard_map/ppermute | solution.py:95
  138.2 10.7 %shard_map.49 = f32[16,32,1024]{2,1,0:T(8,128)} custom-call(bf16[12,32,1024]{2,1,0:T(8,128)(2,1)} %get-tuple-element.23.own_ref, f32[12,16,8,1024]{3,2,1,0:T(8,128)} %broadcast_in_dim.29.src_ref), custom_call_target="tpu_custom_call" | custom-call | tf_op jit(solution)/shard_map/pallas_call | solution.py:162
  150.4 6.5 %collective-permute-start.9 = (bf16[12,32,1024]{2,1,0:T(8,128)(2,1)S(1)}, bf16[12,32,1024]{2,1,0:T(8,128)(2,1)S(1)}, u32[]{:S(2)}, u32[]{:S(2)}) collective-permute-start(bf16[12,32,1024]{2,1,0:T(8,128)(2,1)S(1)} %slice.625), channel_id=1, source_target_pairs={{0,1},{3,2},{4,5},{7,6},{8,9},{11,10},{12,13},{15,14},{16,17},{19,... | collective-permute-start | bytes 2359304 | tf_op jit(solution)/shard_map/ppermute | solution.py:95
  162.8 1.9 slice_add_fusion.35
  166.0 4.2 %collective-permute-done.9 = bf16[12,32,1024]{2,1,0:T(8,128)(2,1)S(1)} collective-permute-done((bf16[12,32,1024]{2,1,0:T(8,128)(2,1)S(1)}, bf16[12,32,1024]{2,1,0:T(8,128)(2,1)S(1)}, u32[]{:S(2)}, u32[]{:S(2)}) %collective-permute-start.9) | collective-permute-done | bytes 786464 | tf_op jit(solution)/shard_map/ppermute | solution.py:95
  172.7 3.4 collective-permute-done.5
  176.9 10.8 %shard_map.50 = f32[16,32,1024]{2,1,0:T(8,128)} custom-call(bf16[12,32,1024]{2,1,0:T(8,128)(2,1)} %get-tuple-element.25.own_ref, f32[12,16,8,1024]{3,2,1,0:T(8,128)} %broadcast_in_dim.29.src_ref), custom_call_target="tpu_custom_call" | custom-call | tf_op jit(solution)/shard_map/pallas_call | solution.py:162
  187.7 2.4 slice.624
  190.1 2.8 collective-permute-start.12
  192.9 10.8 %shard_map.51 = f32[16,32,1024]{2,1,0:T(8,128)} custom-call(bf16[12,32,1024]{2,1,0:T(8,128)(2,1)} %get-tuple-element.27.own_ref, f32[12,16,8,1024]{3,2,1,0:T(8,128)} %broadcast_in_dim.29.src_ref), custom_call_target="tpu_custom_call" | custom-call | tf_op jit(solution)/shard_map/pallas_call | solution.py:162
  203.7 2.6 slice.623
  210.3 2.0 fusion.10
  213.8 7.5 %collective-permute-start.15 = (bf16[12,32,1024]{2,1,0:T(8,128)(2,1)}, bf16[12,32,1024]{2,1,0:T(8,128)(2,1)}, u32[]{:S(2)}, u32[]{:S(2)}) collective-permute-start(bf16[12,32,1024]{2,1,0:T(8,128)(2,1)} %slice.623), channel_id=1, source_target_pairs={{0,1},{3,2},{4,5},{7,6},{8,9},{11,10},{12,13},{15,14},{16,17},{19,... | collective-permute-start | bytes 2359304 | tf_op jit(solution)/shard_map/ppermute | solution.py:95
  224.6 10.8 %shard_map.52 = f32[16,32,1024]{2,1,0:T(8,128)} custom-call(bf16[12,32,1024]{2,1,0:T(8,128)(2,1)} %get-tuple-element.29.own_ref, f32[12,16,8,1024]{3,2,1,0:T(8,128)} %broadcast_in_dim.29.src_ref), custom_call_target="tpu_custom_call" | custom-call | tf_op jit(solution)/shard_map/pallas_call | solution.py:162
  235.4 2.6 slice.622
  242.7 5.5 %collective-permute-start.18 = (bf16[12,32,1024]{2,1,0:T(8,128)(2,1)}, bf16[12,32,1024]{2,1,0:T(8,128)(2,1)}, u32[]{:S(2)}, u32[]{:S(2)}) collective-permute-start(bf16[12,32,1024]{2,1,0:T(8,128)(2,1)} %slice.622), channel_id=1, source_target_pairs={{0,1},{3,2},{4,5},{7,6},{8,9},{11,10},{12,13},{15,14},{16,17},{19,... | collective-permute-start | bytes 2359304 | tf_op jit(solution)/shard_map/ppermute | solution.py:95
  248.2 2.0 fusion.9
  251.8 2.9 convolution_dynamic-update-slice_fusion.7
  254.7 3.0 convolution_dynamic-update-slice_fusion.6
  258.5 10.7 %shard_map.53 = f32[16,32,1024]{2,1,0:T(8,128)} custom-call(bf16[12,32,1024]{2,1,0:T(8,128)(2,1)} %get-tuple-element.31.own_ref, f32[12,16,8,1024]{3,2,1,0:T(8,128)} %broadcast_in_dim.29.src_ref), custom_call_target="tpu_custom_call" | custom-call | tf_op jit(solution)/shard_map/pallas_call | solution.py:162
  269.3 2.6 slice.621
  273.0 2.2 collective-permute-start.21
  276.8 2.9 convolution_dynamic-update-slice_fusion.5
  279.7 2.0 fusion.8
  283.2 3.4 collective-permute-done.17
  287.4 10.8 %shard_map.54 = f32[16,32,1024]{2,1,0:T(8,128)} custom-call(bf16[12,32,1024]{2,1,0:T(8,128)(2,1)} %get-tuple-element.33.own_ref, f32[12,16,8,1024]{3,2,1,0:T(8,128)} %broadcast_in_dim.29.src_ref), custom_call_target="tpu_custom_call" | custom-call | tf_op jit(solution)/shard_map/pallas_call | solution.py:162
  299.8 3.5 %collective-permute-start.24 = (bf16[12,32,1024]{2,1,0:T(8,128)(2,1)S(1)}, bf16[12,32,1024]{2,1,0:T(8,128)(2,1)S(1)}, u32[]{:S(2)}, u32[]{:S(2)}) collective-permute-start(bf16[12,32,1024]{2,1,0:T(8,128)(2,1)S(1)} %slice.620), channel_id=1, source_target_pairs={{0,1},{3,2},{4,5},{7,6},{8,9},{11,10},{12,13},{15,14},{16,17},{19,... | collective-permute-start | bytes 2359304 | tf_op jit(solution)/shard_map/ppermute | solution.py:95
  303.3 3.7 %convolution_dynamic-update-slice_fusion.4 = f32[4,256,1024]{2,1,0:T(8,128)} fusion(f32[4,256,1024]{2,1,0:T(8,128)} %convolution_dynamic-update-slice_fusion.5, f32[8,32,1024]{2,1,0:T(8,128)S(1)} %copy-done.13, f32[16,32,1024]{2,1,0:T(8,128)} %shard_map.50, f32[4,32,1024]{2,1,0:T(8,128)} %copy-done.30, bf16[12,32,1024]{2,1,0:T(8,128)(2,1)} %collective-permute-done.12, ...), kind=kOutput, calls=%fused_computation.26 | convolution fusion | flops 273285120 | bytes 4980737 | tf_op jit(solution)/shard_map/dot_general | solution.py:253
  307.1 3.0 convolution_dynamic-update-slice_fusion.3
  318.6 13.7 %collective-permute-done.20 = f32[4,32,1024]{2,1,0:T(8,128)S(1)} collective-permute-done((f32[4,32,1024]{2,1,0:T(8,128)S(1)}, f32[4,32,1024]{2,1,0:T(8,128)S(1)}, u32[]{:S(2)}, u32[]{:S(2)}) %collective-permute-start.20) | collective-permute-done | bytes 524320 | tf_op jit(solution)/shard_map/ppermute | solution.py:250
  332.3 2.6 convolution_dynamic-update-slice_fusion.2
  334.9 5.5 %collective-permute-done.23 = f32[4,32,1024]{2,1,0:T(8,128)S(1)} collective-permute-done((f32[4,32,1024]{2,1,0:T(8,128)S(1)}, f32[4,32,1024]{2,1,0:T(8,128)S(1)}, u32[]{:S(2)}, u32[]{:S(2)}) %collective-permute-start.23) | collective-permute-done | bytes 524320 | tf_op jit(solution)/shard_map/ppermute | solution.py:250
  340.4 2.6 convolution_dynamic-update-slice_fusion.1
  342.9 3.0 collective-permute-done.26
  (147 shorter events, 65.1 us)
Async XLA Ops:
  14.1 9.0 %copy-start.25 = (s32[4]{0:T(128)S(1)}, s32[4]{0:T(128)}, u32[]{:S(2)}) copy-start(s32[4]{0:T(128)} %param.6) | copy-start | bytes 52
  14.1 12.3 %copy-start.24 = (s32[256,2,6]{0,1,2:T(2,128)S(1)}, s32[256,2,6]{0,1,2:T(2,128)}, u32[]{:S(2)}) copy-start(s32[256,2,6]{0,1,2:T(2,128)} %param.5) | copy-start | bytes 36868
  56.3 1.9 collective-permute-start
  58.5 12.3 %collective-permute-start.1 = (bf16[12,16,1024]{2,1,0:T(8,128)(2,1)S(1)}, bf16[12,16,1024]{2,1,0:T(8,128)(2,1)S(1)}, u32[]{:S(2)}, u32[]{:S(2)}) collective-permute-start(bf16[12,16,1024]{2,1,0:T(8,128)(2,1)S(1)} %fusion.73), channel_id=1, source_target_pairs={{0,8},{4,12},{8,0},{12,4},{16,24},{20,28},{24,16},{28,20},{1,9},{5... | collective-permute-start | bytes 1179656 | tf_op jit(solution)/shard_map/ppermute | solution.py:178
  71.0 10.7 %collective-permute-start.2 = (bf16[12,16,1024]{2,1,0:T(8,128)(2,1)S(1)}, bf16[12,16,1024]{2,1,0:T(8,128)(2,1)S(1)}, u32[]{:S(2)}, u32[]{:S(2)}) collective-permute-start(bf16[12,16,1024]{2,1,0:T(8,128)(2,1)S(1)} %add.192), channel_id=1, source_target_pairs={{0,16},{4,20},{8,24},{12,28},{16,0},{20,4},{24,8},{28,12},{1,17},{... | collective-permute-start | bytes 1179656 | tf_op jit(solution)/shard_map/ppermute | solution.py:178
  97.9 18.8 %collective-permute-start.3 = (bf16[12,32,1024]{2,1,0:T(8,128)(2,1)S(1)}, bf16[12,32,1024]{2,1,0:T(8,128)(2,1)}, u32[]{:S(2)}, u32[]{:S(2)}) collective-permute-start(bf16[12,32,1024]{2,1,0:T(8,128)(2,1)S(1)} %slice.627), channel_id=1, source_target_pairs={{0,1},{3,2},{4,5},{7,6},{8,9},{11,10},{12,13},{15,14},{16,17},{19,... | collective-permute-start | bytes 2359304 | tf_op jit(solution)/shard_map/ppermute | solution.py:95
  113.0 22.6 %copy-start.2 = (f32[16,32,1024]{2,1,0:T(8,128)S(1)}, f32[16,32,1024]{2,1,0:T(8,128)}, u32[]{:S(2)}) copy-start(f32[16,32,1024]{2,1,0:T(8,128)} %shard_map.48) | copy-start | bytes 6291460
  116.7 18.9 %collective-permute-start.6 = (bf16[12,32,1024]{2,1,0:T(8,128)(2,1)S(1)}, bf16[12,32,1024]{2,1,0:T(8,128)(2,1)S(1)}, u32[]{:S(2)}, u32[]{:S(2)}) collective-permute-start(bf16[12,32,1024]{2,1,0:T(8,128)(2,1)S(1)} %slice.626), channel_id=1, source_target_pairs={{0,1},{3,2},{4,5},{7,6},{8,9},{11,10},{12,13},{15,14},{16,17},{19,... | collective-permute-start | bytes 2359304 | tf_op jit(solution)/shard_map/ppermute | solution.py:95
  122.7 34.2 %collective-permute-start.4 = (bf16[8,32,1024]{2,1,0:T(8,128)(2,1)S(1)}, bf16[8,32,1024]{2,1,0:T(8,128)(2,1)}, u32[]{:S(2)}, u32[]{:S(2)}) collective-permute-start(bf16[8,32,1024]{2,1,0:T(8,128)(2,1)S(1)} %fusion.13), channel_id=1, source_target_pairs={{1,2},{2,1},{5,6},{6,5},{9,10},{10,9},{13,14},{14,13},{17,18},{18,... | collective-permute-start | bytes 1572872 | tf_op jit(solution)/shard_map/ppermute | solution.py:247
  136.7 23.9 %collective-permute-start.7 = (bf16[8,32,1024]{2,1,0:T(8,128)(2,1)}, bf16[8,32,1024]{2,1,0:T(8,128)(2,1)}, u32[]{:S(2)}, u32[]{:S(2)}) collective-permute-start(bf16[8,32,1024]{2,1,0:T(8,128)(2,1)} %fusion.12), channel_id=1, source_target_pairs={{1,2},{2,1},{5,6},{6,5},{9,10},{10,9},{13,14},{14,13},{17,18},{18,... | collective-permute-start | bytes 1572872 | tf_op jit(solution)/shard_map/ppermute | solution.py:247
  150.4 19.7 %collective-permute-start.9 = (bf16[12,32,1024]{2,1,0:T(8,128)(2,1)S(1)}, bf16[12,32,1024]{2,1,0:T(8,128)(2,1)S(1)}, u32[]{:S(2)}, u32[]{:S(2)}) collective-permute-start(bf16[12,32,1024]{2,1,0:T(8,128)(2,1)S(1)} %slice.625), channel_id=1, source_target_pairs={{0,1},{3,2},{4,5},{7,6},{8,9},{11,10},{12,13},{15,14},{16,17},{19,... | collective-permute-start | bytes 2359304 | tf_op jit(solution)/shard_map/ppermute | solution.py:95
  158.1 12.1 %copy-start.1 = (f32[16,32,1024]{2,1,0:T(8,128)S(1)}, f32[16,32,1024]{2,1,0:T(8,128)}, u32[]{:S(2)}) copy-start(f32[16,32,1024]{2,1,0:T(8,128)} %shard_map.49) | copy-start | bytes 6291460
  159.3 16.8 %collective-permute-start.5 = (f32[4,32,1024]{2,1,0:T(8,128)S(1)}, f32[4,32,1024]{2,1,0:T(8,128)S(1)}, u32[]{:S(2)}, u32[]{:S(2)}) collective-permute-start(f32[4,32,1024]{2,1,0:T(8,128)S(1)} %slice_add_fusion.39), channel_id=1, source_target_pairs={{1,0},{2,3},{5,4},{6,7},{9,8},{10,11},{13,12},{14,15},{17,16},{18,... | collective-permute-start | bytes 1572872 | tf_op jit(solution)/shard_map/ppermute | solution.py:250
  164.7 28.2 %collective-permute-start.8 = (f32[4,32,1024]{2,1,0:T(8,128)}, f32[4,32,1024]{2,1,0:T(8,128)}, u32[]{:S(2)}, u32[]{:S(2)}) collective-permute-start(f32[4,32,1024]{2,1,0:T(8,128)} %slice_add_fusion.35), channel_id=1, source_target_pairs={{1,0},{2,3},{5,4},{6,7},{9,8},{10,11},{13,12},{14,15},{17,16},{18,... | collective-permute-start | bytes 1572872 | tf_op jit(solution)/shard_map/ppermute | solution.py:250
  170.2 5.9 %copy-start.22 = (bf16[12,32,1024]{2,1,0:T(8,128)(2,1)}, bf16[12,32,1024]{2,1,0:T(8,128)(2,1)S(1)}, u32[]{:S(2)}) copy-start(bf16[12,32,1024]{2,1,0:T(8,128)(2,1)S(1)} %collective-permute-done.9) | copy-start | bytes 2359300
  171.2 35.1 %collective-permute-start.10 = (bf16[8,32,1024]{2,1,0:T(8,128)(2,1)}, bf16[8,32,1024]{2,1,0:T(8,128)(2,1)}, u32[]{:S(2)}, u32[]{:S(2)}) collective-permute-start(bf16[8,32,1024]{2,1,0:T(8,128)(2,1)} %fusion.11), channel_id=1, source_target_pairs={{1,2},{2,1},{5,6},{6,5},{9,10},{10,9},{13,14},{14,13},{17,18},{18,... | collective-permute-start | bytes 1572872 | tf_op jit(solution)/shard_map/ppermute | solution.py:247
  190.1 20.2 %collective-permute-start.12 = (bf16[12,32,1024]{2,1,0:T(8,128)(2,1)}, bf16[12,32,1024]{2,1,0:T(8,128)(2,1)}, u32[]{:S(2)}, u32[]{:S(2)}) collective-permute-start(bf16[12,32,1024]{2,1,0:T(8,128)(2,1)} %slice.624), channel_id=1, source_target_pairs={{0,1},{3,2},{4,5},{7,6},{8,9},{11,10},{12,13},{15,14},{16,17},{19,... | collective-permute-start | bytes 2359304 | tf_op jit(solution)/shard_map/ppermute | solution.py:95
  203.7 6.6 %copy-start.4 = (f32[16,32,1024]{2,1,0:T(8,128)S(1)}, f32[16,32,1024]{2,1,0:T(8,128)}, u32[]{:S(2)}) copy-start(f32[16,32,1024]{2,1,0:T(8,128)} %shard_map.50) | copy-start | bytes 6291460
  207.5 4.8 %copy-start.10 = (f32[8,32,1024]{2,1,0:T(8,128)}, f32[8,32,1024]{2,1,0:T(8,128)S(1)}, u32[]{:S(2)}) copy-start(f32[8,32,1024]{2,1,0:T(8,128)S(1)} %convert_element_type.146) | copy-start | bytes 3145732
  207.5 13.8 %copy-start = (f32[1024,512]{1,0:T(8,128)S(1)}, f32[1024,512]{1,0:T(8,128)}, u32[]{:S(2)}) copy-start(f32[1024,512]{1,0:T(8,128)} %get-tuple-element.20) | copy-start | bytes 6291460
  209.0 14.8 %collective-permute-start.11 = (f32[4,32,1024]{2,1,0:T(8,128)S(1)}, f32[4,32,1024]{2,1,0:T(8,128)S(1)}, u32[]{:S(2)}, u32[]{:S(2)}) collective-permute-start(f32[4,32,1024]{2,1,0:T(8,128)S(1)} %slice_add_fusion.31), channel_id=1, source_target_pairs={{1,0},{2,3},{5,4},{6,7},{9,8},{10,11},{13,12},{14,15},{17,16},{18,... | collective-permute-start | bytes 1572872 | tf_op jit(solution)/shard_map/ppermute | solution.py:250
  212.3 25.7 %collective-permute-start.13 = (bf16[8,32,1024]{2,1,0:T(8,128)(2,1)}, bf16[8,32,1024]{2,1,0:T(8,128)(2,1)}, u32[]{:S(2)}, u32[]{:S(2)}) collective-permute-start(bf16[8,32,1024]{2,1,0:T(8,128)(2,1)} %fusion.10), channel_id=1, source_target_pairs={{1,2},{2,1},{5,6},{6,5},{9,10},{10,9},{13,14},{14,13},{17,18},{18,... | collective-permute-start | bytes 1572872 | tf_op jit(solution)/shard_map/ppermute | solution.py:247
  213.8 28.9 %collective-permute-start.15 = (bf16[12,32,1024]{2,1,0:T(8,128)(2,1)}, bf16[12,32,1024]{2,1,0:T(8,128)(2,1)}, u32[]{:S(2)}, u32[]{:S(2)}) collective-permute-start(bf16[12,32,1024]{2,1,0:T(8,128)(2,1)} %slice.623), channel_id=1, source_target_pairs={{0,1},{3,2},{4,5},{7,6},{8,9},{11,10},{12,13},{15,14},{16,17},{19,... | collective-permute-start | bytes 2359304 | tf_op jit(solution)/shard_map/ppermute | solution.py:95
  235.4 12.8 %copy-start.5 = (f32[16,32,1024]{2,1,0:T(8,128)S(1)}, f32[16,32,1024]{2,1,0:T(8,128)}, u32[]{:S(2)}) copy-start(f32[16,32,1024]{2,1,0:T(8,128)} %shard_map.51) | copy-start | bytes 6291460
  240.1 11.6 %copy-start.16 = (bf16[512,1024]{0,1:T(8,128)(2,1)S(1)}, bf16[512,1024]{0,1:T(8,128)(2,1)}, u32[]{:S(2)}) copy-start(bf16[512,1024]{0,1:T(8,128)(2,1)} %multiply_bitcast_fusion.1) | copy-start | bytes 3145732
  240.1 11.6 %copy-start.19 = (bf16[512,1024]{0,1:T(8,128)(2,1)S(1)}, bf16[512,1024]{0,1:T(8,128)(2,1)}, u32[]{:S(2)}) copy-start(bf16[512,1024]{0,1:T(8,128)(2,1)} %multiply_bitcast_fusion) | copy-start | bytes 3145732
  240.1 11.6 %copy-start.27 = (f32[4,32,1024]{2,1,0:T(8,128)S(1)}, f32[4,32,1024]{2,1,0:T(8,128)}, u32[]{:S(2)}) copy-start(f32[4,32,1024]{2,1,0:T(8,128)} %copy-done.26) | copy-start | bytes 1572868
  241.4 16.3 %collective-permute-start.14 = (f32[4,32,1024]{2,1,0:T(8,128)S(1)}, f32[4,32,1024]{2,1,0:T(8,128)S(1)}, u32[]{:S(2)}, u32[]{:S(2)}) collective-permute-start(f32[4,32,1024]{2,1,0:T(8,128)S(1)} %slice_add_fusion.27), channel_id=1, source_target_pairs={{1,0},{2,3},{5,4},{6,7},{9,8},{10,11},{13,12},{14,15},{17,16},{18,... | collective-permute-start | bytes 1572872 | tf_op jit(solution)/shard_map/ppermute | solution.py:250
  242.7 30.3 %collective-permute-start.18 = (bf16[12,32,1024]{2,1,0:T(8,128)(2,1)}, bf16[12,32,1024]{2,1,0:T(8,128)(2,1)}, u32[]{:S(2)}, u32[]{:S(2)}) collective-permute-start(bf16[12,32,1024]{2,1,0:T(8,128)(2,1)} %slice.622), channel_id=1, source_target_pairs={{0,1},{3,2},{4,5},{7,6},{8,9},{11,10},{12,13},{15,14},{16,17},{19,... | collective-permute-start | bytes 2359304 | tf_op jit(solution)/shard_map/ppermute | solution.py:95
  250.2 21.7 %collective-permute-start.16 = (bf16[8,32,1024]{2,1,0:T(8,128)(2,1)}, bf16[8,32,1024]{2,1,0:T(8,128)(2,1)}, u32[]{:S(2)}, u32[]{:S(2)}) collective-permute-start(bf16[8,32,1024]{2,1,0:T(8,128)(2,1)} %fusion.9), channel_id=1, source_target_pairs={{1,2},{2,1},{5,6},{6,5},{9,10},{10,9},{13,14},{14,13},{17,18},{18,... | collective-permute-start | bytes 1572872 | tf_op jit(solution)/shard_map/ppermute | solution.py:247
  269.3 7.5 %copy-start.11 = (f32[8,32,1024]{2,1,0:T(8,128)S(1)}, f32[8,32,1024]{2,1,0:T(8,128)}, u32[]{:S(2)}) copy-start(f32[8,32,1024]{2,1,0:T(8,128)} %copy-done.10) | copy-start | bytes 3145732
  269.3 7.5 %copy-start.17 = (bf16[512,1024]{0,1:T(8,128)(2,1)S(1)}, bf16[512,1024]{0,1:T(8,128)(2,1)}, u32[]{:S(2)}) copy-start(bf16[512,1024]{0,1:T(8,128)(2,1)} %multiply_bitcast_fusion.1) | copy-start | bytes 3145732
  269.3 7.5 %copy-start.20 = (bf16[512,1024]{0,1:T(8,128)(2,1)S(1)}, bf16[512,1024]{0,1:T(8,128)(2,1)}, u32[]{:S(2)}) copy-start(bf16[512,1024]{0,1:T(8,128)(2,1)} %multiply_bitcast_fusion) | copy-start | bytes 3145732
  269.3 7.6 %copy-start.29 = (f32[4,32,1024]{2,1,0:T(8,128)S(1)}, f32[4,32,1024]{2,1,0:T(8,128)}, u32[]{:S(2)}) copy-start(f32[4,32,1024]{2,1,0:T(8,128)} %copy-done.28) | copy-start | bytes 1572868
  273.0 26.7 %collective-permute-start.21 = (bf16[12,32,1024]{2,1,0:T(8,128)(2,1)}, bf16[12,32,1024]{2,1,0:T(8,128)(2,1)}, u32[]{:S(2)}, u32[]{:S(2)}) collective-permute-start(bf16[12,32,1024]{2,1,0:T(8,128)(2,1)} %slice.621), channel_id=1, source_target_pairs={{0,1},{3,2},{4,5},{7,6},{8,9},{11,10},{12,13},{15,14},{16,17},{19,... | collective-permute-start | bytes 2359304 | tf_op jit(solution)/shard_map/ppermute | solution.py:95
  275.4 11.2 %collective-permute-start.17 = (f32[4,32,1024]{2,1,0:T(8,128)S(1)}, f32[4,32,1024]{2,1,0:T(8,128)S(1)}, u32[]{:S(2)}, u32[]{:S(2)}) collective-permute-start(f32[4,32,1024]{2,1,0:T(8,128)S(1)} %slice_add_fusion.23), channel_id=1, source_target_pairs={{1,0},{2,3},{5,4},{6,7},{9,8},{10,11},{13,12},{14,15},{17,16},{18,... | collective-permute-start | bytes 1572872 | tf_op jit(solution)/shard_map/ppermute | solution.py:250
  281.7 28.4 %collective-permute-start.19 = (bf16[8,32,1024]{2,1,0:T(8,128)(2,1)}, bf16[8,32,1024]{2,1,0:T(8,128)(2,1)}, u32[]{:S(2)}, u32[]{:S(2)}) collective-permute-start(bf16[8,32,1024]{2,1,0:T(8,128)(2,1)} %fusion.8), channel_id=1, source_target_pairs={{1,2},{2,1},{5,6},{6,5},{9,10},{10,9},{13,14},{14,13},{17,18},{18,... | collective-permute-start | bytes 1572872 | tf_op jit(solution)/shard_map/ppermute | solution.py:247
  287.4 15.9 %copy-start.13 = (f32[8,32,1024]{2,1,0:T(8,128)S(1)}, f32[8,32,1024]{2,1,0:T(8,128)}, u32[]{:S(2)}) copy-start(f32[8,32,1024]{2,1,0:T(8,128)} %copy-done.12) | copy-start | bytes 3145732
  299.7 7.3 %copy-start.15 = (f32[8,32,1024]{2,1,0:T(8,128)S(1)}, f32[8,32,1024]{2,1,0:T(8,128)}, u32[]{:S(2)}) copy-start(f32[8,32,1024]{2,1,0:T(8,128)} %copy-done.14) | copy-start | bytes 3145732
  299.7 7.3 %copy-start.18 = (bf16[512,1024]{0,1:T(8,128)(2,1)S(1)}, bf16[512,1024]{0,1:T(8,128)(2,1)}, u32[]{:S(2)}) copy-start(bf16[512,1024]{0,1:T(8,128)(2,1)} %multiply_bitcast_fusion.1) | copy-start | bytes 3145732
  299.7 7.3 %copy-start.21 = (bf16[512,1024]{0,1:T(8,128)(2,1)S(1)}, bf16[512,1024]{0,1:T(8,128)(2,1)}, u32[]{:S(2)}) copy-start(bf16[512,1024]{0,1:T(8,128)(2,1)} %multiply_bitcast_fusion) | copy-start | bytes 3145732
  299.7 7.3 %copy-start.32 = (f32[4,32,1024]{2,1,0:T(8,128)S(1)}, f32[4,32,1024]{2,1,0:T(8,128)}, u32[]{:S(2)}) copy-start(f32[4,32,1024]{2,1,0:T(8,128)} %copy-done.31) | copy-start | bytes 1572868
  299.8 13.6 %collective-permute-start.24 = (bf16[12,32,1024]{2,1,0:T(8,128)(2,1)S(1)}, bf16[12,32,1024]{2,1,0:T(8,128)(2,1)S(1)}, u32[]{:S(2)}, u32[]{:S(2)}) collective-permute-start(bf16[12,32,1024]{2,1,0:T(8,128)(2,1)S(1)} %slice.620), channel_id=1, source_target_pairs={{0,1},{3,2},{4,5},{7,6},{8,9},{11,10},{12,13},{15,14},{16,17},{19,... | collective-permute-start | bytes 2359304 | tf_op jit(solution)/shard_map/ppermute | solution.py:95
  312.6 3.0 collective-permute-start.22
  313.5 3.6 %collective-permute-start.25 = (bf16[8,32,1024]{2,1,0:T(8,128)(2,1)S(1)}, bf16[8,32,1024]{2,1,0:T(8,128)(2,1)S(1)}, u32[]{:S(2)}, u32[]{:S(2)}) collective-permute-start(bf16[8,32,1024]{2,1,0:T(8,128)(2,1)S(1)} %fusion.6), channel_id=1, source_target_pairs={{1,2},{2,1},{5,6},{6,5},{9,10},{10,9},{13,14},{14,13},{17,18},{18,... | collective-permute-start | bytes 1572872 | tf_op jit(solution)/shard_map/ppermute | solution.py:247
  314.3 18.0 %collective-permute-start.20 = (f32[4,32,1024]{2,1,0:T(8,128)S(1)}, f32[4,32,1024]{2,1,0:T(8,128)S(1)}, u32[]{:S(2)}, u32[]{:S(2)}) collective-permute-start(f32[4,32,1024]{2,1,0:T(8,128)S(1)} %slice_add_fusion.19), channel_id=1, source_target_pairs={{1,0},{2,3},{5,4},{6,7},{9,8},{10,11},{13,12},{14,15},{17,16},{18,... | collective-permute-start | bytes 1572872 | tf_op jit(solution)/shard_map/ppermute | solution.py:250
  315.8 24.6 %collective-permute-start.23 = (f32[4,32,1024]{2,1,0:T(8,128)S(1)}, f32[4,32,1024]{2,1,0:T(8,128)S(1)}, u32[]{:S(2)}, u32[]{:S(2)}) collective-permute-start(f32[4,32,1024]{2,1,0:T(8,128)S(1)} %slice_add_fusion.15), channel_id=1, source_target_pairs={{1,0},{2,3},{5,4},{6,7},{9,8},{10,11},{13,12},{14,15},{17,16},{18,... | collective-permute-start | bytes 1572872 | tf_op jit(solution)/shard_map/ppermute | solution.py:250
  317.3 28.7 %collective-permute-start.26 = (f32[4,32,1024]{2,1,0:T(8,128)S(1)}, f32[4,32,1024]{2,1,0:T(8,128)S(1)}, u32[]{:S(2)}, u32[]{:S(2)}) collective-permute-start(f32[4,32,1024]{2,1,0:T(8,128)S(1)} %slice_add_fusion.11), channel_id=1, source_target_pairs={{1,0},{2,3},{5,4},{6,7},{9,8},{10,11},{13,12},{14,15},{17,16},{18,... | collective-permute-start | bytes 1572872 | tf_op jit(solution)/shard_map/ppermute | solution.py:250
  (12 other events, 25.2 us)
